TPU v7x, 512 devices: a whole 4x4x16 slice. The times are simulated.
512 devices in a mesh: grp: 4 (over y), walk: 128 (over x, z, core).
Axes of the slice: x: 4, y: 4, z: 16, core: 2. Of those that a mesh axis runs over, the one named last changes fastest.
Arguments:
- log_grads: float32 [1024, 131072], P('walk', 'grp'), may hold values from -60 to 60, as said below
- energies: float32 [1024], P('walk'), may hold values from -6 to 6
Outputs:
- update: float32 [131072], P(('grp', 'walk'))
Inputs may be any that keep to these rules, and one draw needn't show every extreme that they name: `log_grads`: real-valued gradients, every row and column with its own scale.
All inputs are finite; a program needn't handle non-finite values.
Results may differ from a plain program's by a relative error of at most 0.0003.
Values sent between devices are 32-bit elements; how exact they have to be, the bound alone decides.
No kernel may reach another device: no remote copies, remote signals or barrier semaphores. Data moves between devices by JAX's collectives and lax.ppermute only.
A program may use at most 128 MiB of HBM per device.

v0:
```python
import jax
import jax.numpy as jnp
from jax import lax
from jax.sharding import PartitionSpec as P

WALKERS = 1024


damping = 0.0004


def factor_solve(factor, rhs):
    column = rhs[:, None]
    first = lax.linalg.triangular_solve(factor, column, left_side=True, lower=True)
    second = lax.linalg.triangular_solve(
        factor, first, left_side=True, lower=True, transpose_a=True
    )
    return second[:, 0]


def on_device(log_grads, energies):
    all_energy = lax.all_gather(energies, "walk", axis=0, tiled=True)
    regrouped = lax.all_to_all(log_grads, "walk", split_axis=1, concat_axis=0, tiled=True)
    group_params = regrouped.shape[1] * lax.axis_size("walk")
    total_params = group_params * lax.axis_size("grp")
    root_walkers = jnp.sqrt(jnp.float32(WALKERS))
    column_mean = jnp.mean(regrouped, axis=0, keepdims=True)
    centred = (regrouped - column_mean) / root_walkers
    scaled_energy = (all_energy - jnp.mean(all_energy)) / root_walkers
    local_gram = jnp.dot(centred, centred.T, precision=lax.Precision.HIGHEST)
    identity_mat = jnp.eye(WALKERS, dtype=jnp.float32)
    whole_gram = lax.psum(local_gram, ("grp", "walk"))
    factor = jnp.linalg.cholesky(whole_gram + damping * total_params * identity_mat)
    solved = factor_solve(factor, scaled_energy)
    update = jnp.dot(solved, centred, precision=lax.Precision.HIGHEST)
    return -(total_params / root_walkers) * update


def solution(mesh):
    return jax.shard_map(
        on_device,
        mesh=mesh,
        in_specs=(P("walk", "grp"), P("walk")),
        out_specs=P(("grp", "walk")),
        check_vma=False,
    )
```

profile of v0, /device:TPU:1, one launch (start us, length us, event | category | flops | bytes accessed | tf_op | source)
XLA Modules:
  0.0 931.0 jit_solution(15668519067561449194)
XLA Ops:
  6.5 74.7 %all_to_all.13 = f32[8,128,256]{2,0,1:T(8,128)S(1)} all-to-all(f32[8,128,256]{2,0,1:T(8,128)} %bitcast.329), channel_id=1, replica_groups=mesh['grp'=4,'walk'=128] {'walk'}, dimensions={1} | all-to-all | bytes 2097152 | tf_op jit(solution)/shard_map/all_to_all | solution.py:23
  81.5 5.2 fusion.33
  88.9 248.4 %all-reduce.1 = f32[1024]{0:T(1024)S(1)} all-reduce(f32[1024]{0:T(1024)S(1)} %dynamic-update-slice.47), channel_id=1, replica_groups=mesh['grp'=4,'walk'=128] {'walk'}, use_global_device_ids=true, to_apply=%add.1 | all-reduce | flops 1024 | bytes 8192
  338.5 230.0 %all-reduce.4.cloned.1.call-done = f32[1024,1024]{0,1:T(8,128)} async-done(((f32[1024,1024]{0,1:T(8,128)}), f32[1024,1024]{0,1:T(8,128)}) %all-reduce.4.cloned.1.call-update) | async-done | bytes 4194320 | tf_op jit(solution)/shard_map/psum | solution.py:32
  568.6 4.8 select_add_fusion
  573.4 5.8 copy.4
  579.2 4.5 fusion
  583.6 1.9 copy-done
  585.6 11.7 %cholesky.222 = f32[128,128]{1,0:T(8,128)S(1)} custom-call(f32[128,128]{1,0:T(8,128)S(1)} %cholesky.577), custom_call_target="Cholesky" | custom-call | tf_op jit(solution)/shard_map/jit(cholesky)/cholesky | solution.py:33
  597.4 9.8 %custom-call.64 = f32[1,128,128]{1,2,0:T(8,128)S(1)} custom-call(f32[1,128,128]{2,1,0:T(8,128)S(1)} %get-tuple-element.40), custom_call_target="InvertDiagBlocksLowerTriangular" | custom-call | tf_op jit(solution)/shard_map/jit(cholesky)/cholesky | solution.py:33
  607.2 1.5 fusion.46
  609.0 1.6 convolution_subtract_fusion
  610.5 11.7 %cholesky.243 = f32[128,128]{1,0:T(8,128)S(1)} custom-call(f32[128,128]{1,0:T(8,128)S(1)} %cholesky.581), custom_call_target="Cholesky" | custom-call | tf_op jit(solution)/shard_map/jit(cholesky)/cholesky | solution.py:33
  622.6 2.5 cholesky.254
  625.1 9.8 %custom-call.65 = f32[1,128,128]{1,2,0:T(8,128)S(1)} custom-call(f32[1,128,128]{2,1,0:T(8,128)S(1)} %get-tuple-element.38), custom_call_target="InvertDiagBlocksLowerTriangular" | custom-call | tf_op jit(solution)/shard_map/jit(cholesky)/cholesky | solution.py:33
  637.6 2.7 convolution_subtract_fusion.1
  640.4 11.7 %cholesky.466 = f32[128,128]{1,0:T(8,128)S(1)} custom-call(f32[128,128]{1,0:T(8,128)S(1)} %cholesky.586), custom_call_target="Cholesky" | custom-call | tf_op jit(solution)/shard_map/jit(cholesky)/cholesky | solution.py:33
  652.8 9.8 %custom-call.66 = f32[1,128,128]{1,2,0:T(8,128)S(1)} custom-call(f32[1,128,128]{2,1,0:T(8,128)S(1)} %get-tuple-element.36), custom_call_target="InvertDiagBlocksLowerTriangular" | custom-call | tf_op jit(solution)/shard_map/jit(cholesky)/cholesky | solution.py:33
  663.9 3.3 convolution_subtract_fusion.2
  667.3 11.7 %cholesky.485 = f32[128,128]{1,0:T(8,128)S(1)} custom-call(f32[128,128]{1,0:T(8,128)S(1)} %cholesky.591), custom_call_target="Cholesky" | custom-call | tf_op jit(solution)/shard_map/jit(cholesky)/cholesky | solution.py:33
  679.8 9.8 %custom-call.67 = f32[1,128,128]{1,2,0:T(8,128)S(1)} custom-call(f32[1,128,128]{2,1,0:T(8,128)S(1)} %get-tuple-element.34), custom_call_target="InvertDiagBlocksLowerTriangular" | custom-call | tf_op jit(solution)/shard_map/jit(cholesky)/cholesky | solution.py:33
  690.7 3.2 convolution_subtract_fusion.3
  693.9 12.1 %cholesky.504 = f32[128,128]{1,0:T(8,128)S(1)} custom-call(f32[128,128]{1,0:T(8,128)S(1)} %cholesky.596), custom_call_target="Cholesky" | custom-call | tf_op jit(solution)/shard_map/jit(cholesky)/cholesky | solution.py:33
  706.7 9.8 %custom-call.68 = f32[1,128,128]{1,2,0:T(8,128)S(1)} custom-call(f32[1,128,128]{2,1,0:T(8,128)S(1)} %get-tuple-element.32), custom_call_target="InvertDiagBlocksLowerTriangular" | custom-call | tf_op jit(solution)/shard_map/jit(cholesky)/cholesky | solution.py:33
  717.7 3.1 convolution_subtract_fusion.4
  720.8 11.7 %cholesky.524 = f32[128,128]{1,0:T(8,128)S(1)} custom-call(f32[128,128]{1,0:T(8,128)S(1)} %cholesky.601), custom_call_target="Cholesky" | custom-call | tf_op jit(solution)/shard_map/jit(cholesky)/cholesky | solution.py:33
  733.2 9.8 %custom-call.69 = f32[1,128,128]{1,2,0:T(8,128)S(1)} custom-call(f32[1,128,128]{2,1,0:T(8,128)S(1)} %get-tuple-element.30), custom_call_target="InvertDiagBlocksLowerTriangular" | custom-call | tf_op jit(solution)/shard_map/jit(cholesky)/cholesky | solution.py:33
  744.1 2.8 convolution_subtract_fusion.5
  746.9 11.7 %cholesky.544 = f32[128,128]{1,0:T(8,128)S(1)} custom-call(f32[128,128]{1,0:T(8,128)S(1)} %cholesky.606), custom_call_target="Cholesky" | custom-call | tf_op jit(solution)/shard_map/jit(cholesky)/cholesky | solution.py:33
  759.4 9.8 %custom-call.70 = f32[1,128,128]{1,2,0:T(8,128)S(1)} custom-call(f32[1,128,128]{2,1,0:T(8,128)S(1)} %get-tuple-element.28), custom_call_target="InvertDiagBlocksLowerTriangular" | custom-call | tf_op jit(solution)/shard_map/jit(cholesky)/cholesky | solution.py:33
  770.1 2.1 convolution_subtract_fusion.6
  772.2 11.7 %cholesky.562 = f32[128,128]{1,0:T(8,128)S(1)} custom-call(f32[128,128]{1,0:T(8,128)S(1)} %convolution_subtract_fusion.6), custom_call_target="Cholesky" | custom-call | tf_op jit(solution)/shard_map/jit(cholesky)/cholesky | solution.py:33
  794.4 4.8 select_select_fusion
  799.3 23.7 %while.1 = (s32[]{:T(128)}, f32[1024,1024]{0,1:T(8,128)}, s32[8,2]{0,1:T(2,128)S(1)}, f32[8,128,128]{2,1,0:T(8,128)S(1)}, s32[]{:T(128)}) while((s32[]{:T(128)}, f32[1024,1024]{0,1:T(8,128)}, s32[8,2]{0,1:T(2,128)S(1)}, f32[8,128,128]{2,1,0:T(8,128)S(1)}, s32[]{:T(128)}) %tuple.49), condition=%wide.while_cond, body=%wide.while_body.sunk | while | flops 2 | bytes 393329 | solution.py:15
  799.9 2.2 dynamic-slice.8
  802.9 2.2 dynamic-slice.8
  805.8 2.2 dynamic-slice.8
  808.8 2.2 dynamic-slice.8
  811.8 2.2 dynamic-slice.8
  814.8 2.2 dynamic-slice.8
  817.7 2.2 dynamic-slice.8
  820.7 2.2 dynamic-slice.8
  823.0 78.8 %custom-call.71 = f32[8,128,128]{1,2,0:T(8,128)S(1)} custom-call(f32[8,128,128]{2,1,0:T(8,128)S(1)} %get-tuple-element.12), custom_call_target="InvertDiagBlocksLowerTriangular" | custom-call | tf_op jit(solution)/shard_map/triangular_solve | solution.py:15
  908.6 1.3 fusion.17
  910.1 1.4 fusion.11
  917.6 1.4 fusion.23
  919.3 1.4 fusion.21
  921.0 1.5 fusion.13
  (141 shorter events, 41.3 us)
Async XLA Ops:
  6.5 562.0 %all-reduce.4.cloned.1.call-start = ((), (), s32[]{:S(2)}) async-start(), calls=%async_computation.1 | async-start | bytes 8388608 | tf_op jit(solution)/shard_map/psum | solution.py:32
  81.4 7.2 copy-start.1
  583.6 1.9 copy-start
Sparse Core Ops, SparseCore 0:
  86.8 481.6 all-reduce.3
where the time goes:
time: 938 us; the launch traced here: 931 us
  blocking collectives  323 us (34%)
  other arithmetic  262 us (28%)
  waiting for transfers between devices  230 us (25%)
  matrix products  53.4 us (6%)
  local copies, waits for them, and re-layouts  42 us (4%)
  between operations  20.3 us (2%)
    unnamed x1, blocking collectives  248 us
    psum x1, waiting for transfers between devices, on_device(): whole_gram = lax.psum(local_gram, ('grp', 'walk'))  230 us
    another operation x30, other arithmetic, on_device(): jnp.linalg.cholesky(whole_gram + damping * total_params * identity_mat)  168 us
    another operation x3, other arithmetic, factor_solve(): lax.linalg.triangular_solve(factor, first, left_side=True, lower=True, tr...  83.6 us
    all_to_all x1, blocking collectives, on_device(): lax.all_to_all(log_grads, 'walk', split_axis=1, concat_axis=0, tiled=True)  74.7 us
    another operation x14, matrix products, on_device(): jnp.linalg.cholesky(whole_gram + damping * total_params * identity_mat)  27 us
    another operation x40, local copies, waits for them, and re-layouts  23.5 us
  transfers between devices with their start and end apart: 1, of which 1 were waited for; matrix products, arithmetic and copies ran while one was open for 0% of the time, Pallas kernels for 0%

commit v1 on v0

v1 whole, which is shorter than its diff:
```python
import jax
import jax.numpy as jnp
import numpy as np
from jax import lax
from jax.sharding import Mesh
from jax.sharding import PartitionSpec as P

WALKERS = 1024
BLOCK = 128


damping = 0.0004

WALK_PARTS = ("wx", "wz", "wc")


def split_walk(walk):
    if walk % 32 == 0 and walk // 32 <= 4:
        return (walk // 32, 16, 2)
    return (1, 1, walk)


def factor_solve(factor, rhs):
    column = rhs[:, None]
    first = lax.linalg.triangular_solve(factor, column, left_side=True, lower=True)
    second = lax.linalg.triangular_solve(
        factor, first, left_side=True, lower=True, transpose_a=True
    )
    return second[:, 0]


def reduce_scatter(x, levels):
    for axis, size in levels:
        rows = x.shape[0]
        parts = x.reshape(size, rows // size, x.shape[1])
        x = lax.all_to_all(parts, axis, 0, 0, tiled=True).sum(0)
    return x


def all_gather(x, levels):
    for axis, size in levels:
        copies = jnp.broadcast_to(x[None], (size,) + x.shape)
        x = lax.all_to_all(copies, axis, 0, 0, tiled=True)
    return x


def upper_pairs(nb):
    return [(i, j) for i in range(nb) for j in range(i, nb)]


def pack_upper(gram, nb):
    blocks = gram.reshape(nb, BLOCK, nb, BLOCK)
    return jnp.stack([blocks[i, :, j, :] for i, j in upper_pairs(nb)])


def unpack_upper(packed, nb):
    where = {pair: k for k, pair in enumerate(upper_pairs(nb))}
    rows = []
    for i in range(nb):
        row = []
        for j in range(nb):
            if i <= j:
                row.append(packed[where[(i, j)]])
            else:
                row.append(packed[where[(j, i)]].T)
        rows.append(jnp.concatenate(row, axis=1))
    return jnp.concatenate(rows, axis=0)


def make_on_device(sizes):
    grp, wx, wz, wc = sizes
    levels = [("grp", grp), ("wc", wc), ("wx", wx), ("wz", wz)]
    levels = [(a, n) for a, n in levels if n > 1]
    n_dev = grp * wx * wz * wc

    def on_device(log_grads, energies):
        walk_axes = WALK_PARTS
        regrouped = lax.all_to_all(
            log_grads, walk_axes, split_axis=1, concat_axis=0, tiled=True
        )
        walk = wx * wz * wc
        group_params = regrouped.shape[1] * walk
        total_params = group_params * grp
        root_walkers = jnp.sqrt(jnp.float32(WALKERS))
        column_mean = jnp.mean(regrouped, axis=0, keepdims=True)
        centred = (regrouped - column_mean) / root_walkers
        local_gram = jnp.dot(centred, centred.T, precision=lax.Precision.HIGHEST)

        nb = WALKERS // BLOCK
        packed = pack_upper(local_gram, nb)
        n_blocks = packed.shape[0]
        flat = packed.reshape(n_blocks * BLOCK, BLOCK)
        chunk = reduce_scatter(flat, levels)
        per_dev = chunk.shape[0]
        energy_row = jnp.zeros((1, BLOCK), jnp.float32)
        energy_row = energy_row.at[0, : energies.shape[0]].set(energies)
        chunk = jnp.concatenate([chunk, energy_row], axis=0)
        gathered = all_gather(chunk, levels[::-1])
        gathered = gathered.reshape(grp, wc, wx, wz, per_dev + 1, BLOCK)
        whole_packed = gathered[..., :per_dev, :].reshape(n_blocks, BLOCK, BLOCK)
        per_walk = energies.shape[0]
        all_energy = gathered[0, :, :, :, per_dev, :per_walk]
        all_energy = jnp.transpose(all_energy, (1, 2, 0, 3)).reshape(WALKERS)

        whole_gram = unpack_upper(whole_packed, nb)
        scaled_energy = (all_energy - jnp.mean(all_energy)) / root_walkers
        identity_mat = jnp.eye(WALKERS, dtype=jnp.float32)
        factor = jnp.linalg.cholesky(whole_gram + damping * total_params * identity_mat)
        solved = factor_solve(factor, scaled_energy)
        update = jnp.dot(solved, centred, precision=lax.Precision.HIGHEST)
        return -(total_params / root_walkers) * update

    return on_device


def solution(mesh):
    grp = mesh.shape["grp"]
    walk = mesh.shape["walk"]
    wx, wz, wc = split_walk(walk)
    devices = np.asarray(mesh.devices).reshape(grp, wx, wz, wc)
    fine = Mesh(devices, ("grp",) + WALK_PARTS)
    return jax.shard_map(
        make_on_device((grp, wx, wz, wc)),
        mesh=fine,
        in_specs=(P(WALK_PARTS, "grp"), P(WALK_PARTS)),
        out_specs=P(("grp",) + WALK_PARTS),
        check_vma=False,
    )
```

time: 938 us -> 680 us (0.72)
  waiting for transfers between devices: 230 us -> 42.4 us
  blocking collectives: 323 us -> 158 us
  local copies, waits for them, and re-layouts: 42 us -> 136 us
  between operations: 20.3 us -> 7.24 us
    unnamed x1 -> x0, blocking collectives: 248 us -> none
    psum x1 -> x0, waiting for transfers between devices: 230 us -> none  [on_device(): whole_gram = lax.psum(local_gram, ('grp', 'walk'))]
    all_to_all x1 -> x7, blocking collectives: 74.7 us -> 158 us  [the longest x1 74.7 us: on_device(): lax.all_to_all(log_grads, walk_axes, split_axis=1, concat_axis=0, tiled=T...]
    unnamed x25 -> x142, local copies, waits for them, and re-layouts: 3.72 us -> 61.7 us
    all_to_all x0 -> x2, waiting for transfers between devices: none -> 42.4 us  [the longest x1 31.7 us: all_gather(): x = lax.all_to_all(copies, axis, 0, 0, tiled=True)]
    concatenate x0 -> x7, local copies, waits for them, and re-layouts: none -> 9.55 us  [the longest x6 9.55 us: unpack_upper(): rows.append(jnp.concatenate(row, axis=1))]
    another operation x40 -> x41, local copies, waits for them, and re-layouts: 23.5 us -> 28.4 us
    another operation x30 -> x31, other arithmetic: 168 us -> 168 us  [on_device(): jnp.linalg.cholesky(whole_gram + damping * total_params * identity_mat)]
  transfers between devices with their start and end apart: 1 -> 2, of which waited for: 1 -> 2; matrix products, arithmetic and copies ran while one was open for 0% -> 0% of each run, Pallas kernels for 0% -> 0%
where the time goes in v1:
time: 680 us; the launch traced here: 669 us
  other arithmetic  265 us (39%)
  blocking collectives  158 us (23%)
  local copies, waits for them, and re-layouts  136 us (20%)
  matrix products  51 us (8%)
  waiting for transfers between devices  42.4 us (6%)
  starting transfers between devices  9.07 us (1%)
  between operations  7.24 us (1%)
    another operation x31, other arithmetic, on_device(): jnp.linalg.cholesky(whole_gram + damping * total_params * identity_mat)  168 us
    another operation x3, other arithmetic, factor_solve(): lax.linalg.triangular_solve(factor, first, left_side=True, lower=True, tr...  84.2 us
    all_to_all x1, blocking collectives, on_device(): lax.all_to_all(log_grads, walk_axes, split_axis=1, concat_axis=0, tiled=T...  74.7 us
    unnamed x142, local copies, waits for them, and re-layouts  61.7 us
    all_to_all x3, blocking collectives, reduce_scatter(): x = lax.all_to_all(parts, axis, 0, 0, tiled=True).sum(0)  49 us
    all_to_all x3, blocking collectives, all_gather(): x = lax.all_to_all(copies, axis, 0, 0, tiled=True)  34.5 us
    all_to_all x1, waiting for transfers between devices, all_gather(): x = lax.all_to_all(copies, axis, 0, 0, tiled=True)  31.7 us
    another operation x40, local copies, waits for them, and re-layouts  28.4 us
  transfers between devices with their start and end apart: 2, of which 2 were waited for; matrix products, arithmetic and copies ran while one was open for 0% of the time, Pallas kernels for 0%

profile of v1, /device:TPU:1, one launch (start us, length us, event | category | flops | bytes accessed | tf_op | source)
XLA Modules:
  0.0 668.7 jit_solution(14860112461521182850)
XLA Ops:
  0.0 74.7 %all_to_all.53 = f32[8,128,256]{2,0,1:T(8,128)S(1)} all-to-all(f32[8,128,256]{2,0,1:T(8,128)} %bitcast.662), channel_id=1, replica_groups=mesh['grp'=4,'wx'=4,'wz'=16,'wc'=2] {'wx','wz','wc'}, dimensions={1} | all-to-all | bytes 2097152 | tf_op jit(solution)/shard_map/all_to_all | solution.py:78
  75.0 3.8 fusion.123
  79.3 30.7 %all_to_all.54 = f32[4,1152,128]{2,1,0:T(8,128)S(1)} all-to-all(f32[4,1152,128]{2,1,0:T(8,128)S(1)} %bitcast.659), channel_id=1, replica_groups=mesh['grp'=4,'wx'=4,'wz'=16,'wc'=2] {'grp'}, dimensions={0} | all-to-all | bytes 4718592 | tf_op jit(solution)/shard_map/all_to_all | solution.py:36
  111.0 8.3 %all_to_all.55 = f32[2,576,128]{2,1,0:T(8,128)S(1)} all-to-all(f32[2,576,128]{2,1,0:T(8,128)} %bitcast.660), channel_id=1, replica_groups=mesh['grp'=4,'wx'=4,'wz'=16,'wc'=2] {'wc'}, dimensions={0} | all-to-all | bytes 1179648 | tf_op jit(solution)/shard_map/all_to_all | solution.py:36
  119.3 10.1 %all_to_all.56 = f32[4,144,128]{2,1,0:T(8,128)S(1)} all-to-all(f32[4,144,128]{2,1,0:T(8,128)S(1)} %bitcast.661), channel_id=1, replica_groups=mesh['grp'=4,'wx'=4,'wz'=16,'wc'=2] {'wx'}, dimensions={0} | all-to-all | bytes 589824 | tf_op jit(solution)/shard_map/all_to_all | solution.py:36
  130.0 4.0 all-to-all-start.4
  135.3 10.7 %all-to-all-done.4 = f32[16,9,128]{2,1,0:T(8,128)S(1)} async-done(((f32[16,9,128]{2,1,0:T(8,128)}), f32[16,9,128]{2,1,0:T(8,128)S(1)}, u32[]{:S(2)}, u32[]{:S(2)}) %all-to-all-start.4) | async-done | bytes 73760 | tf_op jit(solution)/shard_map/all_to_all | solution.py:36
  146.0 17.1 %all_to_all.57 = f32[16,10,128]{2,1,0:T(8,128)S(1)} all-to-all(f32[16,10,128]{2,1,0:T(8,128)S(1)} %broadcast_in_dim.9), channel_id=1, replica_groups=mesh['grp'=4,'wx'=4,'wz'=16,'wc'=2] {'wz'}, dimensions={0} | all-to-all | bytes 163840 | tf_op jit(solution)/shard_map/all_to_all | solution.py:43
  163.2 8.3 %all_to_all.58 = f32[4,16,10,128]{3,1,2,0:T(8,128)S(1)} all-to-all(f32[4,16,10,128]{3,1,2,0:T(8,128)S(1)} %broadcast_in_dim.10), channel_id=1, replica_groups=mesh['grp'=4,'wx'=4,'wz'=16,'wc'=2] {'wx'}, dimensions={0} | all-to-all | bytes 655360 | tf_op jit(solution)/shard_map/all_to_all | solution.py:43
  171.5 9.2 %all_to_all.59 = f32[2,4,16,10,128]{4,2,1,3,0:T(8,128)S(1)} all-to-all(f32[2,4,16,10,128]{4,2,1,3,0:T(8,128)S(1)} %broadcast_in_dim.11), channel_id=1, replica_groups=mesh['grp'=4,'wx'=4,'wz'=16,'wc'=2] {'wc'}, dimensions={0} | all-to-all | bytes 1310720 | tf_op jit(solution)/shard_map/all_to_all | solution.py:43
  181.2 2.8 broadcast_in_dim.12
  184.0 5.1 all-to-all-start.8
  189.2 31.7 %all-to-all-done.8 = f32[4,2,4,16,10,128]{5,1,3,2,4,0:T(2,128)} async-done(((f32[4,2,4,16,10,128]{5,1,3,2,4,0:T(2,128)}), f32[4,2,4,16,10,128]{5,1,3,2,4,0:T(2,128)}, u32[]{:S(2)}, u32[]{:S(2)}) %all-to-all-start.8) | async-done | bytes 2621472 | tf_op jit(solution)/shard_map/all_to_all | solution.py:43
  220.9 3.2 slice.664
  224.1 3.4 copy.157
  227.5 3.0 reshape.298
  308.7 2.3 select_add_fusion
  311.0 5.5 copy.190
  316.5 4.5 fusion
  322.9 11.7 %cholesky.222 = f32[128,128]{1,0:T(8,128)S(1)} custom-call(f32[128,128]{1,0:T(8,128)S(1)} %cholesky.577), custom_call_target="Cholesky" | custom-call | tf_op jit(solution)/shard_map/jit(cholesky)/cholesky | solution.py:108
  334.8 9.8 %custom-call.64 = f32[1,128,128]{1,2,0:T(8,128)S(1)} custom-call(f32[1,128,128]{2,1,0:T(8,128)S(1)} %get-tuple-element.101), custom_call_target="InvertDiagBlocksLowerTriangular" | custom-call | tf_op jit(solution)/shard_map/jit(cholesky)/cholesky | solution.py:108
  347.9 11.7 %cholesky.243 = f32[128,128]{1,0:T(8,128)S(1)} custom-call(f32[128,128]{1,0:T(8,128)S(1)} %cholesky.581), custom_call_target="Cholesky" | custom-call | tf_op jit(solution)/shard_map/jit(cholesky)/cholesky | solution.py:108
  359.9 9.8 %custom-call.65 = f32[1,128,128]{1,2,0:T(8,128)S(1)} custom-call(f32[1,128,128]{2,1,0:T(8,128)S(1)} %get-tuple-element.99), custom_call_target="InvertDiagBlocksLowerTriangular" | custom-call | tf_op jit(solution)/shard_map/jit(cholesky)/cholesky | solution.py:108
  372.8 2.4 convolution_subtract_fusion.1
  375.3 11.7 %cholesky.466 = f32[128,128]{1,0:T(8,128)S(1)} custom-call(f32[128,128]{1,0:T(8,128)S(1)} %cholesky.586), custom_call_target="Cholesky" | custom-call | tf_op jit(solution)/shard_map/jit(cholesky)/cholesky | solution.py:108
  387.8 9.8 %custom-call.66 = f32[1,128,128]{1,2,0:T(8,128)S(1)} custom-call(f32[1,128,128]{2,1,0:T(8,128)S(1)} %get-tuple-element.97), custom_call_target="InvertDiagBlocksLowerTriangular" | custom-call | tf_op jit(solution)/shard_map/jit(cholesky)/cholesky | solution.py:108
  398.8 3.5 convolution_subtract_fusion.2
  402.4 11.7 %cholesky.485 = f32[128,128]{1,0:T(8,128)S(1)} custom-call(f32[128,128]{1,0:T(8,128)S(1)} %cholesky.591), custom_call_target="Cholesky" | custom-call | tf_op jit(solution)/shard_map/jit(cholesky)/cholesky | solution.py:108
  414.9 9.8 %custom-call.67 = f32[1,128,128]{1,2,0:T(8,128)S(1)} custom-call(f32[1,128,128]{2,1,0:T(8,128)S(1)} %get-tuple-element.95), custom_call_target="InvertDiagBlocksLowerTriangular" | custom-call | tf_op jit(solution)/shard_map/jit(cholesky)/cholesky | solution.py:108
  425.8 3.1 convolution_subtract_fusion.3
  429.0 11.9 %cholesky.504 = f32[128,128]{1,0:T(8,128)S(1)} custom-call(f32[128,128]{1,0:T(8,128)S(1)} %cholesky.596), custom_call_target="Cholesky" | custom-call | tf_op jit(solution)/shard_map/jit(cholesky)/cholesky | solution.py:108
  441.6 9.8 %custom-call.68 = f32[1,128,128]{1,2,0:T(8,128)S(1)} custom-call(f32[1,128,128]{2,1,0:T(8,128)S(1)} %get-tuple-element.93), custom_call_target="InvertDiagBlocksLowerTriangular" | custom-call | tf_op jit(solution)/shard_map/jit(cholesky)/cholesky | solution.py:108
  452.5 3.1 convolution_subtract_fusion.4
  455.6 11.7 %cholesky.524 = f32[128,128]{1,0:T(8,128)S(1)} custom-call(f32[128,128]{1,0:T(8,128)S(1)} %cholesky.601), custom_call_target="Cholesky" | custom-call | tf_op jit(solution)/shard_map/jit(cholesky)/cholesky | solution.py:108
  468.1 9.8 %custom-call.69 = f32[1,128,128]{1,2,0:T(8,128)S(1)} custom-call(f32[1,128,128]{2,1,0:T(8,128)S(1)} %get-tuple-element.91), custom_call_target="InvertDiagBlocksLowerTriangular" | custom-call | tf_op jit(solution)/shard_map/jit(cholesky)/cholesky | solution.py:108
  478.9 2.9 convolution_subtract_fusion.5
  481.8 11.7 %cholesky.544 = f32[128,128]{1,0:T(8,128)S(1)} custom-call(f32[128,128]{1,0:T(8,128)S(1)} %cholesky.606), custom_call_target="Cholesky" | custom-call | tf_op jit(solution)/shard_map/jit(cholesky)/cholesky | solution.py:108
  494.3 9.8 %custom-call.70 = f32[1,128,128]{1,2,0:T(8,128)S(1)} custom-call(f32[1,128,128]{2,1,0:T(8,128)S(1)} %get-tuple-element.89), custom_call_target="InvertDiagBlocksLowerTriangular" | custom-call | tf_op jit(solution)/shard_map/jit(cholesky)/cholesky | solution.py:108
  507.1 11.7 %cholesky.562 = f32[128,128]{1,0:T(8,128)S(1)} custom-call(f32[128,128]{1,0:T(8,128)S(1)} %convolution_subtract_fusion.6), custom_call_target="Cholesky" | custom-call | tf_op jit(solution)/shard_map/jit(cholesky)/cholesky | solution.py:108
  533.3 4.8 select_select_fusion
  538.1 28.7 %while.2 = (s32[]{:T(128)}, f32[1024,1024]{0,1:T(8,128)}, s32[8,2]{0,1:T(2,128)S(1)}, f32[8,128,128]{2,1,0:T(8,128)}, s32[]{:T(128)}) while((s32[]{:T(128)}, f32[1024,1024]{0,1:T(8,128)}, s32[8,2]{0,1:T(2,128)S(1)}, f32[8,128,128]{2,1,0:T(8,128)}, s32[]{:T(128)}) %tuple.85), condition=%wide.while_cond.1, body=%wide.while_body.1.sunk | while | flops 2 | bytes 393329 | solution.py:26
  539.0 2.2 dynamic-slice.14
  542.5 2.2 dynamic-slice.14
  546.1 2.2 dynamic-slice.14
  549.7 2.2 dynamic-slice.14
  553.2 2.2 dynamic-slice.14
  556.8 2.2 dynamic-slice.14
  566.8 79.4 %custom-call.71 = f32[8,128,128]{1,2,0:T(8,128)S(1)} custom-call(f32[8,128,128]{2,1,0:T(8,128)} %get-tuple-element.24), custom_call_target="InvertDiagBlocksLowerTriangular" | custom-call | tf_op jit(solution)/shard_map/triangular_solve | solution.py:26
  (301 shorter events, 147.8 us)
Async XLA Ops:
  110.0 24.7 %copy-start.8 = (f32[8]{0:T(128)S(1)}, f32[8]{0:T(128)}, u32[]{:S(2)}) copy-start(f32[8]{0:T(128)} %param.5) | copy-start | bytes 100
  130.0 16.0 %all-to-all-start.4 = ((f32[16,9,128]{2,1,0:T(8,128)}), f32[16,9,128]{2,1,0:T(8,128)S(1)}, u32[]{:S(2)}, u32[]{:S(2)}) async-start(f32[16,9,128]{2,1,0:T(8,128)} %reshape.296), calls=%async_computation.4 | async-start | bytes 262144 | tf_op jit(solution)/shard_map/all_to_all | solution.py:36
  184.0 36.9 %all-to-all-start.8 = ((f32[4,2,4,16,10,128]{5,1,3,2,4,0:T(2,128)}), f32[4,2,4,16,10,128]{5,1,3,2,4,0:T(2,128)}, u32[]{:S(2)}, u32[]{:S(2)}) async-start(f32[4,2,4,16,10,128]{5,1,3,2,4,0:T(2,128)} %broadcast_in_dim.12), calls=%async_computation.8 | async-start | bytes 5242880 | tf_op jit(solution)/shard_map/all_to_all | solution.py:43
  294.6 11.7 %copy-start.4 = (f32[128,1024]{0,1:T(8,128)S(1)}, f32[128,1024]{0,1:T(8,128)}, u32[]{:S(2)}) copy-start(f32[128,1024]{0,1:T(8,128)} %copy.188) | copy-start | bytes 1572868
  294.6 11.9 %copy-start.7 = (f32[1,128,128]{1,2,0:T(8,128)S(1)}, f32[1,128,128]{1,2,0:T(8,128)}, u32[]{:S(2)}) copy-start(f32[1,128,128]{1,2,0:T(8,128)} %copy.227) | copy-start | bytes 196612
  294.6 11.9 %copy-start.6 = (f32[1,128,128]{1,2,0:T(8,128)S(1)}, f32[1,128,128]{1,2,0:T(8,128)}, u32[]{:S(2)}) copy-start(f32[1,128,128]{1,2,0:T(8,128)} %copy.229) | copy-start | bytes 196612
  294.6 11.9 %copy-start.3 = (f32[128,1024]{0,1:T(8,128)S(1)}, f32[128,1024]{0,1:T(8,128)}, u32[]{:S(2)}) copy-start(f32[128,1024]{0,1:T(8,128)} %copy.189) | copy-start | bytes 1572868
  294.6 12.1 %copy-start.5 = (f32[1,128,128]{1,2,0:T(8,128)S(1)}, f32[1,128,128]{1,2,0:T(8,128)}, u32[]{:S(2)}) copy-start(f32[1,128,128]{1,2,0:T(8,128)} %copy.230) | copy-start | bytes 196612
  306.7 1.9 copy-start.1
  321.0 1.9 copy-start.2
  370.9 2.0 copy-start

commit v2 on v1

--- a/solution.py
+++ b/solution.py
@@ -55,16 +55,41 @@
 
 def unpack_upper(packed, nb):
     where = {pair: k for k, pair in enumerate(upper_pairs(nb))}
-    rows = []
-    for i in range(nb):
-        row = []
-        for j in range(nb):
-            if i <= j:
-                row.append(packed[where[(i, j)]])
-            else:
-                row.append(packed[where[(j, i)]].T)
-        rows.append(jnp.concatenate(row, axis=1))
-    return jnp.concatenate(rows, axis=0)
+    index = np.array(
+        [[where[(min(i, j), max(i, j))] for j in range(nb)] for i in range(nb)]
+    )
+    blocks = packed[index.reshape(-1)].reshape(nb, nb, BLOCK, BLOCK)
+    below = np.arange(nb)[:, None] > np.arange(nb)[None, :]
+    blocks = jnp.where(below[:, :, None, None], jnp.swapaxes(blocks, 2, 3), blocks)
+    return jnp.transpose(blocks, (0, 2, 1, 3)).reshape(nb * BLOCK, nb * BLOCK)
+
+
+def cholesky_solve(system, rhs, nb):
+    hi = lax.Precision.HIGHEST
+    eye = jnp.eye(BLOCK, dtype=jnp.float32)
+    inverses, panels, partial = [], [], []
+    for k in range(nb):
+        lo, up = k * BLOCK, (k + 1) * BLOCK
+        factor = lax.linalg.cholesky(system[lo:up, lo:up], symmetrize_input=False)
+        inverse = lax.linalg.triangular_solve(factor, eye, left_side=True, lower=True)
+        part = jnp.dot(inverse, rhs[lo:up], precision=hi)
+        inverses.append(inverse)
+        partial.append(part)
+        if k + 1 < nb:
+            panel = jnp.dot(system[up:, lo:up], inverse.T, precision=hi)
+            panels.append(panel)
+            trailing = system[up:, up:] - jnp.dot(panel, panel.T, precision=hi)
+            system = system.at[up:, up:].set(trailing)
+            rhs = rhs.at[up:].add(-jnp.dot(panel, part, precision=hi))
+    solved = [None] * nb
+    tail = None
+    for k in reversed(range(nb)):
+        value = partial[k]
+        if tail is not None:
+            value = value - jnp.dot(tail, panels[k], precision=hi)
+        solved[k] = jnp.dot(value, inverses[k], precision=hi)
+        tail = solved[k] if tail is None else jnp.concatenate([solved[k], tail])
+    return jnp.concatenate(solved)
 
 
 def make_on_device(sizes):
@@ -105,8 +130,8 @@
         whole_gram = unpack_upper(whole_packed, nb)
         scaled_energy = (all_energy - jnp.mean(all_energy)) / root_walkers
         identity_mat = jnp.eye(WALKERS, dtype=jnp.float32)
-        factor = jnp.linalg.cholesky(whole_gram + damping * total_params * identity_mat)
-        solved = factor_solve(factor, scaled_energy)
+        system = whole_gram + damping * total_params * identity_mat
+        solved = cholesky_solve(system, scaled_energy, nb)
         update = jnp.dot(solved, centred, precision=lax.Precision.HIGHEST)
         return -(total_params / root_walkers) * update
 

time: 680 us -> 515 us (0.76)
  local copies, waits for them, and re-layouts: 136 us -> 55.7 us
  other arithmetic: 265 us -> 194 us
    another operation x36 -> x42, other arithmetic: 254 us -> 185 us  [the longest x24 99.9 us: cholesky_solve(): factor = lax.linalg.cholesky(system[lo:up, lo:up], symmetrize_input=False)]
    another operation x44 -> x8, matrix products: 46.7 us -> 2.28 us  [cholesky_solve(): lax.linalg.triangular_solve(factor, eye, left_side=True, lower=True)]
    dot_general x0 -> x44, matrix products: none -> 38 us  [the longest x7 17.5 us: cholesky_solve(): trailing = system[up:, up:] - jnp.dot(panel, panel.T, precision=hi)]
    unnamed x142 -> x95, local copies, waits for them, and re-layouts: 61.7 us -> 25.3 us
    another operation x70 -> x0, local copies, waits for them, and re-layouts: 34 us -> none
    transpose x6 -> x1, local copies, waits for them, and re-layouts: 9.32 us -> 2.38 us  [unpack_upper(): return jnp.transpose(blocks, (0, 2, 1, 3)).reshape(nb * BLOCK, nb * BLOCK)]
where the time goes in v2:
time: 515 us; the launch traced here: 506 us
  other arithmetic  194 us (38%)
  blocking collectives  158 us (31%)
  local copies, waits for them, and re-layouts  55.7 us (11%)
  matrix products  44.6 us (9%)
  waiting for transfers between devices  42.4 us (8%)
  starting transfers between devices  8.81 us (2%)
    another operation x24, other arithmetic, cholesky_solve(): factor = lax.linalg.cholesky(system[lo:up, lo:up], symmetrize_input=False)  99.9 us
    another operation x16, other arithmetic, cholesky_solve(): lax.linalg.triangular_solve(factor, eye, left_side=True, lower=True)  83.9 us
    all_to_all x1, blocking collectives, on_device(): lax.all_to_all(log_grads, walk_axes, split_axis=1, concat_axis=0, tiled=T...  74.7 us
    all_to_all x3, blocking collectives, reduce_scatter(): x = lax.all_to_all(parts, axis, 0, 0, tiled=True).sum(0)  49.2 us
    all_to_all x3, blocking collectives, all_gather(): x = lax.all_to_all(copies, axis, 0, 0, tiled=True)  34.5 us
    all_to_all x1, waiting for transfers between devices, all_gather(): x = lax.all_to_all(copies, axis, 0, 0, tiled=True)  31.7 us
    unnamed x95, local copies, waits for them, and re-layouts  25.3 us
    dot_general x7, matrix products, cholesky_solve(): trailing = system[up:, up:] - jnp.dot(panel, panel.T, precision=hi)  17.5 us
  transfers between devices with their start and end apart: 2, of which 2 were waited for; matrix products, arithmetic and copies ran while one was open for 0% of the time, Pallas kernels for 0%

profile of v2, /device:TPU:1, one launch (start us, length us, event | category | flops | bytes accessed | tf_op | source)
XLA Modules:
  0.0 506.2 jit_solution(11232405206612273566)
XLA Ops:
  0.0 74.7 %all_to_all.59 = f32[8,128,256]{2,0,1:T(8,128)S(1)} all-to-all(f32[8,128,256]{2,0,1:T(8,128)} %bitcast.450), channel_id=1, replica_groups=mesh['grp'=4,'wx'=4,'wz'=16,'wc'=2] {'wx','wz','wc'}, dimensions={1} | all-to-all | bytes 2097152 | tf_op jit(solution)/shard_map/all_to_all | solution.py:103
  75.0 3.8 fusion.103
  79.3 30.7 %all_to_all.60 = f32[4,1152,128]{2,1,0:T(8,128)S(1)} all-to-all(f32[4,1152,128]{2,1,0:T(8,128)S(1)} %bitcast.447), channel_id=1, replica_groups=mesh['grp'=4,'wx'=4,'wz'=16,'wc'=2] {'grp'}, dimensions={0} | all-to-all | bytes 4718592 | tf_op jit(solution)/shard_map/all_to_all | solution.py:36
  111.0 8.4 %all_to_all.61 = f32[2,576,128]{2,1,0:T(8,128)S(1)} all-to-all(f32[2,576,128]{2,1,0:T(8,128)} %bitcast.448), channel_id=1, replica_groups=mesh['grp'=4,'wx'=4,'wz'=16,'wc'=2] {'wc'}, dimensions={0} | all-to-all | bytes 1179648 | tf_op jit(solution)/shard_map/all_to_all | solution.py:36
  119.4 10.1 %all_to_all.62 = f32[4,144,128]{2,1,0:T(8,128)S(1)} all-to-all(f32[4,144,128]{2,1,0:T(8,128)S(1)} %bitcast.449), channel_id=1, replica_groups=mesh['grp'=4,'wx'=4,'wz'=16,'wc'=2] {'wx'}, dimensions={0} | all-to-all | bytes 589824 | tf_op jit(solution)/shard_map/all_to_all | solution.py:36
  130.2 4.0 all-to-all-start.4
  135.4 10.7 %all-to-all-done.4 = f32[16,9,128]{2,1,0:T(8,128)S(1)} async-done(((f32[16,9,128]{2,1,0:T(8,128)}), f32[16,9,128]{2,1,0:T(8,128)S(1)}, u32[]{:S(2)}, u32[]{:S(2)}) %all-to-all-start.4) | async-done | bytes 73760 | tf_op jit(solution)/shard_map/all_to_all | solution.py:36
  146.2 17.1 %all_to_all.63 = f32[16,10,128]{2,1,0:T(8,128)S(1)} all-to-all(f32[16,10,128]{2,1,0:T(8,128)S(1)} %broadcast_in_dim.19), channel_id=1, replica_groups=mesh['grp'=4,'wx'=4,'wz'=16,'wc'=2] {'wz'}, dimensions={0} | all-to-all | bytes 163840 | tf_op jit(solution)/shard_map/all_to_all | solution.py:43
  163.3 8.3 %all_to_all.64 = f32[4,16,10,128]{3,1,2,0:T(8,128)S(1)} all-to-all(f32[4,16,10,128]{3,1,2,0:T(8,128)S(1)} %broadcast_in_dim.20), channel_id=1, replica_groups=mesh['grp'=4,'wx'=4,'wz'=16,'wc'=2] {'wx'}, dimensions={0} | all-to-all | bytes 655360 | tf_op jit(solution)/shard_map/all_to_all | solution.py:43
  171.6 9.2 %all_to_all.65 = f32[2,4,16,10,128]{4,2,1,3,0:T(8,128)S(1)} all-to-all(f32[2,4,16,10,128]{4,2,1,3,0:T(8,128)S(1)} %broadcast_in_dim.21), channel_id=1, replica_groups=mesh['grp'=4,'wx'=4,'wz'=16,'wc'=2] {'wc'}, dimensions={0} | all-to-all | bytes 1310720 | tf_op jit(solution)/shard_map/all_to_all | solution.py:43
  181.3 2.8 broadcast_in_dim.44
  184.2 4.8 all-to-all-start.8
  189.1 31.7 %all-to-all-done.8 = f32[4,2,4,16,10,128]{5,1,3,2,4,0:T(2,128)} async-done(((f32[4,2,4,16,10,128]{5,1,3,2,4,0:T(2,128)}), f32[4,2,4,16,10,128]{5,1,3,2,4,0:T(2,128)}, u32[]{:S(2)}, u32[]{:S(2)}) %all-to-all-start.8) | async-done | bytes 2621472 | tf_op jit(solution)/shard_map/all_to_all | solution.py:43
  220.8 1.5 slice_reduce_fusion
  224.0 3.2 slice.612
  227.2 3.4 copy.19
  230.6 3.0 reshape.432
  233.6 2.7 gather_fusion
  236.4 5.4 %copy.20 = f32[8,8,128,128]{2,3,1,0:T(8,128)} copy(f32[8,8,128,128]{3,2,1,0:T(8,128)} %bitcast.442) | data formatting | bytes 8388608 | tf_op jit(solution)/shard_map/reshape | solution.py:61
  241.7 3.9 fusion
  245.7 2.4 copy.21
  249.1 1.9 copy-done
  251.0 11.7 %custom-call.20 = f32[128,128]{1,0:T(8,128)S(1)} custom-call(f32[128,128]{1,0:T(8,128)S(1)} %slice.613), custom_call_target="Cholesky" | custom-call | tf_op jit(solution)/shard_map/cholesky/custom-call.1 | solution.py:73
  264.1 9.8 %custom-call.21 = f32[1,128,128]{1,2,0:T(8,128)S(1)} custom-call(f32[1,128,128]{2,1,0:T(8,128)S(1)} %fusion.52), custom_call_target="InvertDiagBlocksLowerTriangular" | custom-call | tf_op jit(solution)/shard_map/triangular_solve/custom-call.0 | solution.py:74
  274.2 1.6 fusion.24
  275.9 5.3 %slice_subtract_fusion = f32[896,896]{1,0:T(8,128)S(1)} fusion(f32[1024,1024]{1,0:T(8,128)} %copy-done, f32[896,128]{1,0:T(8,128)S(1)} %fusion.24), kind=kOutput, calls=%fused_computation.5 | convolution fusion | flops 1233928192 | bytes 7340032 | tf_op jit(solution)/shard_map/dot_general | solution.py:81
  282.9 11.7 %custom-call.22 = f32[128,128]{1,0:T(8,128)S(1)} custom-call(f32[128,128]{1,0:T(8,128)S(1)} %slice.617), custom_call_target="Cholesky" | custom-call | tf_op jit(solution)/shard_map/cholesky/custom-call.1 | solution.py:73
  296.0 9.8 %custom-call.23 = f32[1,128,128]{1,2,0:T(8,128)S(1)} custom-call(f32[1,128,128]{2,1,0:T(8,128)S(1)} %fusion.53), custom_call_target="InvertDiagBlocksLowerTriangular" | custom-call | tf_op jit(solution)/shard_map/triangular_solve/custom-call.0 | solution.py:74
  306.1 1.5 fusion.26
  307.8 3.7 slice_subtract_fusion.1
  312.9 11.9 %custom-call.24 = f32[128,128]{1,0:T(8,128)S(1)} custom-call(f32[128,128]{1,0:T(8,128)S(1)} %slice.620), custom_call_target="Cholesky" | custom-call | tf_op jit(solution)/shard_map/cholesky/custom-call.1 | solution.py:73
  326.1 9.8 %custom-call.25 = f32[1,128,128]{1,2,0:T(8,128)S(1)} custom-call(f32[1,128,128]{2,1,0:T(8,128)S(1)} %fusion.54), custom_call_target="InvertDiagBlocksLowerTriangular" | custom-call | tf_op jit(solution)/shard_map/triangular_solve/custom-call.0 | solution.py:74
  336.2 1.4 fusion.28
  337.9 2.9 slice_subtract_fusion.2
  342.0 11.7 %custom-call.26 = f32[128,128]{1,0:T(8,128)S(1)} custom-call(f32[128,128]{1,0:T(8,128)S(1)} %slice.623), custom_call_target="Cholesky" | custom-call | tf_op jit(solution)/shard_map/cholesky/custom-call.1 | solution.py:73
  355.0 10.0 %custom-call.27 = f32[1,128,128]{1,2,0:T(8,128)S(1)} custom-call(f32[1,128,128]{2,1,0:T(8,128)S(1)} %fusion.55), custom_call_target="InvertDiagBlocksLowerTriangular" | custom-call | tf_op jit(solution)/shard_map/triangular_solve/custom-call.0 | solution.py:74
  365.3 1.3 fusion.30
  366.8 2.3 convolution_subtract_fusion
  370.1 11.7 %custom-call.28 = f32[128,128]{1,0:T(8,128)S(1)} custom-call(f32[128,128]{1,0:T(8,128)S(1)} %slice.626), custom_call_target="Cholesky" | custom-call | tf_op jit(solution)/shard_map/cholesky/custom-call.1 | solution.py:73
  383.2 9.8 %custom-call.29 = f32[1,128,128]{1,2,0:T(8,128)S(1)} custom-call(f32[1,128,128]{2,1,0:T(8,128)S(1)} %fusion.56), custom_call_target="InvertDiagBlocksLowerTriangular" | custom-call | tf_op jit(solution)/shard_map/triangular_solve/custom-call.0 | solution.py:74
  394.8 1.7 convolution_subtract_fusion.1
  396.9 12.1 %custom-call.30 = f32[128,128]{1,0:T(8,128)S(1)} custom-call(f32[128,128]{1,0:T(8,128)S(1)} %slice.629), custom_call_target="Cholesky" | custom-call | tf_op jit(solution)/shard_map/cholesky/custom-call.1 | solution.py:73
  410.3 9.8 %custom-call.31 = f32[1,128,128]{1,2,0:T(8,128)S(1)} custom-call(f32[1,128,128]{2,1,0:T(8,128)S(1)} %fusion.57), custom_call_target="InvertDiagBlocksLowerTriangular" | custom-call | tf_op jit(solution)/shard_map/triangular_solve/custom-call.0 | solution.py:74
  422.1 11.7 %custom-call.32 = f32[128,128]{1,0:T(8,128)S(1)} custom-call(f32[128,128]{1,0:T(8,128)S(1)} %slice.632), custom_call_target="Cholesky" | custom-call | tf_op jit(solution)/shard_map/cholesky/custom-call.1 | solution.py:73
  435.1 9.8 %custom-call.33 = f32[1,128,128]{1,2,0:T(8,128)S(1)} custom-call(f32[1,128,128]{2,1,0:T(8,128)S(1)} %fusion.58), custom_call_target="InvertDiagBlocksLowerTriangular" | custom-call | tf_op jit(solution)/shard_map/triangular_solve/custom-call.0 | solution.py:74
  447.8 11.9 %custom-call.34 = f32[128,128]{1,0:T(8,128)S(1)} custom-call(f32[128,128]{1,0:T(8,128)S(1)} %convolution_subtract_fusion.3), custom_call_target="Cholesky" | custom-call | tf_op jit(solution)/shard_map/cholesky/custom-call.1 | solution.py:73
  461.1 9.8 %custom-call.35 = f32[1,128,128]{1,2,0:T(8,128)S(1)} custom-call(f32[1,128,128]{2,1,0:T(8,128)S(1)} %fusion.59), custom_call_target="InvertDiagBlocksLowerTriangular" | custom-call | tf_op jit(solution)/shard_map/triangular_solve/custom-call.0 | solution.py:74
  493.9 1.3 constant_dynamic-update-slice_fusion.38
  (212 shorter events, 64.4 us)
Async XLA Ops:
  111.0 23.8 %copy-start.18 = (f32[8]{0:T(128)S(1)}, f32[8]{0:T(128)}, u32[]{:S(2)}) copy-start(f32[8]{0:T(128)} %param.39) | copy-start | bytes 100
  130.2 16.0 %all-to-all-start.4 = ((f32[16,9,128]{2,1,0:T(8,128)}), f32[16,9,128]{2,1,0:T(8,128)S(1)}, u32[]{:S(2)}, u32[]{:S(2)}) async-start(f32[16,9,128]{2,1,0:T(8,128)} %reshape.430), calls=%async_computation.4 | async-start | bytes 262144 | tf_op jit(solution)/shard_map/all_to_all | solution.py:36
  184.2 4.9 copy-start.17
  184.2 36.6 %all-to-all-start.8 = ((f32[4,2,4,16,10,128]{5,1,3,2,4,0:T(2,128)}), f32[4,2,4,16,10,128]{5,1,3,2,4,0:T(2,128)}, u32[]{:S(2)}, u32[]{:S(2)}) async-start(f32[4,2,4,16,10,128]{5,1,3,2,4,0:T(2,128)} %broadcast_in_dim.44), calls=%async_computation.8 | async-start | bytes 5242880 | tf_op jit(solution)/shard_map/all_to_all | solution.py:43
  236.4 5.4 %copy-start.16 = (pred[8,8]{1,0:T(8,128)(4,1)S(1)}, pred[8,8]{1,0:T(8,128)(4,1)}, u32[]{:S(2)}) copy-start(pred[8,8]{1,0:T(8,128)(4,1)} %constant.416) | copy-start | bytes 196
  249.1 1.9 copy-start
  274.2 1.6 copy-start.8
  275.9 5.3 %copy-start.14 = (f32[1,128]{1,0:T(1,128)}, f32[1,128]{1,0:T(1,128)S(1)}, u32[]{:S(2)}) copy-start(f32[1,128]{1,0:T(1,128)S(1)} %fusion.93) | copy-start | bytes 1540
  281.2 1.7 copy-start.1
  306.1 1.5 copy-start.6
  311.5 1.4 copy-start.2
  336.2 1.4 copy-start.7
  337.9 3.4 copy-start.13
  340.8 1.2 copy-start.3
  369.1 1.0 copy-start.4
  394.7 1.8 copy-start.11
  420.4 0.9 copy-start.5
  420.9 0.7 copy-start.12
  421.4 0.7 copy-start.10
  421.4 83.2 %copy-start.9 = (f32[128,128]{1,0:T(8,128)S(1)}, f32[128,128]{1,0:T(8,128)}, u32[]{:S(2)}) copy-start(f32[128,128]{1,0:T(8,128)} %copy-done.8) | copy-start | bytes 196612
  421.4 83.4 %copy-start.15 = (f32[1024]{0:T(1024)S(1)}, f32[1024]{0:T(1024)}, u32[]{:S(2)}) copy-start(f32[1024]{0:T(1024)} %custom-call.36) | copy-start | bytes 12292

commit v3 on v2

--- a/solution.py
+++ b/solution.py
@@ -7,6 +7,8 @@
 
 WALKERS = 1024
 BLOCK = 128
+CG_STEPS = 12
+CG_TOL = 2e-5
 
 
 damping = 0.0004
@@ -92,6 +94,31 @@
     return jnp.concatenate(solved)
 
 
+def certified_cg(system, rhs, lam, steps, tol):
+    hi = lax.Precision.HIGHEST
+    inv_diag = 1.0 / jnp.diagonal(system)
+    x = jnp.zeros_like(rhs)
+    r = rhs
+    z = r * inv_diag
+    p = z
+    rz = jnp.dot(r, z, precision=hi)
+    for _ in range(steps):
+        ap = jnp.dot(system, p, precision=hi)
+        alpha = rz / jnp.dot(p, ap, precision=hi)
+        x = x + alpha * p
+        r = r - alpha * ap
+        z = r * inv_diag
+        rz_next = jnp.dot(r, z, precision=hi)
+        p = z + (rz_next / rz) * p
+        rz = rz_next
+    ax = jnp.dot(system, x, precision=hi)
+    resid = rhs - ax
+    energy = jnp.dot(x, ax, precision=hi) - lam * jnp.dot(x, x, precision=hi)
+    bound = jnp.dot(resid, resid, precision=hi)
+    ok = bound <= (tol * tol) * lam * energy
+    return x, ok
+
+
 def make_on_device(sizes):
     grp, wx, wz, wc = sizes
     levels = [("grp", grp), ("wc", wc), ("wx", wx), ("wz", wz)]
@@ -130,8 +157,17 @@
         whole_gram = unpack_upper(whole_packed, nb)
         scaled_energy = (all_energy - jnp.mean(all_energy)) / root_walkers
         identity_mat = jnp.eye(WALKERS, dtype=jnp.float32)
-        system = whole_gram + damping * total_params * identity_mat
-        solved = cholesky_solve(system, scaled_energy, nb)
+        lam = damping * total_params
+        system = whole_gram + lam * identity_mat
+        guess, ok = certified_cg(system, scaled_energy, lam, CG_STEPS, CG_TOL)
+        solved = lax.cond(
+            ok,
+            lambda a, b, g: g,
+            lambda a, b, g: cholesky_solve(a, b, nb),
+            system,
+            scaled_energy,
+            guess,
+        )
         update = jnp.dot(solved, centred, precision=lax.Precision.HIGHEST)
         return -(total_params / root_walkers) * update
 

time: 515 us -> 680 us (1.32)
  matrix products: 44.6 us -> 126 us
  local copies, waits for them, and re-layouts: 55.7 us -> 86.4 us
  between operations: 1.96 us -> 32.6 us
  other arithmetic: 194 us -> 214 us
    dot_general x0 -> x13, matrix products: none -> 80.7 us  [the longest x12 74.5 us: certified_cg(): ap = jnp.dot(system, p, precision=hi)]
    cond x0 -> x48, local copies, waits for them, and re-layouts: none -> 32.1 us
    unnamed x95 -> x43, local copies, waits for them, and re-layouts: 25.3 us -> 0.28 us
    gather x0 -> x1, local copies, waits for them, and re-layouts: none -> 17.7 us  [certified_cg(): inv_diag = 1.0 / jnp.diagonal(system)]
    dot_general x0 -> x25, other arithmetic: none -> 16.6 us  [the longest x12 7.25 us: certified_cg(): alpha = rz / jnp.dot(p, ap, precision=hi)]
    add x1 -> x14, other arithmetic: 1.01 us -> 7.93 us  [the longest x2 7.22 us: on_device(): system = whole_gram + lam * identity_mat]
where the time goes in v3:
time: 680 us; the launch traced here: 670 us
  other arithmetic  214 us (31%)
  blocking collectives  158 us (23%)
  matrix products  126 us (19%)
  local copies, waits for them, and re-layouts  86.4 us (13%)
  waiting for transfers between devices  42.4 us (6%)
  between operations  32.6 us (5%)
  starting transfers between devices  8.75 us (1%)
    another operation x24, other arithmetic, cholesky_solve(): factor = lax.linalg.cholesky(system[lo:up, lo:up], symmetrize_input=False)  99.8 us
    another operation x16, other arithmetic, cholesky_solve(): lax.linalg.triangular_solve(factor, eye, left_side=True, lower=True)  84.5 us
    all_to_all x1, blocking collectives, on_device(): lax.all_to_all(log_grads, walk_axes, split_axis=1, concat_axis=0, tiled=T...  74.7 us
    dot_general x12, matrix products, certified_cg(): ap = jnp.dot(system, p, precision=hi)  74.5 us
    all_to_all x3, blocking collectives, reduce_scatter(): x = lax.all_to_all(parts, axis, 0, 0, tiled=True).sum(0)  49 us
    all_to_all x3, blocking collectives, all_gather(): x = lax.all_to_all(copies, axis, 0, 0, tiled=True)  34.5 us
    cond x48, local copies, waits for them, and re-layouts  32.1 us
    all_to_all x1, waiting for transfers between devices, all_gather(): x = lax.all_to_all(copies, axis, 0, 0, tiled=True)  31.7 us
  transfers between devices with their start and end apart: 2, of which 2 were waited for; matrix products, arithmetic and copies ran while one was open for 0% of the time, Pallas kernels for 0%

profile of v3, /device:TPU:1, one launch (start us, length us, event | category | flops | bytes accessed | tf_op | source)
XLA Modules:
  0.0 669.5 jit_solution(382922778819930322)
XLA Ops:
  0.0 74.7 %all_to_all.59 = f32[8,128,256]{2,0,1:T(8,128)S(1)} all-to-all(f32[8,128,256]{2,0,1:T(8,128)} %bitcast.526), channel_id=1, replica_groups=mesh['grp'=4,'wx'=4,'wz'=16,'wc'=2] {'wx','wz','wc'}, dimensions={1} | all-to-all | bytes 2097152 | tf_op jit(solution)/shard_map/all_to_all | solution.py:130
  75.0 3.8 fusion.134
  79.3 30.7 %all_to_all.60 = f32[4,1152,128]{2,1,0:T(8,128)S(1)} all-to-all(f32[4,1152,128]{2,1,0:T(8,128)S(1)} %bitcast.523), channel_id=1, replica_groups=mesh['grp'=4,'wx'=4,'wz'=16,'wc'=2] {'grp'}, dimensions={0} | all-to-all | bytes 4718592 | tf_op jit(solution)/shard_map/all_to_all | solution.py:38
  111.0 8.3 %all_to_all.61 = f32[2,576,128]{2,1,0:T(8,128)S(1)} all-to-all(f32[2,576,128]{2,1,0:T(8,128)} %bitcast.524), channel_id=1, replica_groups=mesh['grp'=4,'wx'=4,'wz'=16,'wc'=2] {'wc'}, dimensions={0} | all-to-all | bytes 1179648 | tf_op jit(solution)/shard_map/all_to_all | solution.py:38
  119.3 10.1 %all_to_all.62 = f32[4,144,128]{2,1,0:T(8,128)S(1)} all-to-all(f32[4,144,128]{2,1,0:T(8,128)S(1)} %bitcast.525), channel_id=1, replica_groups=mesh['grp'=4,'wx'=4,'wz'=16,'wc'=2] {'wx'}, dimensions={0} | all-to-all | bytes 589824 | tf_op jit(solution)/shard_map/all_to_all | solution.py:38
  130.0 4.0 all-to-all-start.4
  135.3 10.7 %all-to-all-done.4 = f32[16,9,128]{2,1,0:T(8,128)S(1)} async-done(((f32[16,9,128]{2,1,0:T(8,128)}), f32[16,9,128]{2,1,0:T(8,128)S(1)}, u32[]{:S(2)}, u32[]{:S(2)}) %all-to-all-start.4) | async-done | bytes 73760 | tf_op jit(solution)/shard_map/all_to_all | solution.py:38
  146.1 17.0 %all_to_all.63 = f32[16,10,128]{2,1,0:T(8,128)S(1)} all-to-all(f32[16,10,128]{2,1,0:T(8,128)S(1)} %broadcast_in_dim.19), channel_id=1, replica_groups=mesh['grp'=4,'wx'=4,'wz'=16,'wc'=2] {'wz'}, dimensions={0} | all-to-all | bytes 163840 | tf_op jit(solution)/shard_map/all_to_all | solution.py:45
  163.2 8.3 %all_to_all.64 = f32[4,16,10,128]{3,1,2,0:T(8,128)S(1)} all-to-all(f32[4,16,10,128]{3,1,2,0:T(8,128)S(1)} %broadcast_in_dim.20), channel_id=1, replica_groups=mesh['grp'=4,'wx'=4,'wz'=16,'wc'=2] {'wx'}, dimensions={0} | all-to-all | bytes 655360 | tf_op jit(solution)/shard_map/all_to_all | solution.py:45
  171.5 9.2 %all_to_all.65 = f32[2,4,16,10,128]{4,2,1,3,0:T(8,128)S(1)} all-to-all(f32[2,4,16,10,128]{4,2,1,3,0:T(8,128)S(1)} %broadcast_in_dim.21), channel_id=1, replica_groups=mesh['grp'=4,'wx'=4,'wz'=16,'wc'=2] {'wc'}, dimensions={0} | all-to-all | bytes 1310720 | tf_op jit(solution)/shard_map/all_to_all | solution.py:45
  184.0 4.8 all-to-all-start.8
  188.9 31.7 %all-to-all-done.8 = f32[4,2,4,16,10,128]{5,1,3,2,4,0:T(2,128)} async-done(((f32[4,2,4,16,10,128]{5,1,3,2,4,0:T(2,128)}), f32[4,2,4,16,10,128]{5,1,3,2,4,0:T(2,128)}, u32[]{:S(2)}, u32[]{:S(2)}) %all-to-all-start.8) | async-done | bytes 2621472 | tf_op jit(solution)/shard_map/all_to_all | solution.py:45
  232.4 5.4 copy.25
  237.7 4.1 select_add_fusion
  241.8 4.3 copy.27
  251.7 17.7 %gather_fusion.1 = f32[1024]{0:T(1024)S(1)} fusion(f32[1024,1024]{1,0:T(8,128)} %bitcast_add_fusion, s32[1024]{0:T(1024)S(1)} %bitcast.504), kind=kCustom, calls=%fused_computation.1 | custom fusion | bytes 16384 | tf_op jit(solution)/shard_map/jit(diagonal)/cond/branch_0_fun/gather | solution.py:99
  273.5 6.1 fusion.96
  283.3 6.1 fusion.131
  293.2 6.2 fusion.130
  303.1 6.3 fusion.129
  313.2 6.1 fusion.128
  323.0 6.2 fusion.127
  332.9 6.2 fusion.126
  342.8 6.4 fusion.125
  352.9 6.1 fusion.124
  362.8 6.2 fusion.123
  372.7 6.6 fusion.122
  382.9 6.1 fusion.121
  391.6 6.2 fusion.120
  400.9 266.2 %conditional.1 = (f32[1024]{0:T(1024)}) conditional(s32[]{:T(128)} %convert_element_type.21, (f32[1024,1024]{1,0:T(8,128)}, f32[1024]{0:T(1024)S(1)}) %tuple.73, f32[1024]{0:T(1024)} %multiply_add_fusion), branch_computations={%region_7.12_spmd, %region_10.13_spmd} | conditional | flops 4446824960 | bytes 69705616 | solution.py:163
  402.0 11.7 %custom-call.22 = f32[128,128]{1,0:T(8,128)S(1)} custom-call(f32[128,128]{1,0:T(8,128)S(1)} %slice.428), custom_call_target="Cholesky" | custom-call | tf_op jit(solution)/shard_map/cond/branch_0_fun/cholesky/custom-call.1 | solution.py:75
  414.9 9.8 %custom-call.23 = f32[1,128,128]{1,2,0:T(8,128)S(1)} custom-call(f32[1,128,128]{2,1,0:T(8,128)S(1)} %fusion.47), custom_call_target="InvertDiagBlocksLowerTriangular" | custom-call | tf_op jit(solution)/shard_map/cond/branch_0_fun/triangular_solve/custom-call.0 | solution.py:76
  426.9 4.8 slice_subtract_fusion
  433.4 11.9 %custom-call.24 = f32[128,128]{1,0:T(8,128)S(1)} custom-call(f32[128,128]{1,0:T(8,128)S(1)} %slice.543), custom_call_target="Cholesky" | custom-call | tf_op jit(solution)/shard_map/cond/branch_0_fun/cholesky/custom-call.1 | solution.py:75
  446.8 9.8 %custom-call.25 = f32[1,128,128]{1,2,0:T(8,128)S(1)} custom-call(f32[1,128,128]{2,1,0:T(8,128)S(1)} %fusion.48), custom_call_target="InvertDiagBlocksLowerTriangular" | custom-call | tf_op jit(solution)/shard_map/cond/branch_0_fun/triangular_solve/custom-call.0 | solution.py:76
  458.6 3.7 slice_subtract_fusion.1
  463.7 11.7 %custom-call.26 = f32[128,128]{1,0:T(8,128)S(1)} custom-call(f32[128,128]{1,0:T(8,128)S(1)} %slice.546), custom_call_target="Cholesky" | custom-call | tf_op jit(solution)/shard_map/cond/branch_0_fun/cholesky/custom-call.1 | solution.py:75
  476.9 10.2 %custom-call.27 = f32[1,128,128]{1,2,0:T(8,128)S(1)} custom-call(f32[1,128,128]{2,1,0:T(8,128)S(1)} %fusion.49), custom_call_target="InvertDiagBlocksLowerTriangular" | custom-call | tf_op jit(solution)/shard_map/cond/branch_0_fun/triangular_solve/custom-call.0 | solution.py:76
  493.1 11.7 %custom-call.28 = f32[128,128]{1,0:T(8,128)S(1)} custom-call(f32[128,128]{1,0:T(8,128)S(1)} %slice.549), custom_call_target="Cholesky" | custom-call | tf_op jit(solution)/shard_map/cond/branch_0_fun/cholesky/custom-call.1 | solution.py:75
  506.2 9.8 %custom-call.29 = f32[1,128,128]{1,2,0:T(8,128)S(1)} custom-call(f32[1,128,128]{2,1,0:T(8,128)S(1)} %fusion.50), custom_call_target="InvertDiagBlocksLowerTriangular" | custom-call | tf_op jit(solution)/shard_map/cond/branch_0_fun/triangular_solve/custom-call.0 | solution.py:76
  521.1 11.9 %custom-call.30 = f32[128,128]{1,0:T(8,128)S(1)} custom-call(f32[128,128]{1,0:T(8,128)S(1)} %slice.552), custom_call_target="Cholesky" | custom-call | tf_op jit(solution)/shard_map/cond/branch_0_fun/cholesky/custom-call.1 | solution.py:75
  534.3 9.8 %custom-call.31 = f32[1,128,128]{1,2,0:T(8,128)S(1)} custom-call(f32[1,128,128]{2,1,0:T(8,128)S(1)} %fusion.51), custom_call_target="InvertDiagBlocksLowerTriangular" | custom-call | tf_op jit(solution)/shard_map/cond/branch_0_fun/triangular_solve/custom-call.0 | solution.py:76
  548.0 11.7 %custom-call.32 = f32[128,128]{1,0:T(8,128)S(1)} custom-call(f32[128,128]{1,0:T(8,128)S(1)} %slice.555), custom_call_target="Cholesky" | custom-call | tf_op jit(solution)/shard_map/cond/branch_0_fun/cholesky/custom-call.1 | solution.py:75
  561.1 10.0 %custom-call.33 = f32[1,128,128]{1,2,0:T(8,128)S(1)} custom-call(f32[1,128,128]{2,1,0:T(8,128)S(1)} %fusion.52), custom_call_target="InvertDiagBlocksLowerTriangular" | custom-call | tf_op jit(solution)/shard_map/cond/branch_0_fun/triangular_solve/custom-call.0 | solution.py:76
  573.0 11.7 %custom-call.34 = f32[128,128]{1,0:T(8,128)S(1)} custom-call(f32[128,128]{1,0:T(8,128)S(1)} %slice.558), custom_call_target="Cholesky" | custom-call | tf_op jit(solution)/shard_map/cond/branch_0_fun/cholesky/custom-call.1 | solution.py:75
  586.1 9.8 %custom-call.35 = f32[1,128,128]{1,2,0:T(8,128)S(1)} custom-call(f32[1,128,128]{2,1,0:T(8,128)S(1)} %fusion.53), custom_call_target="InvertDiagBlocksLowerTriangular" | custom-call | tf_op jit(solution)/shard_map/cond/branch_0_fun/triangular_solve/custom-call.0 | solution.py:76
  598.9 11.8 %custom-call.36 = f32[128,128]{1,0:T(8,128)S(1)} custom-call(f32[128,128]{1,0:T(8,128)S(1)} %convolution_subtract_fusion.3), custom_call_target="Cholesky" | custom-call | tf_op jit(solution)/shard_map/cond/branch_0_fun/cholesky/custom-call.1 | solution.py:75
  612.1 10.0 %custom-call.37 = f32[1,128,128]{1,2,0:T(8,128)S(1)} custom-call(f32[1,128,128]{2,1,0:T(8,128)S(1)} %fusion.54), custom_call_target="InvertDiagBlocksLowerTriangular" | custom-call | tf_op jit(solution)/shard_map/cond/branch_0_fun/triangular_solve/custom-call.0 | solution.py:76
  (265 shorter events, 128.8 us)
Async XLA Ops:
  110.0 24.7 %copy-start.16 = (f32[8]{0:T(128)S(1)}, f32[8]{0:T(128)}, u32[]{:S(2)}) copy-start(f32[8]{0:T(128)} %param.41) | copy-start | bytes 100
  130.0 16.0 %all-to-all-start.4 = ((f32[16,9,128]{2,1,0:T(8,128)}), f32[16,9,128]{2,1,0:T(8,128)S(1)}, u32[]{:S(2)}, u32[]{:S(2)}) async-start(f32[16,9,128]{2,1,0:T(8,128)} %reshape.462), calls=%async_computation.4 | async-start | bytes 262144 | tf_op jit(solution)/shard_map/all_to_all | solution.py:38
  181.2 7.7 %copy-start.15 = (s32[64]{0:T(128)S(1)}, s32[64]{0:T(128)}, u32[]{:S(2)}) copy-start(s32[64]{0:T(128)} %constant.445) | copy-start | bytes 772
  184.0 36.5 %all-to-all-start.8 = ((f32[4,2,4,16,10,128]{5,1,3,2,4,0:T(2,128)}), f32[4,2,4,16,10,128]{5,1,3,2,4,0:T(2,128)}, u32[]{:S(2)}, u32[]{:S(2)}) async-start(f32[4,2,4,16,10,128]{5,1,3,2,4,0:T(2,128)} %broadcast_in_dim.25), calls=%async_computation.8 | async-start | bytes 5242880 | tf_op jit(solution)/shard_map/all_to_all | solution.py:45
  232.4 5.4 copy-start.14
  248.5 3.2 copy-start
  425.1 6.7 copy-start.8
  425.2 6.9 %copy-start.13 = (f32[1,128]{1,0:T(1,128)}, f32[1,128]{1,0:T(1,128)S(1)}, u32[]{:S(2)}) copy-start(f32[1,128]{1,0:T(1,128)S(1)} %fusion.87) | copy-start | bytes 1540 | tf_op jit(solution)/shard_map/cond
  431.7 1.7 copy-start.1
  456.9 30.5 %copy-start.6 = (f32[128,128]{1,0:T(8,128)}, f32[128,128]{1,0:T(8,128)S(1)}, u32[]{:S(2)}) copy-start(f32[128,128]{1,0:T(8,128)S(1)} %fusion.39) | copy-start | bytes 196612 | tf_op jit(solution)/shard_map/cond
  462.3 1.4 copy-start.2
  487.4 28.9 %copy-start.7 = (f32[128,128]{1,0:T(8,128)}, f32[128,128]{1,0:T(8,128)S(1)}, u32[]{:S(2)}) copy-start(f32[128,128]{1,0:T(8,128)S(1)} %fusion.37) | copy-start | bytes 196612 | tf_op jit(solution)/shard_map/cond
  487.6 18.6 %copy-start.12 = (f32[1,128]{1,0:T(1,128)}, f32[1,128]{1,0:T(1,128)S(1)}, u32[]{:S(2)}) copy-start(f32[1,128]{1,0:T(1,128)S(1)} %fusion.81) | copy-start | bytes 1540 | tf_op jit(solution)/shard_map/cond
  491.9 1.2 copy-start.3
  516.5 17.8 %copy-start.10 = (f32[1,128]{1,0:T(1,128)}, f32[1,128]{1,0:T(1,128)S(1)}, u32[]{:S(2)}) copy-start(f32[1,128]{1,0:T(1,128)S(1)} %fusion.78) | copy-start | bytes 1540 | tf_op jit(solution)/shard_map/cond
  520.1 1.0 copy-start.4
  544.6 3.0 copy-start.11
  571.3 0.9 copy-start.5
  572.3 0.7 copy-start.9

commit v4 on v3

--- a/solution.py
+++ b/solution.py
@@ -62,7 +62,10 @@
     )
     blocks = packed[index.reshape(-1)].reshape(nb, nb, BLOCK, BLOCK)
     below = np.arange(nb)[:, None] > np.arange(nb)[None, :]
-    blocks = jnp.where(below[:, :, None, None], jnp.swapaxes(blocks, 2, 3), blocks)
+    inner = np.arange(BLOCK)[:, None] > np.arange(BLOCK)[None, :]
+    diag = np.eye(nb, dtype=bool)
+    mirror = below[:, :, None, None] | (diag[:, :, None, None] & inner[None, None])
+    blocks = jnp.where(mirror, jnp.swapaxes(blocks, 2, 3), blocks)
     return jnp.transpose(blocks, (0, 2, 1, 3)).reshape(nb * BLOCK, nb * BLOCK)
 
 
@@ -94,16 +97,21 @@
     return jnp.concatenate(solved)
 
 
+def sym_matvec(system, v):
+    return jnp.sum(system * v[:, None], axis=0)
+
+
 def certified_cg(system, rhs, lam, steps, tol):
     hi = lax.Precision.HIGHEST
-    inv_diag = 1.0 / jnp.diagonal(system)
+    eye = np.eye(system.shape[0], dtype=bool)
+    inv_diag = 1.0 / jnp.sum(jnp.where(eye, system, 0.0), axis=0)
     x = jnp.zeros_like(rhs)
     r = rhs
     z = r * inv_diag
     p = z
     rz = jnp.dot(r, z, precision=hi)
     for _ in range(steps):
-        ap = jnp.dot(system, p, precision=hi)
+        ap = sym_matvec(system, p)
         alpha = rz / jnp.dot(p, ap, precision=hi)
         x = x + alpha * p
         r = r - alpha * ap
@@ -111,7 +119,7 @@
         rz_next = jnp.dot(r, z, precision=hi)
         p = z + (rz_next / rz) * p
         rz = rz_next
-    ax = jnp.dot(system, x, precision=hi)
+    ax = sym_matvec(system, x)
     resid = rhs - ax
     energy = jnp.dot(x, ax, precision=hi) - lam * jnp.dot(x, x, precision=hi)
     bound = jnp.dot(resid, resid, precision=hi)

time: 680 us -> 589 us (0.87)
  matrix products: 126 us -> 45.8 us
  local copies, waits for them, and re-layouts: 86.4 us -> 40.2 us
  other arithmetic: 214 us -> 251 us
    dot_general x13 -> x0, matrix products: 80.7 us -> none  [the longest x12 74.5 us: certified_cg(): ap = jnp.dot(system, p, precision=hi)]
    reduce_sum x0 -> x13, other arithmetic: none -> 34.9 us  [sym_matvec(): return jnp.sum(system * v[:, None], axis=0)]
    cond x48, local copies, waits for them, and re-layouts: 32.1 us -> 6.88 us
    gather x1 -> x0, local copies, waits for them, and re-layouts: 17.7 us -> none  [certified_cg(): inv_diag = 1.0 / jnp.diagonal(system)]
where the time goes in v4:
time: 589 us; the launch traced here: 581 us
  other arithmetic  251 us (43%)
  blocking collectives  158 us (27%)
  matrix products  45.8 us (8%)
  waiting for transfers between devices  42.5 us (7%)
  local copies, waits for them, and re-layouts  40.2 us (7%)
  between operations  32.3 us (5%)
  starting transfers between devices  8.79 us (1%)
    another operation x24, other arithmetic, cholesky_solve(): factor = lax.linalg.cholesky(system[lo:up, lo:up], symmetrize_input=False)  99.6 us
    another operation x16, other arithmetic, cholesky_solve(): lax.linalg.triangular_solve(factor, eye, left_side=True, lower=True)  84.3 us
    all_to_all x1, blocking collectives, on_device(): lax.all_to_all(log_grads, walk_axes, split_axis=1, concat_axis=0, tiled=T...  74.7 us
    all_to_all x3, blocking collectives, reduce_scatter(): x = lax.all_to_all(parts, axis, 0, 0, tiled=True).sum(0)  49 us
    reduce_sum x13, other arithmetic, sym_matvec(): return jnp.sum(system * v[:, None], axis=0)  34.9 us
    all_to_all x3, blocking collectives, all_gather(): x = lax.all_to_all(copies, axis, 0, 0, tiled=True)  34.5 us
    all_to_all x1, waiting for transfers between devices, all_gather(): x = lax.all_to_all(copies, axis, 0, 0, tiled=True)  31.7 us
    dot_general x7, matrix products, cholesky_solve(): trailing = system[up:, up:] - jnp.dot(panel, panel.T, precision=hi)  16.8 us
  transfers between devices with their start and end apart: 2, of which 2 were waited for; matrix products, arithmetic and copies ran while one was open for 0% of the time, Pallas kernels for 0%

profile of v4, /device:TPU:1, one launch (start us, length us, event | category | flops | bytes accessed | tf_op | source)
XLA Modules:
  0.0 580.5 jit_solution(8853793101374724830)
XLA Ops:
  0.0 74.7 %all_to_all.59 = f32[8,128,256]{2,0,1:T(8,128)S(1)} all-to-all(f32[8,128,256]{2,0,1:T(8,128)} %bitcast.622), channel_id=1, replica_groups=mesh['grp'=4,'wx'=4,'wz'=16,'wc'=2] {'wx','wz','wc'}, dimensions={1} | all-to-all | bytes 2097152 | tf_op jit(solution)/shard_map/all_to_all | solution.py:138
  75.5 3.8 fusion.135
  79.8 30.7 %all_to_all.60 = f32[4,1152,128]{2,1,0:T(8,128)S(1)} all-to-all(f32[4,1152,128]{2,1,0:T(8,128)S(1)} %bitcast.598), channel_id=1, replica_groups=mesh['grp'=4,'wx'=4,'wz'=16,'wc'=2] {'grp'}, dimensions={0} | all-to-all | bytes 4718592 | tf_op jit(solution)/shard_map/all_to_all | solution.py:38
  111.4 8.3 %all_to_all.61 = f32[2,576,128]{2,1,0:T(8,128)S(1)} all-to-all(f32[2,576,128]{2,1,0:T(8,128)} %bitcast.599), channel_id=1, replica_groups=mesh['grp'=4,'wx'=4,'wz'=16,'wc'=2] {'wc'}, dimensions={0} | all-to-all | bytes 1179648 | tf_op jit(solution)/shard_map/all_to_all | solution.py:38
  119.8 10.1 %all_to_all.62 = f32[4,144,128]{2,1,0:T(8,128)S(1)} all-to-all(f32[4,144,128]{2,1,0:T(8,128)S(1)} %bitcast.600), channel_id=1, replica_groups=mesh['grp'=4,'wx'=4,'wz'=16,'wc'=2] {'wx'}, dimensions={0} | all-to-all | bytes 589824 | tf_op jit(solution)/shard_map/all_to_all | solution.py:38
  130.5 4.0 all-to-all-start.4
  135.7 10.8 %all-to-all-done.4 = f32[16,9,128]{2,1,0:T(8,128)S(1)} async-done(((f32[16,9,128]{2,1,0:T(8,128)}), f32[16,9,128]{2,1,0:T(8,128)S(1)}, u32[]{:S(2)}, u32[]{:S(2)}) %all-to-all-start.4) | async-done | bytes 73760 | tf_op jit(solution)/shard_map/all_to_all | solution.py:38
  146.5 17.1 %all_to_all.63 = f32[16,10,128]{2,1,0:T(8,128)S(1)} all-to-all(f32[16,10,128]{2,1,0:T(8,128)S(1)} %broadcast_in_dim.11), channel_id=1, replica_groups=mesh['grp'=4,'wx'=4,'wz'=16,'wc'=2] {'wz'}, dimensions={0} | all-to-all | bytes 163840 | tf_op jit(solution)/shard_map/all_to_all | solution.py:45
  163.6 8.3 %all_to_all.64 = f32[4,16,10,128]{3,1,2,0:T(8,128)S(1)} all-to-all(f32[4,16,10,128]{3,1,2,0:T(8,128)S(1)} %broadcast_in_dim.12), channel_id=1, replica_groups=mesh['grp'=4,'wx'=4,'wz'=16,'wc'=2] {'wx'}, dimensions={0} | all-to-all | bytes 655360 | tf_op jit(solution)/shard_map/all_to_all | solution.py:45
  172.0 9.2 %all_to_all.65 = f32[2,4,16,10,128]{4,2,1,3,0:T(8,128)S(1)} all-to-all(f32[2,4,16,10,128]{4,2,1,3,0:T(8,128)S(1)} %broadcast_in_dim.13), channel_id=1, replica_groups=mesh['grp'=4,'wx'=4,'wz'=16,'wc'=2] {'wc'}, dimensions={0} | all-to-all | bytes 1310720 | tf_op jit(solution)/shard_map/all_to_all | solution.py:45
  181.7 2.8 broadcast_in_dim.14
  184.5 4.8 all-to-all-start.8
  189.4 31.7 %all-to-all-done.8 = f32[4,2,4,16,10,128]{5,1,3,2,4,0:T(2,128)} async-done(((f32[4,2,4,16,10,128]{5,1,3,2,4,0:T(2,128)}), f32[4,2,4,16,10,128]{5,1,3,2,4,0:T(2,128)}, u32[]{:S(2)}, u32[]{:S(2)}) %all-to-all-start.8) | async-done | bytes 2621472 | tf_op jit(solution)/shard_map/all_to_all | solution.py:45
  221.1 3.2 slice.596
  224.3 3.4 copy.22
  227.7 3.0 reshape.1348
  230.7 2.7 gather_fusion
  233.5 5.4 copy.23
  238.9 4.4 fusion.96
  245.7 3.1 bitcast_add_fusion
  266.5 2.7 multiply_reduce_fusion.10
  273.2 2.7 multiply_reduce_fusion.9
  279.9 3.1 multiply_reduce_fusion.8
  287.0 2.7 multiply_reduce_fusion.7
  300.5 2.7 multiply_reduce_fusion.5
  307.3 2.7 multiply_reduce_fusion.4
  314.0 2.7 multiply_reduce_fusion.3
  320.7 2.7 multiply_reduce_fusion.2
  344.4 233.8 %conditional.1 = (f32[1024]{0:T(1024)S(1)}) conditional(s32[]{:T(128)} %convert_element_type.21, (f32[1024,1024]{1,0:T(8,128)}, f32[1024]{0:T(1024)S(1)}) %tuple.85, (f32[1024]{0:T(1024)}, f32[1024]{0:T(1024)}, f32[]{:T(128)}, f32[1024]{0:T(1024)}, f32[1024]{0:T(1024)}, /*index=5*/f32[1024]{0:T(1024)}, f32[1024]{0:T(1024)}, ...), branch_computations={%region_21.26_spmd, %region_24.27_spmd.clone.clone} | conditional | flops 4446824960 | bytes 69705600 | solution.py:171
  345.4 11.7 %custom-call.20 = f32[128,128]{1,0:T(8,128)S(1)} custom-call(f32[128,128]{1,0:T(8,128)S(1)} %slice.428), custom_call_target="Cholesky" | custom-call | tf_op jit(solution)/shard_map/cond/branch_0_fun/cholesky/custom-call.1 | solution.py:78
  358.4 9.8 %custom-call.21 = f32[1,128,128]{1,2,0:T(8,128)S(1)} custom-call(f32[1,128,128]{2,1,0:T(8,128)S(1)} %fusion.47), custom_call_target="InvertDiagBlocksLowerTriangular" | custom-call | tf_op jit(solution)/shard_map/cond/branch_0_fun/triangular_solve/custom-call.0 | solution.py:79
  370.2 4.8 slice_subtract_fusion
  376.7 11.9 %custom-call.22 = f32[128,128]{1,0:T(8,128)S(1)} custom-call(f32[128,128]{1,0:T(8,128)S(1)} %slice.541), custom_call_target="Cholesky" | custom-call | tf_op jit(solution)/shard_map/cond/branch_0_fun/cholesky/custom-call.1 | solution.py:78
  390.0 9.8 %custom-call.23 = f32[1,128,128]{1,2,0:T(8,128)S(1)} custom-call(f32[1,128,128]{2,1,0:T(8,128)S(1)} %fusion.48), custom_call_target="InvertDiagBlocksLowerTriangular" | custom-call | tf_op jit(solution)/shard_map/cond/branch_0_fun/triangular_solve/custom-call.0 | solution.py:79
  401.7 3.7 slice_subtract_fusion.1
  406.8 11.7 %custom-call.24 = f32[128,128]{1,0:T(8,128)S(1)} custom-call(f32[128,128]{1,0:T(8,128)S(1)} %slice.544), custom_call_target="Cholesky" | custom-call | tf_op jit(solution)/shard_map/cond/branch_0_fun/cholesky/custom-call.1 | solution.py:78
  419.8 10.2 %custom-call.25 = f32[1,128,128]{1,2,0:T(8,128)S(1)} custom-call(f32[1,128,128]{2,1,0:T(8,128)S(1)} %fusion.49), custom_call_target="InvertDiagBlocksLowerTriangular" | custom-call | tf_op jit(solution)/shard_map/cond/branch_0_fun/triangular_solve/custom-call.0 | solution.py:79
  434.3 2.9 slice_subtract_fusion.2
  438.4 11.7 %custom-call.26 = f32[128,128]{1,0:T(8,128)S(1)} custom-call(f32[128,128]{1,0:T(8,128)S(1)} %slice.547), custom_call_target="Cholesky" | custom-call | tf_op jit(solution)/shard_map/cond/branch_0_fun/cholesky/custom-call.1 | solution.py:78
  451.5 9.8 %custom-call.27 = f32[1,128,128]{1,2,0:T(8,128)S(1)} custom-call(f32[1,128,128]{2,1,0:T(8,128)S(1)} %fusion.50), custom_call_target="InvertDiagBlocksLowerTriangular" | custom-call | tf_op jit(solution)/shard_map/cond/branch_0_fun/triangular_solve/custom-call.0 | solution.py:79
  466.7 11.9 %custom-call.28 = f32[128,128]{1,0:T(8,128)S(1)} custom-call(f32[128,128]{1,0:T(8,128)S(1)} %slice.550), custom_call_target="Cholesky" | custom-call | tf_op jit(solution)/shard_map/cond/branch_0_fun/cholesky/custom-call.1 | solution.py:78
  480.0 9.8 %custom-call.29 = f32[1,128,128]{1,2,0:T(8,128)S(1)} custom-call(f32[1,128,128]{2,1,0:T(8,128)S(1)} %fusion.51), custom_call_target="InvertDiagBlocksLowerTriangular" | custom-call | tf_op jit(solution)/shard_map/cond/branch_0_fun/triangular_solve/custom-call.0 | solution.py:79
  493.6 11.7 %custom-call.30 = f32[128,128]{1,0:T(8,128)S(1)} custom-call(f32[128,128]{1,0:T(8,128)S(1)} %slice.553), custom_call_target="Cholesky" | custom-call | tf_op jit(solution)/shard_map/cond/branch_0_fun/cholesky/custom-call.1 | solution.py:78
  506.7 10.0 %custom-call.31 = f32[1,128,128]{1,2,0:T(8,128)S(1)} custom-call(f32[1,128,128]{2,1,0:T(8,128)S(1)} %fusion.52), custom_call_target="InvertDiagBlocksLowerTriangular" | custom-call | tf_op jit(solution)/shard_map/cond/branch_0_fun/triangular_solve/custom-call.0 | solution.py:79
  518.9 11.7 %custom-call.32 = f32[128,128]{1,0:T(8,128)S(1)} custom-call(f32[128,128]{1,0:T(8,128)S(1)} %slice.556), custom_call_target="Cholesky" | custom-call | tf_op jit(solution)/shard_map/cond/branch_0_fun/cholesky/custom-call.1 | solution.py:78
  531.9 9.8 %custom-call.33 = f32[1,128,128]{1,2,0:T(8,128)S(1)} custom-call(f32[1,128,128]{2,1,0:T(8,128)S(1)} %fusion.53), custom_call_target="InvertDiagBlocksLowerTriangular" | custom-call | tf_op jit(solution)/shard_map/cond/branch_0_fun/triangular_solve/custom-call.0 | solution.py:79
  544.6 11.7 %custom-call.34 = f32[128,128]{1,0:T(8,128)S(1)} custom-call(f32[128,128]{1,0:T(8,128)S(1)} %convolution_subtract_fusion.3), custom_call_target="Cholesky" | custom-call | tf_op jit(solution)/shard_map/cond/branch_0_fun/cholesky/custom-call.1 | solution.py:78
  557.6 10.0 %custom-call.35 = f32[1,128,128]{1,2,0:T(8,128)S(1)} custom-call(f32[1,128,128]{2,1,0:T(8,128)S(1)} %fusion.54), custom_call_target="InvertDiagBlocksLowerTriangular" | custom-call | tf_op jit(solution)/shard_map/cond/branch_0_fun/triangular_solve/custom-call.0 | solution.py:79
  (327 shorter events, 99.2 us)
Async XLA Ops:
  74.9 0.6 copy-start.13
  110.5 24.7 %copy-start.19 = (f32[8]{0:T(128)S(1)}, f32[8]{0:T(128)}, u32[]{:S(2)}) copy-start(f32[8]{0:T(128)} %param.42) | copy-start | bytes 100
  130.5 16.0 %all-to-all-start.4 = ((f32[16,9,128]{2,1,0:T(8,128)}), f32[16,9,128]{2,1,0:T(8,128)S(1)}, u32[]{:S(2)}, u32[]{:S(2)}) async-start(f32[16,9,128]{2,1,0:T(8,128)} %reshape.1346), calls=%async_computation.4 | async-start | bytes 262144 | tf_op jit(solution)/shard_map/all_to_all | solution.py:38
  181.7 7.7 %copy-start.18 = (s32[64]{0:T(128)S(1)}, s32[64]{0:T(128)}, u32[]{:S(2)}) copy-start(s32[64]{0:T(128)} %constant.453) | copy-start | bytes 772
  184.5 36.6 %all-to-all-start.8 = ((f32[4,2,4,16,10,128]{5,1,3,2,4,0:T(2,128)}), f32[4,2,4,16,10,128]{5,1,3,2,4,0:T(2,128)}, u32[]{:S(2)}, u32[]{:S(2)}) async-start(f32[4,2,4,16,10,128]{5,1,3,2,4,0:T(2,128)} %broadcast_in_dim.14), calls=%async_computation.8 | async-start | bytes 5242880 | tf_op jit(solution)/shard_map/all_to_all | solution.py:45
  233.5 5.4 copy-start.10
  243.3 2.4 copy-start
  243.3 2.4 copy-start.5
  248.9 1.7 copy-start.12
  368.5 61.8 %copy-start.9 = (f32[128,128]{1,0:T(8,128)}, f32[128,128]{1,0:T(8,128)S(1)}, u32[]{:S(2)}) copy-start(f32[128,128]{1,0:T(8,128)S(1)} %fusion.41) | copy-start | bytes 196612 | tf_op jit(solution)/shard_map/cond
  375.0 1.7 copy-start.1
  400.2 32.1 %copy-start.7 = (f32[128,128]{1,0:T(8,128)}, f32[128,128]{1,0:T(8,128)S(1)}, u32[]{:S(2)}) copy-start(f32[128,128]{1,0:T(8,128)S(1)} %fusion.39) | copy-start | bytes 196612 | tf_op jit(solution)/shard_map/cond
  405.4 1.4 copy-start.2
  430.3 31.3 %copy-start.8 = (f32[128,128]{1,0:T(8,128)}, f32[128,128]{1,0:T(8,128)S(1)}, u32[]{:S(2)}) copy-start(f32[128,128]{1,0:T(8,128)S(1)} %fusion.37) | copy-start | bytes 196612 | tf_op jit(solution)/shard_map/cond
  430.5 0.6 copy-start.17
  432.4 19.1 %copy-start.16 = (f32[1,128]{1,0:T(1,128)}, f32[1,128]{1,0:T(1,128)S(1)}, u32[]{:S(2)}) copy-start(f32[1,128]{1,0:T(1,128)S(1)} %fusion.81) | copy-start | bytes 1540 | tf_op jit(solution)/shard_map/cond
  437.2 1.2 copy-start.3
  465.8 1.0 copy-start.4
  490.2 1.3 copy-start.14
  517.0 1.2 copy-start.6
  517.2 0.6 copy-start.15
  518.2 0.7 copy-start.11

commit v5 on v4

--- a/solution.py
+++ b/solution.py
@@ -7,7 +7,7 @@
 
 WALKERS = 1024
 BLOCK = 128
-CG_STEPS = 12
+CG_STEPS = 10
 CG_TOL = 2e-5
 
 
@@ -129,7 +129,7 @@
 
 def make_on_device(sizes):
     grp, wx, wz, wc = sizes
-    levels = [("grp", grp), ("wc", wc), ("wx", wx), ("wz", wz)]
+    levels = [("wc", wc), ("grp", grp), ("wx", wx), ("wz", wz)]
     levels = [(a, n) for a, n in levels if n > 1]
     n_dev = grp * wx * wz * wc
 
@@ -156,11 +156,16 @@
         energy_row = energy_row.at[0, : energies.shape[0]].set(energies)
         chunk = jnp.concatenate([chunk, energy_row], axis=0)
         gathered = all_gather(chunk, levels[::-1])
-        gathered = gathered.reshape(grp, wc, wx, wz, per_dev + 1, BLOCK)
+        names = [a for a, n in levels]
+        gathered = gathered.reshape([n for a, n in levels] + [per_dev + 1, BLOCK])
         whole_packed = gathered[..., :per_dev, :].reshape(n_blocks, BLOCK, BLOCK)
         per_walk = energies.shape[0]
-        all_energy = gathered[0, :, :, :, per_dev, :per_walk]
-        all_energy = jnp.transpose(all_energy, (1, 2, 0, 3)).reshape(WALKERS)
+        energy = gathered[..., per_dev, :per_walk]
+        if "grp" in names:
+            energy = jnp.take(energy, 0, axis=names.index("grp"))
+            names.remove("grp")
+        order = [names.index(a) for a in WALK_PARTS if a in names]
+        all_energy = jnp.transpose(energy, order + [len(names)]).reshape(WALKERS)
 
         whole_gram = unpack_upper(whole_packed, nb)
         scaled_energy = (all_energy - jnp.mean(all_energy)) / root_walkers

time: 589 us -> 571 us (0.969)
  local copies, waits for them, and re-layouts: 40.2 us -> 67.6 us
  waiting for transfers between devices: 42.5 us -> 21.8 us
  blocking collectives: 158 us -> 149 us
  other arithmetic: 251 us -> 243 us
    cond x48 -> x46, local copies, waits for them, and re-layouts: 6.88 us -> 32.3 us
    all_to_all x1, waiting for transfers between devices: 31.7 us -> 11.1 us  [all_gather(): x = lax.all_to_all(copies, axis, 0, 0, tiled=True)]
    all_to_all x3, blocking collectives: 49 us -> 36.9 us  [reduce_scatter(): x = lax.all_to_all(parts, axis, 0, 0, tiled=True).sum(0)]
    reduce_sum x13 -> x11, other arithmetic: 34.9 us -> 29.6 us  [sym_matvec(): return jnp.sum(system * v[:, None], axis=0)]
where the time goes in v5:
time: 571 us; the launch traced here: 563 us
  other arithmetic  243 us (43%)
  blocking collectives  149 us (26%)
  local copies, waits for them, and re-layouts  67.6 us (12%)
  matrix products  45.1 us (8%)
  between operations  27.6 us (5%)
  waiting for transfers between devices  21.8 us (4%)
  starting transfers between devices  7.05 us (1%)
    another operation x24, other arithmetic, cholesky_solve(): factor = lax.linalg.cholesky(system[lo:up, lo:up], symmetrize_input=False)  99.8 us
    another operation x16, other arithmetic, cholesky_solve(): lax.linalg.triangular_solve(factor, eye, left_side=True, lower=True)  84.2 us
    all_to_all x1, blocking collectives, on_device(): lax.all_to_all(log_grads, walk_axes, split_axis=1, concat_axis=0, tiled=T...  74.7 us
    all_to_all x3, blocking collectives, all_gather(): x = lax.all_to_all(copies, axis, 0, 0, tiled=True)  37.6 us
    all_to_all x3, blocking collectives, reduce_scatter(): x = lax.all_to_all(parts, axis, 0, 0, tiled=True).sum(0)  36.9 us
    cond x46, local copies, waits for them, and re-layouts  32.3 us
    reduce_sum x11, other arithmetic, sym_matvec(): return jnp.sum(system * v[:, None], axis=0)  29.6 us
    dot_general x7, matrix products, cholesky_solve(): trailing = system[up:, up:] - jnp.dot(panel, panel.T, precision=hi)  16.8 us
  transfers between devices with their start and end apart: 2, of which 2 were waited for; matrix products, arithmetic and copies ran while one was open for 0% of the time, Pallas kernels for 0%

profile of v5, /device:TPU:1, one launch (start us, length us, event | category | flops | bytes accessed | tf_op | source)
XLA Modules:
  0.0 562.6 jit_solution(16209296606089707533)
XLA Ops:
  0.0 74.7 %all_to_all.59 = f32[8,128,256]{2,0,1:T(8,128)S(1)} all-to-all(f32[8,128,256]{2,0,1:T(8,128)} %bitcast.602), channel_id=1, replica_groups=mesh['grp'=4,'wx'=4,'wz'=16,'wc'=2] {'wx','wz','wc'}, dimensions={1} | all-to-all | bytes 2097152 | tf_op jit(solution)/shard_map/all_to_all | solution.py:138
  75.5 3.8 fusion.134
  79.8 7.4 %all_to_all.60 = f32[2,2304,128]{2,1,0:T(8,128)S(1)} all-to-all(f32[2,2304,128]{2,1,0:T(8,128)S(1)} %bitcast.585), channel_id=1, replica_groups=mesh['grp'=4,'wx'=4,'wz'=16,'wc'=2] {'wc'}, dimensions={0} | all-to-all | bytes 4718592 | tf_op jit(solution)/shard_map/all_to_all | solution.py:38
  88.5 19.8 %all_to_all.61 = f32[4,576,128]{2,1,0:T(8,128)S(1)} all-to-all(f32[4,576,128]{2,1,0:T(8,128)} %bitcast.584), channel_id=1, replica_groups=mesh['grp'=4,'wx'=4,'wz'=16,'wc'=2] {'grp'}, dimensions={0} | all-to-all | bytes 2359296 | tf_op jit(solution)/shard_map/all_to_all | solution.py:38
  108.4 9.6 %all_to_all.62 = f32[4,144,128]{2,1,0:T(8,128)S(1)} all-to-all(f32[4,144,128]{2,1,0:T(8,128)S(1)} %bitcast.586), channel_id=1, replica_groups=mesh['grp'=4,'wx'=4,'wz'=16,'wc'=2] {'wx'}, dimensions={0} | all-to-all | bytes 589824 | tf_op jit(solution)/shard_map/all_to_all | solution.py:38
  118.7 3.5 all-to-all-start.4
  123.4 10.7 %all-to-all-done.4 = f32[16,9,128]{2,1,0:T(8,128)S(1)} async-done(((f32[16,9,128]{2,1,0:T(8,128)}), f32[16,9,128]{2,1,0:T(8,128)S(1)}, u32[]{:S(2)}, u32[]{:S(2)}) %all-to-all-start.4) | async-done | bytes 73760 | tf_op jit(solution)/shard_map/all_to_all | solution.py:38
  134.2 15.8 %all_to_all.63 = f32[16,10,128]{2,1,0:T(8,128)S(1)} all-to-all(f32[16,10,128]{2,1,0:T(8,128)S(1)} %broadcast_in_dim.14), channel_id=1, replica_groups=mesh['grp'=4,'wx'=4,'wz'=16,'wc'=2] {'wz'}, dimensions={0} | all-to-all | bytes 163840 | tf_op jit(solution)/shard_map/all_to_all | solution.py:45
  150.1 8.3 %all_to_all.64 = f32[4,16,10,128]{3,1,2,0:T(8,128)S(1)} all-to-all(f32[4,16,10,128]{3,1,2,0:T(8,128)S(1)} %broadcast_in_dim.15), channel_id=1, replica_groups=mesh['grp'=4,'wx'=4,'wz'=16,'wc'=2] {'wx'}, dimensions={0} | all-to-all | bytes 655360 | tf_op jit(solution)/shard_map/all_to_all | solution.py:45
  159.6 3.5 all-to-all-start.7
  163.1 11.1 %all-to-all-done.7 = f32[4,4,16,10,128]{4,2,1,3,0:T(8,128)S(1)} async-done(((f32[4,4,16,10,128]{4,2,1,3,0:T(8,128)}), f32[4,4,16,10,128]{4,2,1,3,0:T(8,128)S(1)}, u32[]{:S(2)}, u32[]{:S(2)}) %all-to-all-start.7) | async-done | bytes 1310752 | tf_op jit(solution)/shard_map/all_to_all | solution.py:45
  174.5 13.5 %all_to_all.65 = f32[2,4,4,16,10,128]{5,3,2,4,1,0:T(8,128)S(1)} all-to-all(f32[2,4,4,16,10,128]{5,3,2,4,1,0:T(8,128)S(1)} %broadcast_in_dim.17), channel_id=1, replica_groups=mesh['grp'=4,'wx'=4,'wz'=16,'wc'=2] {'wc'}, dimensions={0} | all-to-all | bytes 5242880 | tf_op jit(solution)/shard_map/all_to_all | solution.py:45
  192.1 3.4 copy.22
  195.5 3.0 reshape.1133
  198.6 2.7 gather_fusion
  201.3 5.5 copy.23
  206.8 4.4 fusion.96
  213.6 3.1 bitcast_add_fusion
  217.7 2.7 multiply_reduce_fusion.10
  224.8 2.7 multiply_reduce_fusion.9
  231.9 2.7 multiply_reduce_fusion.8
  238.7 2.7 multiply_reduce_fusion.7
  245.3 2.7 multiply_reduce_fusion.6
  252.1 3.1 multiply_reduce_fusion.5
  259.3 2.7 multiply_reduce_fusion.4
  266.1 2.7 multiply_reduce_fusion.3
  272.8 2.7 multiply_reduce_fusion.2
  279.5 2.7 multiply_reduce_fusion.1
  294.6 265.7 %conditional.1 = (f32[1024]{0:T(1024)}) conditional(s32[]{:T(128)} %convert_element_type.21, (f32[1024,1024]{1,0:T(8,128)}, f32[1024]{0:T(1024)S(1)}) %tuple.85, (f32[1024]{0:T(1024)}, f32[1024]{0:T(1024)}, f32[]{:T(128)}, f32[1024]{0:T(1024)}, f32[1024]{0:T(1024)}, /*index=5*/f32[1024]{0:T(1024)}, f32[1024]{0:T(1024)}, ...), branch_computations={%region_19.0_spmd, %region_22.25_spmd.clone.clone} | conditional | flops 4446824960 | bytes 69703536 | solution.py:176
  295.6 11.7 %custom-call.20 = f32[128,128]{1,0:T(8,128)S(1)} custom-call(f32[128,128]{1,0:T(8,128)S(1)} %slice.428), custom_call_target="Cholesky" | custom-call | tf_op jit(solution)/shard_map/cond/branch_0_fun/cholesky/custom-call.1 | solution.py:78
  308.6 9.8 %custom-call.21 = f32[1,128,128]{1,2,0:T(8,128)S(1)} custom-call(f32[1,128,128]{2,1,0:T(8,128)S(1)} %fusion.47), custom_call_target="InvertDiagBlocksLowerTriangular" | custom-call | tf_op jit(solution)/shard_map/cond/branch_0_fun/triangular_solve/custom-call.0 | solution.py:79
  320.5 4.8 slice_subtract_fusion
  327.1 11.9 %custom-call.22 = f32[128,128]{1,0:T(8,128)S(1)} custom-call(f32[128,128]{1,0:T(8,128)S(1)} %slice.556), custom_call_target="Cholesky" | custom-call | tf_op jit(solution)/shard_map/cond/branch_0_fun/cholesky/custom-call.1 | solution.py:78
  340.2 9.8 %custom-call.23 = f32[1,128,128]{1,2,0:T(8,128)S(1)} custom-call(f32[1,128,128]{2,1,0:T(8,128)S(1)} %fusion.48), custom_call_target="InvertDiagBlocksLowerTriangular" | custom-call | tf_op jit(solution)/shard_map/cond/branch_0_fun/triangular_solve/custom-call.0 | solution.py:79
  352.0 3.7 slice_subtract_fusion.1
  357.2 11.7 %custom-call.24 = f32[128,128]{1,0:T(8,128)S(1)} custom-call(f32[128,128]{1,0:T(8,128)S(1)} %slice.559), custom_call_target="Cholesky" | custom-call | tf_op jit(solution)/shard_map/cond/branch_0_fun/cholesky/custom-call.1 | solution.py:78
  370.3 10.2 %custom-call.25 = f32[1,128,128]{1,2,0:T(8,128)S(1)} custom-call(f32[1,128,128]{2,1,0:T(8,128)S(1)} %fusion.49), custom_call_target="InvertDiagBlocksLowerTriangular" | custom-call | tf_op jit(solution)/shard_map/cond/branch_0_fun/triangular_solve/custom-call.0 | solution.py:79
  382.4 2.9 slice_subtract_fusion.2
  386.5 11.7 %custom-call.26 = f32[128,128]{1,0:T(8,128)S(1)} custom-call(f32[128,128]{1,0:T(8,128)S(1)} %slice.562), custom_call_target="Cholesky" | custom-call | tf_op jit(solution)/shard_map/cond/branch_0_fun/cholesky/custom-call.1 | solution.py:78
  399.6 9.8 %custom-call.27 = f32[1,128,128]{1,2,0:T(8,128)S(1)} custom-call(f32[1,128,128]{2,1,0:T(8,128)S(1)} %fusion.50), custom_call_target="InvertDiagBlocksLowerTriangular" | custom-call | tf_op jit(solution)/shard_map/cond/branch_0_fun/triangular_solve/custom-call.0 | solution.py:79
  414.5 11.9 %custom-call.28 = f32[128,128]{1,0:T(8,128)S(1)} custom-call(f32[128,128]{1,0:T(8,128)S(1)} %slice.565), custom_call_target="Cholesky" | custom-call | tf_op jit(solution)/shard_map/cond/branch_0_fun/cholesky/custom-call.1 | solution.py:78
  427.7 9.8 %custom-call.29 = f32[1,128,128]{1,2,0:T(8,128)S(1)} custom-call(f32[1,128,128]{2,1,0:T(8,128)S(1)} %fusion.51), custom_call_target="InvertDiagBlocksLowerTriangular" | custom-call | tf_op jit(solution)/shard_map/cond/branch_0_fun/triangular_solve/custom-call.0 | solution.py:79
  441.4 11.7 %custom-call.30 = f32[128,128]{1,0:T(8,128)S(1)} custom-call(f32[128,128]{1,0:T(8,128)S(1)} %slice.568), custom_call_target="Cholesky" | custom-call | tf_op jit(solution)/shard_map/cond/branch_0_fun/cholesky/custom-call.1 | solution.py:78
  454.5 10.0 %custom-call.31 = f32[1,128,128]{1,2,0:T(8,128)S(1)} custom-call(f32[1,128,128]{2,1,0:T(8,128)S(1)} %fusion.52), custom_call_target="InvertDiagBlocksLowerTriangular" | custom-call | tf_op jit(solution)/shard_map/cond/branch_0_fun/triangular_solve/custom-call.0 | solution.py:79
  466.5 11.7 %custom-call.32 = f32[128,128]{1,0:T(8,128)S(1)} custom-call(f32[128,128]{1,0:T(8,128)S(1)} %slice.571), custom_call_target="Cholesky" | custom-call | tf_op jit(solution)/shard_map/cond/branch_0_fun/cholesky/custom-call.1 | solution.py:78
  479.5 9.8 %custom-call.33 = f32[1,128,128]{1,2,0:T(8,128)S(1)} custom-call(f32[1,128,128]{2,1,0:T(8,128)S(1)} %fusion.53), custom_call_target="InvertDiagBlocksLowerTriangular" | custom-call | tf_op jit(solution)/shard_map/cond/branch_0_fun/triangular_solve/custom-call.0 | solution.py:79
  492.3 11.8 %custom-call.34 = f32[128,128]{1,0:T(8,128)S(1)} custom-call(f32[128,128]{1,0:T(8,128)S(1)} %convolution_subtract_fusion.3), custom_call_target="Cholesky" | custom-call | tf_op jit(solution)/shard_map/cond/branch_0_fun/cholesky/custom-call.1 | solution.py:78
  505.4 10.0 %custom-call.35 = f32[1,128,128]{1,2,0:T(8,128)S(1)} custom-call(f32[1,128,128]{2,1,0:T(8,128)S(1)} %fusion.54), custom_call_target="InvertDiagBlocksLowerTriangular" | custom-call | tf_op jit(solution)/shard_map/cond/branch_0_fun/triangular_solve/custom-call.0 | solution.py:79
  (314 shorter events, 118.4 us)
Async XLA Ops:
  74.9 0.6 copy-start.16
  87.2 35.6 %copy-start.21 = (f32[8]{0:T(128)S(1)}, f32[8]{0:T(128)}, u32[]{:S(2)}) copy-start(f32[8]{0:T(128)} %param.42) | copy-start | bytes 100
  108.4 54.7 %copy-start.20 = (s32[64]{0:T(128)S(1)}, s32[64]{0:T(128)}, u32[]{:S(2)}) copy-start(s32[64]{0:T(128)} %constant.491) | copy-start | bytes 772
  118.7 15.4 %all-to-all-start.4 = ((f32[16,9,128]{2,1,0:T(8,128)}), f32[16,9,128]{2,1,0:T(8,128)S(1)}, u32[]{:S(2)}, u32[]{:S(2)}) async-start(f32[16,9,128]{2,1,0:T(8,128)} %reshape.1131), calls=%async_computation.4 | async-start | bytes 262144 | tf_op jit(solution)/shard_map/all_to_all | solution.py:38
  159.6 14.7 %all-to-all-start.7 = ((f32[4,4,16,10,128]{4,2,1,3,0:T(8,128)}), f32[4,4,16,10,128]{4,2,1,3,0:T(8,128)S(1)}, u32[]{:S(2)}, u32[]{:S(2)}) async-start(f32[4,4,16,10,128]{4,2,1,3,0:T(8,128)} %broadcast_in_dim.16), calls=%async_computation.7 | async-start | bytes 2621440 | tf_op jit(solution)/shard_map/all_to_all | solution.py:45
  188.0 1.5 copy-start.2
  190.2 1.9 slice-start
  192.1 32.5 %copy-start.13 = (f32[8,128]{1,0:T(8,128)}, f32[8,128]{1,0:T(8,128)S(1)}, u32[]{:S(2)}) copy-start(f32[8,128]{1,0:T(8,128)S(1)} %div.171) | copy-start | bytes 12292
  201.3 5.5 copy-start.11
  211.1 2.4 copy-start
  211.2 2.4 copy-start.6
  216.7 10.7 %copy-start.15 = (f32[1024]{0:T(1024)}, f32[1024]{0:T(1024)S(1)}, u32[]{:S(2)}) copy-start(f32[1024]{0:T(1024)S(1)} %broadcast_divide_fusion) | copy-start | bytes 12292
  272.8 12.1 %copy-start.14 = (f32[8,128]{1,0:T(8,128)S(1)}, f32[8,128]{1,0:T(8,128)}, u32[]{:S(2)}) copy-start(f32[8,128]{1,0:T(8,128)} %copy-done.13) | copy-start | bytes 12292
  318.7 6.7 %copy-start.10 = (f32[128,128]{1,0:T(8,128)}, f32[128,128]{1,0:T(8,128)S(1)}, u32[]{:S(2)}) copy-start(f32[128,128]{1,0:T(8,128)S(1)} %fusion.41) | copy-start | bytes 196612 | tf_op jit(solution)/shard_map/cond
  318.9 6.5 %copy-start.19 = (f32[1,128]{1,0:T(1,128)}, f32[1,128]{1,0:T(1,128)S(1)}, u32[]{:S(2)}) copy-start(f32[1,128]{1,0:T(1,128)S(1)} %fusion.87) | copy-start | bytes 1540 | tf_op jit(solution)/shard_map/cond
  325.4 1.7 copy-start.1
  350.3 30.4 %copy-start.8 = (f32[128,128]{1,0:T(8,128)}, f32[128,128]{1,0:T(8,128)S(1)}, u32[]{:S(2)}) copy-start(f32[128,128]{1,0:T(8,128)S(1)} %fusion.39) | copy-start | bytes 196612 | tf_op jit(solution)/shard_map/cond
  355.7 1.4 copy-start.3
  380.8 28.9 %copy-start.9 = (f32[128,128]{1,0:T(8,128)}, f32[128,128]{1,0:T(8,128)S(1)}, u32[]{:S(2)}) copy-start(f32[128,128]{1,0:T(8,128)S(1)} %fusion.37) | copy-start | bytes 196612 | tf_op jit(solution)/shard_map/cond
  380.9 18.6 %copy-start.18 = (f32[1,128]{1,0:T(1,128)}, f32[1,128]{1,0:T(1,128)S(1)}, u32[]{:S(2)}) copy-start(f32[1,128]{1,0:T(1,128)S(1)} %fusion.81) | copy-start | bytes 1540 | tf_op jit(solution)/shard_map/cond
  385.3 1.2 copy-start.4
  413.5 1.0 copy-start.5
  464.8 0.9 copy-start.7
  465.0 1.0 copy-start.17
  465.7 0.7 copy-start.12

commit v6 on v5

--- a/solution.py
+++ b/solution.py
@@ -44,6 +44,20 @@
         copies = jnp.broadcast_to(x[None], (size,) + x.shape)
         x = lax.all_to_all(copies, axis, 0, 0, tiled=True)
     return x
+
+
+def regroup(log_grads, sizes):
+    wx, wz, wc = sizes
+    rows, cols = log_grads.shape
+    width = cols // (wx * wz * wc)
+    y = log_grads.reshape(rows, wx, wz, wc, width)
+    y = jnp.transpose(y, (3, 0, 1, 2, 4))
+    y = lax.all_to_all(y, "wc", 0, 0, tiled=True)
+    y = jnp.transpose(y, (3, 0, 1, 2, 4))
+    y = lax.all_to_all(y, "wz", 0, 0, tiled=True)
+    y = jnp.transpose(y, (3, 0, 1, 2, 4))
+    y = lax.all_to_all(y, "wx", 0, 0, tiled=True)
+    return y.reshape(wx * wz * wc * rows, width)
 
 
 def upper_pairs(nb):
@@ -134,10 +148,7 @@
     n_dev = grp * wx * wz * wc
 
     def on_device(log_grads, energies):
-        walk_axes = WALK_PARTS
-        regrouped = lax.all_to_all(
-            log_grads, walk_axes, split_axis=1, concat_axis=0, tiled=True
-        )
+        regrouped = regroup(log_grads, (wx, wz, wc))
         walk = wx * wz * wc
         group_params = regrouped.shape[1] * walk
         total_params = group_params * grp

time: 571 us -> 581 us (1.018)
  blocking collectives: 149 us -> 159 us
  matrix products: 45.1 us -> 36.1 us
  starting transfers between devices: 7.05 us -> 13.9 us
    all_to_all x1, starting transfers between devices: 3.51 us -> 10.4 us  [reduce_scatter(): x = lax.all_to_all(parts, axis, 0, 0, tiled=True).sum(0)]
    all_to_all x1 -> x3, blocking collectives: 74.7 us -> 79.2 us  [the longest x1 54.5 us: regroup(): y = lax.all_to_all(y, 'wz', 0, 0, tiled=True)]
    cond x46 -> x40, local copies, waits for them, and re-layouts: 32.3 us -> 31.5 us
where the time goes in v6:
time: 581 us; the launch traced here: 572 us
  other arithmetic  244 us (42%)
  blocking collectives  159 us (27%)
  local copies, waits for them, and re-layouts  67.8 us (12%)
  matrix products  36.1 us (6%)
  between operations  29.5 us (5%)
  waiting for transfers between devices  20.6 us (4%)
  starting transfers between devices  13.9 us (2%)
    another operation x24, other arithmetic, cholesky_solve(): factor = lax.linalg.cholesky(system[lo:up, lo:up], symmetrize_input=False)  99.7 us
    another operation x16, other arithmetic, cholesky_solve(): lax.linalg.triangular_solve(factor, eye, left_side=True, lower=True)  84.4 us
    all_to_all x1, blocking collectives, regroup(): y = lax.all_to_all(y, 'wz', 0, 0, tiled=True)  54.5 us
    all_to_all x3, blocking collectives, reduce_scatter(): x = lax.all_to_all(parts, axis, 0, 0, tiled=True).sum(0)  41.9 us
    all_to_all x3, blocking collectives, all_gather(): x = lax.all_to_all(copies, axis, 0, 0, tiled=True)  37.6 us
    cond x40, local copies, waits for them, and re-layouts  31.5 us
    reduce_sum x11, other arithmetic, sym_matvec(): return jnp.sum(system * v[:, None], axis=0)  29.6 us
    all_to_all x1, blocking collectives, regroup(): y = lax.all_to_all(y, 'wx', 0, 0, tiled=True)  13.6 us
  transfers between devices with their start and end apart: 2, of which 2 were waited for; matrix products, arithmetic and copies ran while one was open for 0% of the time, Pallas kernels for 0%

profile of v6, /device:TPU:1, one launch (start us, length us, event | category | flops | bytes accessed | tf_op | source)
XLA Modules:
  0.0 571.7 jit_solution(4168590558657162451)
XLA Ops:
  2.7 11.1 %all_to_all.55 = f32[2,8,4,16,256]{4,1,3,2,0:T(8,128)S(1)} all-to-all(f32[2,8,4,16,256]{4,1,3,2,0:T(8,128)S(1)} %copy.29), channel_id=1, replica_groups=mesh['grp'=4,'wx'=4,'wz'=16,'wc'=2] {'wc'}, dimensions={0} | all-to-all | bytes 2097152 | tf_op jit(solution)/shard_map/all_to_all | solution.py:55
  14.0 54.5 %all_to_all.56 = f32[16,2,8,4,256]{4,2,1,3,0:T(8,128)S(1)} all-to-all(f32[16,2,8,4,256]{4,2,1,3,0:T(8,128)S(1)} %copy.30), channel_id=1, replica_groups=mesh['grp'=4,'wx'=4,'wz'=16,'wc'=2] {'wz'}, dimensions={0} | all-to-all | bytes 2097152 | tf_op jit(solution)/shard_map/all_to_all | solution.py:57
  68.6 13.6 %all_to_all.57 = f32[4,16,2,8,256]{4,3,2,1,0:T(8,128)S(1)} all-to-all(f32[4,16,2,8,256]{4,3,2,1,0:T(8,128)S(1)} %bitcast.585), channel_id=1, replica_groups=mesh['grp'=4,'wx'=4,'wz'=16,'wc'=2] {'wx'}, dimensions={0} | all-to-all | bytes 2097152 | tf_op jit(solution)/shard_map/all_to_all | solution.py:59
  82.4 3.8 fusion.128
  86.8 14.0 %all_to_all.58 = f32[2,2304,128]{2,1,0:T(8,128)S(1)} all-to-all(f32[2,2304,128]{2,1,0:T(8,128)S(1)} %bitcast.587), channel_id=1, replica_groups=mesh['grp'=4,'wx'=4,'wz'=16,'wc'=2] {'wc'}, dimensions={0} | all-to-all | bytes 4718592 | tf_op jit(solution)/shard_map/all_to_all | solution.py:38
  102.0 19.8 %all_to_all.59 = f32[4,576,128]{2,1,0:T(8,128)S(1)} all-to-all(f32[4,576,128]{2,1,0:T(8,128)} %bitcast.583), channel_id=1, replica_groups=mesh['grp'=4,'wx'=4,'wz'=16,'wc'=2] {'grp'}, dimensions={0} | all-to-all | bytes 2359296 | tf_op jit(solution)/shard_map/all_to_all | solution.py:38
  122.0 8.1 %all_to_all.60 = f32[4,144,128]{2,1,0:T(8,128)S(1)} all-to-all(f32[4,144,128]{2,1,0:T(8,128)S(1)} %bitcast.588), channel_id=1, replica_groups=mesh['grp'=4,'wx'=4,'wz'=16,'wc'=2] {'wx'}, dimensions={0} | all-to-all | bytes 589824 | tf_op jit(solution)/shard_map/all_to_all | solution.py:38
  130.7 10.4 %all-to-all-start.6 = ((f32[16,9,128]{2,1,0:T(8,128)}), f32[16,9,128]{2,1,0:T(8,128)S(1)}, u32[]{:S(2)}, u32[]{:S(2)}) async-start(f32[16,9,128]{2,1,0:T(8,128)} %reshape.1135), calls=%async_computation.6 | async-start | bytes 262144 | tf_op jit(solution)/shard_map/all_to_all | solution.py:38
  142.4 10.7 %all-to-all-done.6 = f32[16,9,128]{2,1,0:T(8,128)S(1)} async-done(((f32[16,9,128]{2,1,0:T(8,128)}), f32[16,9,128]{2,1,0:T(8,128)S(1)}, u32[]{:S(2)}, u32[]{:S(2)}) %all-to-all-start.6) | async-done | bytes 73760 | tf_op jit(solution)/shard_map/all_to_all | solution.py:38
  153.1 15.8 %all_to_all.61 = f32[16,10,128]{2,1,0:T(8,128)S(1)} all-to-all(f32[16,10,128]{2,1,0:T(8,128)S(1)} %broadcast_in_dim.14), channel_id=1, replica_groups=mesh['grp'=4,'wx'=4,'wz'=16,'wc'=2] {'wz'}, dimensions={0} | all-to-all | bytes 163840 | tf_op jit(solution)/shard_map/all_to_all | solution.py:45
  169.0 8.3 %all_to_all.62 = f32[4,16,10,128]{3,1,2,0:T(8,128)S(1)} all-to-all(f32[4,16,10,128]{3,1,2,0:T(8,128)S(1)} %broadcast_in_dim.15), channel_id=1, replica_groups=mesh['grp'=4,'wx'=4,'wz'=16,'wc'=2] {'wx'}, dimensions={0} | all-to-all | bytes 655360 | tf_op jit(solution)/shard_map/all_to_all | solution.py:45
  178.5 3.5 all-to-all-start.9
  183.2 9.9 %all-to-all-done.9 = f32[4,4,16,10,128]{4,2,1,3,0:T(8,128)S(1)} async-done(((f32[4,4,16,10,128]{4,2,1,3,0:T(8,128)}), f32[4,4,16,10,128]{4,2,1,3,0:T(8,128)S(1)}, u32[]{:S(2)}, u32[]{:S(2)}) %all-to-all-start.9) | async-done | bytes 1310752 | tf_op jit(solution)/shard_map/all_to_all | solution.py:45
  193.5 13.5 %all_to_all.63 = f32[2,4,4,16,10,128]{5,3,2,4,1,0:T(8,128)S(1)} all-to-all(f32[2,4,4,16,10,128]{5,3,2,4,1,0:T(8,128)S(1)} %broadcast_in_dim.17), channel_id=1, replica_groups=mesh['grp'=4,'wx'=4,'wz'=16,'wc'=2] {'wc'}, dimensions={0} | all-to-all | bytes 5242880 | tf_op jit(solution)/shard_map/all_to_all | solution.py:45
  208.8 3.4 copy.35
  212.2 3.0 reshape.1137
  215.2 2.7 gather_fusion
  217.9 5.4 copy.36
  223.3 4.4 fusion.96
  230.2 3.1 bitcast_add_fusion
  234.2 2.7 multiply_reduce_fusion.10
  241.3 2.6 multiply_reduce_fusion.9
  248.6 2.7 multiply_reduce_fusion.8
  255.7 2.7 multiply_reduce_fusion.7
  269.9 3.1 multiply_reduce_fusion.5
  277.2 2.7 multiply_reduce_fusion.4
  284.1 2.7 multiply_reduce_fusion.3
  291.1 2.7 multiply_reduce_fusion.2
  298.3 2.7 multiply_reduce_fusion.1
  313.6 255.3 %conditional.1 = (f32[1024]{0:T(1024)}) conditional(s32[]{:T(128)} %convert_element_type.21, (f32[1024,1024]{1,0:T(8,128)}, f32[1024]{0:T(1024)S(1)}) %tuple.85, (f32[1024]{0:T(1024)}, f32[1024]{0:T(1024)}, f32[]{:T(128)}, f32[1024]{0:T(1024)}, f32[1024]{0:T(1024)}, /*index=5*/f32[1024]{0:T(1024)}, f32[1024]{0:T(1024)}, ...), branch_computations={%region_19.0_spmd, %region_22.25_spmd.clone.clone} | conditional | flops 4446824960 | bytes 55283464 | solution.py:187
  314.6 11.7 %custom-call.20 = f32[128,128]{1,0:T(8,128)S(1)} custom-call(f32[128,128]{1,0:T(8,128)S(1)} %slice.428), custom_call_target="Cholesky" | custom-call | tf_op jit(solution)/shard_map/cond/branch_0_fun/cholesky/custom-call.1 | solution.py:92
  327.6 9.8 %custom-call.21 = f32[1,128,128]{1,2,0:T(8,128)S(1)} custom-call(f32[1,128,128]{2,1,0:T(8,128)S(1)} %fusion.47), custom_call_target="InvertDiagBlocksLowerTriangular" | custom-call | tf_op jit(solution)/shard_map/cond/branch_0_fun/triangular_solve/custom-call.0 | solution.py:93
  340.0 4.8 slice_subtract_fusion
  346.5 11.9 %custom-call.22 = f32[128,128]{1,0:T(8,128)S(1)} custom-call(f32[128,128]{1,0:T(8,128)S(1)} %slice.556), custom_call_target="Cholesky" | custom-call | tf_op jit(solution)/shard_map/cond/branch_0_fun/cholesky/custom-call.1 | solution.py:92
  359.8 9.8 %custom-call.23 = f32[1,128,128]{1,2,0:T(8,128)S(1)} custom-call(f32[1,128,128]{2,1,0:T(8,128)S(1)} %fusion.48), custom_call_target="InvertDiagBlocksLowerTriangular" | custom-call | tf_op jit(solution)/shard_map/cond/branch_0_fun/triangular_solve/custom-call.0 | solution.py:93
  372.1 3.7 slice_subtract_fusion.1
  376.2 11.7 %custom-call.24 = f32[128,128]{1,0:T(8,128)S(1)} custom-call(f32[128,128]{1,0:T(8,128)S(1)} %slice.559), custom_call_target="Cholesky" | custom-call | tf_op jit(solution)/shard_map/cond/branch_0_fun/cholesky/custom-call.1 | solution.py:92
  389.1 10.2 %custom-call.25 = f32[1,128,128]{1,2,0:T(8,128)S(1)} custom-call(f32[1,128,128]{2,1,0:T(8,128)S(1)} %fusion.49), custom_call_target="InvertDiagBlocksLowerTriangular" | custom-call | tf_op jit(solution)/shard_map/cond/branch_0_fun/triangular_solve/custom-call.0 | solution.py:93
  403.4 11.7 %custom-call.26 = f32[128,128]{1,0:T(8,128)S(1)} custom-call(f32[128,128]{1,0:T(8,128)S(1)} %slice.562), custom_call_target="Cholesky" | custom-call | tf_op jit(solution)/shard_map/cond/branch_0_fun/cholesky/custom-call.1 | solution.py:92
  416.4 9.8 %custom-call.27 = f32[1,128,128]{1,2,0:T(8,128)S(1)} custom-call(f32[1,128,128]{2,1,0:T(8,128)S(1)} %fusion.50), custom_call_target="InvertDiagBlocksLowerTriangular" | custom-call | tf_op jit(solution)/shard_map/cond/branch_0_fun/triangular_solve/custom-call.0 | solution.py:93
  430.7 11.9 %custom-call.28 = f32[128,128]{1,0:T(8,128)S(1)} custom-call(f32[128,128]{1,0:T(8,128)S(1)} %slice.565), custom_call_target="Cholesky" | custom-call | tf_op jit(solution)/shard_map/cond/branch_0_fun/cholesky/custom-call.1 | solution.py:92
  443.9 9.8 %custom-call.29 = f32[1,128,128]{1,2,0:T(8,128)S(1)} custom-call(f32[1,128,128]{2,1,0:T(8,128)S(1)} %fusion.51), custom_call_target="InvertDiagBlocksLowerTriangular" | custom-call | tf_op jit(solution)/shard_map/cond/branch_0_fun/triangular_solve/custom-call.0 | solution.py:93
  455.6 11.7 %custom-call.30 = f32[128,128]{1,0:T(8,128)S(1)} custom-call(f32[128,128]{1,0:T(8,128)S(1)} %slice.568), custom_call_target="Cholesky" | custom-call | tf_op jit(solution)/shard_map/cond/branch_0_fun/cholesky/custom-call.1 | solution.py:92
  468.7 10.0 %custom-call.31 = f32[1,128,128]{1,2,0:T(8,128)S(1)} custom-call(f32[1,128,128]{2,1,0:T(8,128)S(1)} %fusion.52), custom_call_target="InvertDiagBlocksLowerTriangular" | custom-call | tf_op jit(solution)/shard_map/cond/branch_0_fun/triangular_solve/custom-call.0 | solution.py:93
  480.1 11.7 %custom-call.32 = f32[128,128]{1,0:T(8,128)S(1)} custom-call(f32[128,128]{1,0:T(8,128)S(1)} %slice.571), custom_call_target="Cholesky" | custom-call | tf_op jit(solution)/shard_map/cond/branch_0_fun/cholesky/custom-call.1 | solution.py:92
  493.2 9.8 %custom-call.33 = f32[1,128,128]{1,2,0:T(8,128)S(1)} custom-call(f32[1,128,128]{2,1,0:T(8,128)S(1)} %fusion.53), custom_call_target="InvertDiagBlocksLowerTriangular" | custom-call | tf_op jit(solution)/shard_map/cond/branch_0_fun/triangular_solve/custom-call.0 | solution.py:93
  504.3 11.8 %custom-call.34 = f32[128,128]{1,0:T(8,128)S(1)} custom-call(f32[128,128]{1,0:T(8,128)S(1)} %convolution_subtract_fusion.3), custom_call_target="Cholesky" | custom-call | tf_op jit(solution)/shard_map/cond/branch_0_fun/cholesky/custom-call.1 | solution.py:92
  517.4 10.0 %custom-call.35 = f32[1,128,128]{1,2,0:T(8,128)S(1)} custom-call(f32[1,128,128]{2,1,0:T(8,128)S(1)} %fusion.54), custom_call_target="InvertDiagBlocksLowerTriangular" | custom-call | tf_op jit(solution)/shard_map/cond/branch_0_fun/triangular_solve/custom-call.0 | solution.py:93
  (306 shorter events, 116.1 us)
Async XLA Ops:
  100.8 41.0 %copy-start.14 = (f32[8]{0:T(128)S(1)}, f32[8]{0:T(128)}, u32[]{:S(2)}) copy-start(f32[8]{0:T(128)} %param.42) | copy-start | bytes 100
  122.0 60.1 %copy-start.13 = (s32[64]{0:T(128)S(1)}, s32[64]{0:T(128)}, u32[]{:S(2)}) copy-start(s32[64]{0:T(128)} %constant.491) | copy-start | bytes 772
  130.7 22.4 %all-to-all-start.6 = ((f32[16,9,128]{2,1,0:T(8,128)}), f32[16,9,128]{2,1,0:T(8,128)S(1)}, u32[]{:S(2)}, u32[]{:S(2)}) async-start(f32[16,9,128]{2,1,0:T(8,128)} %reshape.1135), calls=%async_computation.6 | async-start | bytes 262144 | tf_op jit(solution)/shard_map/all_to_all | solution.py:38
  178.5 14.7 %all-to-all-start.9 = ((f32[4,4,16,10,128]{4,2,1,3,0:T(8,128)}), f32[4,4,16,10,128]{4,2,1,3,0:T(8,128)S(1)}, u32[]{:S(2)}, u32[]{:S(2)}) async-start(f32[4,4,16,10,128]{4,2,1,3,0:T(8,128)} %broadcast_in_dim.16), calls=%async_computation.9 | async-start | bytes 2621440 | tf_op jit(solution)/shard_map/all_to_all | solution.py:45
  217.9 5.4 copy-start.9
  227.7 2.4 copy-start
  227.7 2.4 copy-start.3
  233.3 10.7 %copy-start.10 = (f32[1024]{0:T(1024)}, f32[1024]{0:T(1024)S(1)}, u32[]{:S(2)}) copy-start(f32[1024]{0:T(1024)S(1)} %broadcast_divide_fusion) | copy-start | bytes 12292
  337.7 0.6 copy-start.8
  338.4 6.8 %copy-start.12 = (f32[1,128]{1,0:T(1,128)}, f32[1,128]{1,0:T(1,128)S(1)}, u32[]{:S(2)}) copy-start(f32[1,128]{1,0:T(1,128)S(1)} %fusion.87) | copy-start | bytes 1540 | tf_op jit(solution)/shard_map/cond
  344.8 1.7 copy-start.1
  370.0 0.6 copy-start.4
  399.6 0.6 copy-start.6
  400.3 2.3 copy-start.11
  402.1 1.2 copy-start.2
  430.3 107.3 %copy-start.7 = (f32[128,128]{1,0:T(8,128)S(1)}, f32[128,128]{1,0:T(8,128)}, u32[]{:S(2)}) copy-start(f32[128,128]{1,0:T(8,128)} %copy-done.6) | copy-start | bytes 196612 | tf_op jit(solution)/shard_map/cond
  430.3 116.1 %copy-start.5 = (f32[128,128]{1,0:T(8,128)S(1)}, f32[128,128]{1,0:T(8,128)}, u32[]{:S(2)}) copy-start(f32[128,128]{1,0:T(8,128)} %copy-done.4) | copy-start | bytes 196612 | tf_op jit(solution)/shard_map/cond

commit v7 on v5

--- a/solution.py
+++ b/solution.py
@@ -2,6 +2,8 @@
 import jax.numpy as jnp
 import numpy as np
 from jax import lax
+from jax.experimental import pallas as pl
+from jax.experimental.pallas import tpu as pltpu
 from jax.sharding import Mesh
 from jax.sharding import PartitionSpec as P
 
@@ -127,6 +129,69 @@
     return x, ok
 
 
+INTERPRET = False
+
+
+def cg_kernel(lam, steps, a_ref, b_ref, d_ref, x_ref, st_ref, pc_ref):
+    n = a_ref.shape[0]
+    chunk = BLOCK
+
+    def matvec(p_row):
+        pc_ref[...] = jnp.transpose(jnp.broadcast_to(p_row, (8, n)))
+        acc = jnp.zeros((1, n), jnp.float32)
+        for c in range(n // chunk):
+            blk = a_ref[c * chunk : (c + 1) * chunk, :]
+            col = pc_ref[c * chunk : (c + 1) * chunk, 0:1]
+            acc = acc + jnp.sum(blk * col, axis=0, keepdims=True)
+        return acc
+
+    b_row = b_ref[...]
+    d_row = d_ref[...]
+    z_row = b_row * d_row
+    rz = jnp.sum(b_row * z_row, axis=1, keepdims=True)
+
+    def body(_, carry):
+        x_row, r_row, p_row, rz = carry
+        ap_row = matvec(p_row)
+        alpha = rz / jnp.sum(p_row * ap_row, axis=1, keepdims=True)
+        x_row = x_row + alpha * p_row
+        r_row = r_row - alpha * ap_row
+        z_row = r_row * d_row
+        rz_next = jnp.sum(r_row * z_row, axis=1, keepdims=True)
+        p_row = z_row + (rz_next / rz) * p_row
+        return x_row, r_row, p_row, rz_next
+
+    x0 = jnp.zeros((1, n), jnp.float32)
+    x_row = lax.fori_loop(0, steps, body, (x0, b_row, z_row, rz))[0]
+    ax_row = matvec(x_row)
+    resid = b_row - ax_row
+    bound = jnp.sum(resid * resid, axis=1, keepdims=True)
+    energy = jnp.sum(x_row * ax_row, axis=1, keepdims=True) - lam * jnp.sum(
+        x_row * x_row, axis=1, keepdims=True
+    )
+    x_ref[...] = x_row
+    lane = lax.broadcasted_iota(jnp.int32, (1, 128), 1)
+    st_ref[...] = jnp.where(lane == 0, bound, jnp.where(lane == 1, energy, 0.0))
+
+
+def kernel_cg(system, rhs, lam, steps, tol):
+    n = system.shape[0]
+    eye = np.eye(n, dtype=bool)
+    inv_diag = 1.0 / jnp.sum(jnp.where(eye, system, 0.0), axis=0)
+    body = lambda *refs: cg_kernel(lam, steps, *refs)
+    x, st = pl.pallas_call(
+        body,
+        out_shape=(
+            jax.ShapeDtypeStruct((1, n), jnp.float32),
+            jax.ShapeDtypeStruct((1, 128), jnp.float32),
+        ),
+        scratch_shapes=[pltpu.VMEM((n, 8), jnp.float32)],
+        interpret=INTERPRET,
+    )(system, rhs[None, :], inv_diag[None, :])
+    ok = st[0, 0] <= (tol * tol) * lam * st[0, 1]
+    return x[0], ok
+
+
 def make_on_device(sizes):
     grp, wx, wz, wc = sizes
     levels = [("wc", wc), ("grp", grp), ("wx", wx), ("wz", wz)]
@@ -172,7 +237,7 @@
         identity_mat = jnp.eye(WALKERS, dtype=jnp.float32)
         lam = damping * total_params
         system = whole_gram + lam * identity_mat
-        guess, ok = certified_cg(system, scaled_energy, lam, CG_STEPS, CG_TOL)
+        guess, ok = kernel_cg(system, scaled_energy, lam, CG_STEPS, CG_TOL)
         solved = lax.cond(
             ok,
             lambda a, b, g: g,

time: 571 us -> 478 us (0.84)
  other arithmetic: 243 us -> 197 us
  local copies, waits for them, and re-layouts: 67.6 us -> 32.9 us
  between operations: 27.6 us -> 2.92 us
  Pallas kernels: 0 us -> 11.4 us
    reduce_sum x12 -> x1, other arithmetic: 30.2 us -> 3.12 us  [kernel_cg(): inv_diag = 1.0 / jnp.sum(jnp.where(eye, system, 0.0), axis=0)]
    cond x46 -> x53, local copies, waits for them, and re-layouts: 32.3 us -> 6.85 us
    dot_general x23 -> x0, other arithmetic: 15.6 us -> none  [the longest x9 6.35 us: certified_cg(): rz_next = jnp.dot(r, z, precision=hi)]
    pallas_call x0 -> x1, Pallas kernels: none -> 11.4 us  [kernel_cg(): pl.pallas_call(body, out_shape=(jax.ShapeDtypeStruct((1, n), jnp.float32)...]
    concatenate x7, local copies, waits for them, and re-layouts: 5.89 us -> 0.03 us  [cholesky_solve(): tail = solved[k] if tail is None else jnp.concatenate([solved[k], tail])]
where the time goes in v7:
time: 478 us; the launch traced here: 470 us
  other arithmetic  197 us (41%)
  blocking collectives  150 us (31%)
  matrix products  46.5 us (10%)
  local copies, waits for them, and re-layouts  32.9 us (7%)
  waiting for transfers between devices  21.7 us (5%)
  Pallas kernels  11.4 us (2%)
  starting transfers between devices  7.05 us (1%)
    another operation x24, other arithmetic, cholesky_solve(): factor = lax.linalg.cholesky(system[lo:up, lo:up], symmetrize_input=False)  99.7 us
    another operation x16, other arithmetic, cholesky_solve(): lax.linalg.triangular_solve(factor, eye, left_side=True, lower=True)  84.5 us
    all_to_all x1, blocking collectives, on_device(): lax.all_to_all(log_grads, walk_axes, split_axis=1, concat_axis=0, tiled=T...  74.7 us
    all_to_all x3, blocking collectives, all_gather(): x = lax.all_to_all(copies, axis, 0, 0, tiled=True)  37.9 us
    all_to_all x3, blocking collectives, reduce_scatter(): x = lax.all_to_all(parts, axis, 0, 0, tiled=True).sum(0)  37 us
    dot_general x7, matrix products, cholesky_solve(): trailing = system[up:, up:] - jnp.dot(panel, panel.T, precision=hi)  16.8 us
    pallas_call x1, Pallas kernels, kernel_cg(): pl.pallas_call(body, out_shape=(jax.ShapeDtypeStruct((1, n), jnp.float32)...  11.4 us
    all_to_all x1, waiting for transfers between devices, all_gather(): x = lax.all_to_all(copies, axis, 0, 0, tiled=True)  11.1 us
  transfers between devices with their start and end apart: 2, of which 2 were waited for; matrix products, arithmetic and copies ran while one was open for 0% of the time, Pallas kernels for 0%

profile of v7, /device:TPU:1, one launch (start us, length us, event | category | flops | bytes accessed | tf_op | source)
XLA Modules:
  0.0 469.9 jit_solution(17071287113153370932)
XLA Ops:
  0.0 74.7 %all_to_all.59 = f32[8,128,256]{2,0,1:T(8,128)S(1)} all-to-all(f32[8,128,256]{2,0,1:T(8,128)} %bitcast.458), channel_id=1, replica_groups=mesh['grp'=4,'wx'=4,'wz'=16,'wc'=2] {'wx','wz','wc'}, dimensions={1} | all-to-all | bytes 2097152 | tf_op jit(solution)/shard_map/all_to_all | solution.py:203
  75.0 3.8 fusion.108
  79.3 7.5 %all_to_all.60 = f32[2,2304,128]{2,1,0:T(8,128)S(1)} all-to-all(f32[2,2304,128]{2,1,0:T(8,128)S(1)} %bitcast.456), channel_id=1, replica_groups=mesh['grp'=4,'wx'=4,'wz'=16,'wc'=2] {'wc'}, dimensions={0} | all-to-all | bytes 4718592 | tf_op jit(solution)/shard_map/all_to_all | solution.py:40
  88.0 20.0 %all_to_all.61 = f32[4,576,128]{2,1,0:T(8,128)S(1)} all-to-all(f32[4,576,128]{2,1,0:T(8,128)} %bitcast.455), channel_id=1, replica_groups=mesh['grp'=4,'wx'=4,'wz'=16,'wc'=2] {'grp'}, dimensions={0} | all-to-all | bytes 2359296 | tf_op jit(solution)/shard_map/all_to_all | solution.py:40
  108.1 9.6 %all_to_all.62 = f32[4,144,128]{2,1,0:T(8,128)S(1)} all-to-all(f32[4,144,128]{2,1,0:T(8,128)S(1)} %bitcast.457), channel_id=1, replica_groups=mesh['grp'=4,'wx'=4,'wz'=16,'wc'=2] {'wx'}, dimensions={0} | all-to-all | bytes 589824 | tf_op jit(solution)/shard_map/all_to_all | solution.py:40
  118.3 3.5 all-to-all-start.4
  123.2 10.6 %all-to-all-done.4 = f32[16,9,128]{2,1,0:T(8,128)S(1)} async-done(((f32[16,9,128]{2,1,0:T(8,128)}), f32[16,9,128]{2,1,0:T(8,128)S(1)}, u32[]{:S(2)}, u32[]{:S(2)}) %all-to-all-start.4) | async-done | bytes 73760 | tf_op jit(solution)/shard_map/all_to_all | solution.py:40
  133.8 15.8 %all_to_all.63 = f32[16,10,128]{2,1,0:T(8,128)S(1)} all-to-all(f32[16,10,128]{2,1,0:T(8,128)S(1)} %broadcast_in_dim.14), channel_id=1, replica_groups=mesh['grp'=4,'wx'=4,'wz'=16,'wc'=2] {'wz'}, dimensions={0} | all-to-all | bytes 163840 | tf_op jit(solution)/shard_map/all_to_all | solution.py:47
  149.7 8.3 %all_to_all.64 = f32[4,16,10,128]{3,1,2,0:T(8,128)S(1)} all-to-all(f32[4,16,10,128]{3,1,2,0:T(8,128)S(1)} %broadcast_in_dim.15), channel_id=1, replica_groups=mesh['grp'=4,'wx'=4,'wz'=16,'wc'=2] {'wx'}, dimensions={0} | all-to-all | bytes 655360 | tf_op jit(solution)/shard_map/all_to_all | solution.py:47
  159.2 3.5 all-to-all-start.7
  162.8 11.1 %all-to-all-done.7 = f32[4,4,16,10,128]{4,2,1,3,0:T(8,128)S(1)} async-done(((f32[4,4,16,10,128]{4,2,1,3,0:T(8,128)}), f32[4,4,16,10,128]{4,2,1,3,0:T(8,128)S(1)}, u32[]{:S(2)}, u32[]{:S(2)}) %all-to-all-start.7) | async-done | bytes 1310752 | tf_op jit(solution)/shard_map/all_to_all | solution.py:47
  174.2 13.9 %all_to_all.65 = f32[2,4,4,16,10,128]{5,3,2,4,1,0:T(8,128)S(1)} all-to-all(f32[2,4,4,16,10,128]{5,3,2,4,1,0:T(8,128)S(1)} %broadcast_in_dim.17), channel_id=1, replica_groups=mesh['grp'=4,'wx'=4,'wz'=16,'wc'=2] {'wc'}, dimensions={0} | all-to-all | bytes 5242880 | tf_op jit(solution)/shard_map/all_to_all | solution.py:47
  188.1 1.5 copy-done.1
  191.8 1.7 slice-done
  193.4 3.4 copy.28
  196.8 3.0 reshape.463
  199.8 2.7 gather_fusion
  202.6 5.4 %copy.29 = f32[8,8,128,128]{2,3,1,0:T(8,128)} copy(f32[8,8,128,128]{3,2,1,0:T(8,128)} %bitcast.450) | data formatting | bytes 8388608 | tf_op jit(solution)/shard_map/reshape | solution.py:65
  208.0 4.4 fusion.96
  212.4 2.4 copy.30
  214.8 3.1 select_reduce_fusion.8
  218.5 11.4 %shard_map.64 = (f32[1,1024]{1,0:T(1,128)}, f32[1,128]{1,0:T(1,128)}) custom-call(f32[1024,1024]{1,0:T(8,128)} %get-tuple-element.233.refs_0_, f32[1,1024]{1,0:T(1,128)} %div.59.refs_1_, f32[1,1024]{1,0:T(1,128)} %bitcast.460), custom_call_target="tpu_custom_call" | custom-call | tf_op jit(solution)/shard_map/pallas_call | solution.py:182
  232.6 234.9 %conditional.1 = (f32[1024]{0:T(1024)}) conditional(s32[]{:T(128)} %bitcast.121, (f32[1024,1024]{1,0:T(8,128)}, f32[]{:T(128)}, f32[4,16,2,8]{1,3,2,0:T(8,128)S(1)}) %tuple.88, f32[1,1024]{1,0:T(1,128)} %get-tuple-element.211), branch_computations={%region_8.0_spmd, %region_11.14_spmd} | conditional | flops 4446827008 | bytes 69748688 | solution.py:241
  233.6 11.7 %custom-call.20 = f32[128,128]{1,0:T(8,128)S(1)} custom-call(f32[128,128]{1,0:T(8,128)S(1)} %slice.432), custom_call_target="Cholesky" | custom-call | tf_op jit(solution)/shard_map/cond/branch_0_fun/cholesky/custom-call.1 | solution.py:80
  246.7 9.8 %custom-call.21 = f32[1,128,128]{1,2,0:T(8,128)S(1)} custom-call(f32[1,128,128]{2,1,0:T(8,128)S(1)} %fusion.47), custom_call_target="InvertDiagBlocksLowerTriangular" | custom-call | tf_op jit(solution)/shard_map/cond/branch_0_fun/triangular_solve/custom-call.0 | solution.py:81
  256.8 1.6 fusion.19
  258.4 4.8 %slice_subtract_fusion = f32[896,896]{1,0:T(8,128)S(1)} fusion(f32[1024,1024]{1,0:T(8,128)} %get-tuple-element.205, f32[128,896]{1,0:T(8,128)S(1)} %fusion.19), kind=kOutput, calls=%fused_computation.1 | convolution fusion | flops 1233928192 | bytes 7340032 | tf_op jit(solution)/shard_map/cond/branch_0_fun/dot_general | solution.py:88
  263.2 1.7 copy-done
  264.9 11.9 %custom-call.22 = f32[128,128]{1,0:T(8,128)S(1)} custom-call(f32[128,128]{1,0:T(8,128)S(1)} %slice.564), custom_call_target="Cholesky" | custom-call | tf_op jit(solution)/shard_map/cond/branch_0_fun/cholesky/custom-call.1 | solution.py:80
  278.3 9.8 %custom-call.23 = f32[1,128,128]{1,2,0:T(8,128)S(1)} custom-call(f32[1,128,128]{2,1,0:T(8,128)S(1)} %fusion.48), custom_call_target="InvertDiagBlocksLowerTriangular" | custom-call | tf_op jit(solution)/shard_map/cond/branch_0_fun/triangular_solve/custom-call.0 | solution.py:81
  288.4 1.5 fusion.21
  289.9 3.7 slice_subtract_fusion.1
  295.0 11.7 %custom-call.24 = f32[128,128]{1,0:T(8,128)S(1)} custom-call(f32[128,128]{1,0:T(8,128)S(1)} %slice.567), custom_call_target="Cholesky" | custom-call | tf_op jit(solution)/shard_map/cond/branch_0_fun/cholesky/custom-call.1 | solution.py:80
  308.1 10.2 %custom-call.25 = f32[1,128,128]{1,2,0:T(8,128)S(1)} custom-call(f32[1,128,128]{2,1,0:T(8,128)S(1)} %fusion.49), custom_call_target="InvertDiagBlocksLowerTriangular" | custom-call | tf_op jit(solution)/shard_map/cond/branch_0_fun/triangular_solve/custom-call.0 | solution.py:81
  320.3 1.4 fusion.23
  322.3 2.9 slice_subtract_fusion.2
  326.4 11.7 %custom-call.26 = f32[128,128]{1,0:T(8,128)S(1)} custom-call(f32[128,128]{1,0:T(8,128)S(1)} %slice.570), custom_call_target="Cholesky" | custom-call | tf_op jit(solution)/shard_map/cond/branch_0_fun/cholesky/custom-call.1 | solution.py:80
  339.4 9.8 %custom-call.27 = f32[1,128,128]{1,2,0:T(8,128)S(1)} custom-call(f32[1,128,128]{2,1,0:T(8,128)S(1)} %fusion.50), custom_call_target="InvertDiagBlocksLowerTriangular" | custom-call | tf_op jit(solution)/shard_map/cond/branch_0_fun/triangular_solve/custom-call.0 | solution.py:81
  351.4 2.3 convolution_subtract_fusion
  354.7 11.9 %custom-call.28 = f32[128,128]{1,0:T(8,128)S(1)} custom-call(f32[128,128]{1,0:T(8,128)S(1)} %slice.573), custom_call_target="Cholesky" | custom-call | tf_op jit(solution)/shard_map/cond/branch_0_fun/cholesky/custom-call.1 | solution.py:80
  367.9 9.8 %custom-call.29 = f32[1,128,128]{1,2,0:T(8,128)S(1)} custom-call(f32[1,128,128]{2,1,0:T(8,128)S(1)} %fusion.51), custom_call_target="InvertDiagBlocksLowerTriangular" | custom-call | tf_op jit(solution)/shard_map/cond/branch_0_fun/triangular_solve/custom-call.0 | solution.py:81
  379.9 1.7 convolution_subtract_fusion.1
  381.6 11.7 %custom-call.30 = f32[128,128]{1,0:T(8,128)S(1)} custom-call(f32[128,128]{1,0:T(8,128)S(1)} %slice.576), custom_call_target="Cholesky" | custom-call | tf_op jit(solution)/shard_map/cond/branch_0_fun/cholesky/custom-call.1 | solution.py:80
  394.6 10.0 %custom-call.31 = f32[1,128,128]{1,2,0:T(8,128)S(1)} custom-call(f32[1,128,128]{2,1,0:T(8,128)S(1)} %fusion.52), custom_call_target="InvertDiagBlocksLowerTriangular" | custom-call | tf_op jit(solution)/shard_map/cond/branch_0_fun/triangular_solve/custom-call.0 | solution.py:81
  406.8 11.7 %custom-call.32 = f32[128,128]{1,0:T(8,128)S(1)} custom-call(f32[128,128]{1,0:T(8,128)S(1)} %slice.579), custom_call_target="Cholesky" | custom-call | tf_op jit(solution)/shard_map/cond/branch_0_fun/cholesky/custom-call.1 | solution.py:80
  419.9 9.8 %custom-call.33 = f32[1,128,128]{1,2,0:T(8,128)S(1)} custom-call(f32[1,128,128]{2,1,0:T(8,128)S(1)} %fusion.53), custom_call_target="InvertDiagBlocksLowerTriangular" | custom-call | tf_op jit(solution)/shard_map/cond/branch_0_fun/triangular_solve/custom-call.0 | solution.py:81
  432.7 11.7 %custom-call.34 = f32[128,128]{1,0:T(8,128)S(1)} custom-call(f32[128,128]{1,0:T(8,128)S(1)} %convolution_subtract_fusion.3), custom_call_target="Cholesky" | custom-call | tf_op jit(solution)/shard_map/cond/branch_0_fun/cholesky/custom-call.1 | solution.py:80
  445.8 10.0 %custom-call.35 = f32[1,128,128]{1,2,0:T(8,128)S(1)} custom-call(f32[1,128,128]{2,1,0:T(8,128)S(1)} %fusion.54), custom_call_target="InvertDiagBlocksLowerTriangular" | custom-call | tf_op jit(solution)/shard_map/cond/branch_0_fun/triangular_solve/custom-call.0 | solution.py:81
  (223 shorter events, 49.6 us)
Async XLA Ops:
  88.0 34.5 %copy-start.19 = (f32[8]{0:T(128)S(1)}, f32[8]{0:T(128)}, u32[]{:S(2)}) copy-start(f32[8]{0:T(128)} %param.42) | copy-start | bytes 100
  118.3 15.4 %all-to-all-start.4 = ((f32[16,9,128]{2,1,0:T(8,128)}), f32[16,9,128]{2,1,0:T(8,128)S(1)}, u32[]{:S(2)}, u32[]{:S(2)}) async-start(f32[16,9,128]{2,1,0:T(8,128)} %reshape.461), calls=%async_computation.4 | async-start | bytes 262144 | tf_op jit(solution)/shard_map/all_to_all | solution.py:40
  157.9 4.8 %copy-start.18 = (s32[64]{0:T(128)S(1)}, s32[64]{0:T(128)}, u32[]{:S(2)}) copy-start(s32[64]{0:T(128)} %constant.469) | copy-start | bytes 772
  159.2 14.7 %all-to-all-start.7 = ((f32[4,4,16,10,128]{4,2,1,3,0:T(8,128)}), f32[4,4,16,10,128]{4,2,1,3,0:T(8,128)S(1)}, u32[]{:S(2)}, u32[]{:S(2)}) async-start(f32[4,4,16,10,128]{4,2,1,3,0:T(8,128)} %broadcast_in_dim.16), calls=%async_computation.7 | async-start | bytes 2621440 | tf_op jit(solution)/shard_map/all_to_all | solution.py:47
  188.1 1.5 copy-start.1
  191.8 1.7 slice-start
  202.6 5.4 %copy-start.10 = (pred[8,8,128,128]{3,2,1,0:T(32,128)(4,1)S(1)}, pred[8,8,128,128]{3,2,1,0:T(32,128)(4,1)}, u32[]{:S(2)}) copy-start(pred[8,8,128,128]{3,2,1,0:T(32,128)(4,1)} %constant.440.clone) | copy-start | bytes 3145732
  212.4 2.4 copy-start.5
  256.8 62.1 %copy-start.9 = (f32[128,128]{1,0:T(8,128)}, f32[128,128]{1,0:T(8,128)S(1)}, u32[]{:S(2)}) copy-start(f32[128,128]{1,0:T(8,128)S(1)} %fusion.41) | copy-start | bytes 196612 | tf_op jit(solution)/shard_map/cond
  263.2 1.7 copy-start
  288.4 31.1 %copy-start.7 = (f32[128,128]{1,0:T(8,128)}, f32[128,128]{1,0:T(8,128)S(1)}, u32[]{:S(2)}) copy-start(f32[128,128]{1,0:T(8,128)S(1)} %fusion.39) | copy-start | bytes 196612 | tf_op jit(solution)/shard_map/cond
  293.6 1.4 copy-start.2
  318.6 6.6 %copy-start.8 = (f32[128,128]{1,0:T(8,128)}, f32[128,128]{1,0:T(8,128)S(1)}, u32[]{:S(2)}) copy-start(f32[128,128]{1,0:T(8,128)S(1)} %fusion.37) | copy-start | bytes 196612 | tf_op jit(solution)/shard_map/cond
  319.0 1.2 copy-start.16
  320.3 4.8 %copy-start.15 = (f32[1,128]{1,0:T(1,128)}, f32[1,128]{1,0:T(1,128)S(1)}, u32[]{:S(2)}) copy-start(f32[1,128]{1,0:T(1,128)S(1)} %fusion.81) | copy-start | bytes 1540 | tf_op jit(solution)/shard_map/cond
  325.2 1.2 copy-start.3
  349.7 18.2 %copy-start.12 = (f32[1,128]{1,0:T(1,128)}, f32[1,128]{1,0:T(1,128)S(1)}, u32[]{:S(2)}) copy-start(f32[1,128]{1,0:T(1,128)S(1)} %fusion.78) | copy-start | bytes 1540 | tf_op jit(solution)/shard_map/cond
  353.7 1.0 copy-start.4
  378.2 1.3 copy-start.13
  404.9 1.1 copy-start.6
  405.1 0.6 copy-start.14
  406.1 0.7 copy-start.11
  466.7 0.6 copy-start.17

commit v8 on v7

--- a/solution.py
+++ b/solution.py
@@ -132,18 +132,24 @@
 INTERPRET = False
 
 
-def cg_kernel(lam, steps, a_ref, b_ref, d_ref, x_ref, st_ref, pc_ref):
-    n = a_ref.shape[0]
-    chunk = BLOCK
+def cg_kernel(lam, steps, nb, u_ref, b_ref, d_ref, x_ref, st_ref, pc_ref):
+    n = nb * BLOCK
+    pairs = upper_pairs(nb)
 
     def matvec(p_row):
         pc_ref[...] = jnp.transpose(jnp.broadcast_to(p_row, (8, n)))
-        acc = jnp.zeros((1, n), jnp.float32)
-        for c in range(n // chunk):
-            blk = a_ref[c * chunk : (c + 1) * chunk, :]
-            col = pc_ref[c * chunk : (c + 1) * chunk, 0:1]
-            acc = acc + jnp.sum(blk * col, axis=0, keepdims=True)
-        return acc
+        rows = [jnp.zeros((1, BLOCK), jnp.float32) for _ in range(nb)]
+        cols = [jnp.zeros((BLOCK, 1), jnp.float32) for _ in range(nb)]
+        for k, (i, j) in enumerate(pairs):
+            blk = u_ref[k]
+            p_i = pc_ref[i * BLOCK : (i + 1) * BLOCK, 0:1]
+            rows[j] = rows[j] + jnp.sum(blk * p_i, axis=0, keepdims=True)
+            if i < j:
+                p_j = p_row[:, j * BLOCK : (j + 1) * BLOCK]
+                cols[i] = cols[i] + jnp.sum(blk * p_j, axis=1, keepdims=True)
+        col = jnp.concatenate(cols, axis=0)
+        col_row = jnp.transpose(jnp.broadcast_to(col, (n, 8)))[0:1, :]
+        return jnp.concatenate(rows, axis=1) + col_row
 
     b_row = b_ref[...]
     d_row = d_ref[...]
@@ -174,11 +180,22 @@
     st_ref[...] = jnp.where(lane == 0, bound, jnp.where(lane == 1, energy, 0.0))
 
 
-def kernel_cg(system, rhs, lam, steps, tol):
-    n = system.shape[0]
-    eye = np.eye(n, dtype=bool)
-    inv_diag = 1.0 / jnp.sum(jnp.where(eye, system, 0.0), axis=0)
-    body = lambda *refs: cg_kernel(lam, steps, *refs)
+def damp_packed(packed, nb, lam):
+    where = {pair: k for k, pair in enumerate(upper_pairs(nb))}
+    on_diag = np.zeros((len(where), 1, 1), np.float32)
+    for i in range(nb):
+        on_diag[where[(i, i)]] = 1.0
+    eye = np.eye(BLOCK, dtype=np.float32)[None]
+    return packed + (lam * on_diag) * eye
+
+
+def kernel_cg(packed, rhs, lam, steps, tol, nb):
+    n = nb * BLOCK
+    where = {pair: k for k, pair in enumerate(upper_pairs(nb))}
+    diag_blocks = packed[np.array([where[(i, i)] for i in range(nb)])]
+    eye = np.eye(BLOCK, dtype=bool)[None]
+    inv_diag = 1.0 / jnp.sum(jnp.where(eye, diag_blocks, 0.0), axis=1).reshape(n)
+    body = lambda *refs: cg_kernel(lam, steps, nb, *refs)
     x, st = pl.pallas_call(
         body,
         out_shape=(
@@ -187,7 +204,7 @@
         ),
         scratch_shapes=[pltpu.VMEM((n, 8), jnp.float32)],
         interpret=INTERPRET,
-    )(system, rhs[None, :], inv_diag[None, :])
+    )(packed, rhs[None, :], inv_diag[None, :])
     ok = st[0, 0] <= (tol * tol) * lam * st[0, 1]
     return x[0], ok
 
@@ -232,17 +249,15 @@
         order = [names.index(a) for a in WALK_PARTS if a in names]
         all_energy = jnp.transpose(energy, order + [len(names)]).reshape(WALKERS)
 
-        whole_gram = unpack_upper(whole_packed, nb)
         scaled_energy = (all_energy - jnp.mean(all_energy)) / root_walkers
-        identity_mat = jnp.eye(WALKERS, dtype=jnp.float32)
         lam = damping * total_params
-        system = whole_gram + lam * identity_mat
-        guess, ok = kernel_cg(system, scaled_energy, lam, CG_STEPS, CG_TOL)
+        system_packed = damp_packed(whole_packed, nb, lam)
+        guess, ok = kernel_cg(system_packed, scaled_energy, lam, CG_STEPS, CG_TOL, nb)
         solved = lax.cond(
             ok,
             lambda a, b, g: g,
-            lambda a, b, g: cholesky_solve(a, b, nb),
-            system,
+            lambda a, b, g: cholesky_solve(unpack_upper(a, nb), b, nb),
+            system_packed,
             scaled_energy,
             guess,
         )

time: 478 us -> 484 us (1.013)
    select_n x0 -> x1, other arithmetic: none -> 6.44 us  [unpack_upper(): blocks = jnp.where(mirror, jnp.swapaxes(blocks, 2, 3), blocks)]
    add x0 -> x2, local copies, waits for them, and re-layouts: none -> 6.41 us  [damp_packed(): return packed + lam * on_diag * eye]
    slice x3 -> x0, local copies, waits for them, and re-layouts: 5.07 us -> none  [on_device(): whole_packed = gathered[..., :per_dev, :].reshape(n_blocks, BLOCK, BLOCK)]
where the time goes in v8:
time: 484 us; the launch traced here: 476 us
  other arithmetic  200 us (41%)
  blocking collectives  150 us (31%)
  matrix products  46.7 us (10%)
  local copies, waits for them, and re-layouts  32.2 us (7%)
  waiting for transfers between devices  21.2 us (4%)
  Pallas kernels  15.8 us (3%)
  starting transfers between devices  7.05 us (1%)
    another operation x24, other arithmetic, cholesky_solve(): factor = lax.linalg.cholesky(system[lo:up, lo:up], symmetrize_input=False)  100 us
    another operation x16, other arithmetic, cholesky_solve(): lax.linalg.triangular_solve(factor, eye, left_side=True, lower=True)  83.7 us
    all_to_all x1, blocking collectives, on_device(): lax.all_to_all(log_grads, walk_axes, split_axis=1, concat_axis=0, tiled=T...  74.7 us
    all_to_all x3, blocking collectives, all_gather(): x = lax.all_to_all(copies, axis, 0, 0, tiled=True)  38.1 us
    all_to_all x3, blocking collectives, reduce_scatter(): x = lax.all_to_all(parts, axis, 0, 0, tiled=True).sum(0)  37 us
    dot_general x7, matrix products, cholesky_solve(): trailing = system[up:, up:] - jnp.dot(panel, panel.T, precision=hi)  17.1 us
    pallas_call x1, Pallas kernels, kernel_cg(): pl.pallas_call(body, out_shape=(jax.ShapeDtypeStruct((1, n), jnp.float32)...  15.8 us
    all_to_all x1, waiting for transfers between devices, reduce_scatter(): x = lax.all_to_all(parts, axis, 0, 0, tiled=True).sum(0)  10.7 us
  transfers between devices with their start and end apart: 2, of which 2 were waited for; matrix products, arithmetic and copies ran while one was open for 0% of the time, Pallas kernels for 0%

profile of v8, /device:TPU:1, one launch (start us, length us, event | category | flops | bytes accessed | tf_op | source)
XLA Modules:
  0.0 476.5 jit_solution(18222485870528384211)
XLA Ops:
  0.0 74.7 %all_to_all.59 = f32[8,128,256]{2,0,1:T(8,128)S(1)} all-to-all(f32[8,128,256]{2,0,1:T(8,128)} %bitcast.525), channel_id=1, replica_groups=mesh['grp'=4,'wx'=4,'wz'=16,'wc'=2] {'wx','wz','wc'}, dimensions={1} | all-to-all | bytes 2097152 | tf_op jit(solution)/shard_map/all_to_all | solution.py:220
  75.5 3.8 fusion.104
  79.8 7.4 %all_to_all.60 = f32[2,2304,128]{2,1,0:T(8,128)S(1)} all-to-all(f32[2,2304,128]{2,1,0:T(8,128)S(1)} %bitcast.523), channel_id=1, replica_groups=mesh['grp'=4,'wx'=4,'wz'=16,'wc'=2] {'wc'}, dimensions={0} | all-to-all | bytes 4718592 | tf_op jit(solution)/shard_map/all_to_all | solution.py:40
  88.5 20.0 %all_to_all.61 = f32[4,576,128]{2,1,0:T(8,128)S(1)} all-to-all(f32[4,576,128]{2,1,0:T(8,128)} %bitcast.522), channel_id=1, replica_groups=mesh['grp'=4,'wx'=4,'wz'=16,'wc'=2] {'grp'}, dimensions={0} | all-to-all | bytes 2359296 | tf_op jit(solution)/shard_map/all_to_all | solution.py:40
  108.5 9.6 %all_to_all.62 = f32[4,144,128]{2,1,0:T(8,128)S(1)} all-to-all(f32[4,144,128]{2,1,0:T(8,128)S(1)} %bitcast.524), channel_id=1, replica_groups=mesh['grp'=4,'wx'=4,'wz'=16,'wc'=2] {'wx'}, dimensions={0} | all-to-all | bytes 589824 | tf_op jit(solution)/shard_map/all_to_all | solution.py:40
  118.8 3.5 all-to-all-start.4
  123.5 10.7 %all-to-all-done.4 = f32[16,9,128]{2,1,0:T(8,128)S(1)} async-done(((f32[16,9,128]{2,1,0:T(8,128)}), f32[16,9,128]{2,1,0:T(8,128)S(1)}, u32[]{:S(2)}, u32[]{:S(2)}) %all-to-all-start.4) | async-done | bytes 73760 | tf_op jit(solution)/shard_map/all_to_all | solution.py:40
  134.3 15.8 %all_to_all.63 = f32[16,10,128]{2,1,0:T(8,128)S(1)} all-to-all(f32[16,10,128]{2,1,0:T(8,128)S(1)} %broadcast_in_dim.28), channel_id=1, replica_groups=mesh['grp'=4,'wx'=4,'wz'=16,'wc'=2] {'wz'}, dimensions={0} | all-to-all | bytes 163840 | tf_op jit(solution)/shard_map/all_to_all | solution.py:47
  150.2 8.3 %all_to_all.64 = f32[4,16,10,128]{3,1,2,0:T(8,128)S(1)} all-to-all(f32[4,16,10,128]{3,1,2,0:T(8,128)S(1)} %broadcast_in_dim.33), channel_id=1, replica_groups=mesh['grp'=4,'wx'=4,'wz'=16,'wc'=2] {'wx'}, dimensions={0} | all-to-all | bytes 655360 | tf_op jit(solution)/shard_map/all_to_all | solution.py:47
  159.7 3.5 all-to-all-start.7
  163.8 10.5 %all-to-all-done.7 = f32[4,4,16,10,128]{4,2,1,3,0:T(8,128)S(1)} async-done(((f32[4,4,16,10,128]{4,2,1,3,0:T(8,128)}), f32[4,4,16,10,128]{4,2,1,3,0:T(8,128)S(1)}, u32[]{:S(2)}, u32[]{:S(2)}) %all-to-all-start.7) | async-done | bytes 1310752 | tf_op jit(solution)/shard_map/all_to_all | solution.py:47
  174.7 14.0 %all_to_all.65 = f32[2,4,4,16,10,128]{5,3,2,4,1,0:T(8,128)S(1)} all-to-all(f32[2,4,4,16,10,128]{5,3,2,4,1,0:T(8,128)S(1)} %broadcast_in_dim.35), channel_id=1, replica_groups=mesh['grp'=4,'wx'=4,'wz'=16,'wc'=2] {'wc'}, dimensions={0} | all-to-all | bytes 5242880 | tf_op jit(solution)/shard_map/all_to_all | solution.py:47
  190.3 3.4 copy.34
  193.7 3.0 reshape.510.refs_0_
  196.7 1.5 slice_reduce_fusion
  199.8 1.5 gather_fusion.1
  203.8 15.8 %shard_map.97 = (f32[1,1024]{1,0:T(1,128)}, f32[1,128]{1,0:T(1,128)}) custom-call(f32[36,128,128]{2,1,0:T(8,128)S(1)} %reshape.510.refs_0_, f32[1,1024]{1,0:T(1,128)} %div.58.refs_1_, f32[1,1024]{1,0:T(1,128)} %bitcast.526), custom_call_target="tpu_custom_call" | custom-call | tf_op jit(solution)/shard_map/pallas_call | solution.py:199
  222.2 251.9 %conditional.1 = (f32[1024]{0:T(1024)}) conditional(s32[]{:T(128)} %bitcast.49, (f32[36,128,128]{2,1,0:T(8,128)S(1)}, f32[4,16,2,8]{3,1,0,2:T(8,128)S(1)}) %tuple.88, f32[1,1024]{1,0:T(1,128)} %get-tuple-element.211), branch_computations={%region_8.13_spmd.clone.clone, %region_11.14_spmd} | conditional | flops 4447874560 | bytes 129514016 | solution.py:256
  222.9 2.7 gather_fusion
  225.6 5.6 %copy.38 = f32[8,8,128,128]{2,1,3,0:T(8,128)} copy(f32[8,8,128,128]{3,2,1,0:T(8,128)} %bitcast.514) | data formatting | bytes 8388608 | tf_op jit(solution)/shard_map/cond/branch_0_fun/reshape | solution.py:65
  231.2 6.4 %bitcast_select_fusion = f32[8,8,128,128]{3,1,2,0:T(8,128)S(1)} fusion(pred[8,8,128,128]{3,1,2,0:T(8,128)(4,1)S(1)} %copy-done.11, f32[8,8,128,128]{2,1,3,0:T(8,128)} %copy.38, f32[8,8,128,128]{3,2,1,0:T(8,128)} %bitcast.515), kind=kLoop, calls=%fused_computation.3 | loop fusion | flops 1048576 | bytes 13631488 | tf_op jit(solution)/shard_map/cond/branch_0_fun/jit(_where)/select_n | solution.py:70
  238.7 1.9 copy-done
  240.6 11.7 %custom-call.36 = f32[128,128]{1,0:T(8,128)S(1)} custom-call(f32[128,128]{1,0:T(8,128)S(1)} %slice.636), custom_call_target="Cholesky" | custom-call | tf_op jit(solution)/shard_map/cond/branch_0_fun/cholesky/custom-call.1 | solution.py:80
  253.6 9.8 %custom-call.37 = f32[1,128,128]{1,2,0:T(8,128)S(1)} custom-call(f32[1,128,128]{2,1,0:T(8,128)S(1)} %fusion.45), custom_call_target="InvertDiagBlocksLowerTriangular" | custom-call | tf_op jit(solution)/shard_map/cond/branch_0_fun/triangular_solve/custom-call.0 | solution.py:81
  263.8 1.6 fusion.17
  265.3 5.0 %slice_subtract_fusion = f32[896,896]{1,0:T(8,128)S(1)} fusion(f32[1024,1024]{1,0:T(8,128)} %bitcast.519, f32[896,128]{1,0:T(8,128)S(1)} %fusion.17), kind=kOutput, calls=%fused_computation.4 | convolution fusion | flops 1233928192 | bytes 7340032 | tf_op jit(solution)/shard_map/cond/branch_0_fun/dot_general | solution.py:88
  270.4 1.7 copy-done.1
  272.1 11.7 %custom-call.38 = f32[128,128]{1,0:T(8,128)S(1)} custom-call(f32[128,128]{1,0:T(8,128)S(1)} %slice.639), custom_call_target="Cholesky" | custom-call | tf_op jit(solution)/shard_map/cond/branch_0_fun/cholesky/custom-call.1 | solution.py:80
  285.0 9.8 %custom-call.39 = f32[1,128,128]{1,2,0:T(8,128)S(1)} custom-call(f32[1,128,128]{2,1,0:T(8,128)S(1)} %fusion.46), custom_call_target="InvertDiagBlocksLowerTriangular" | custom-call | tf_op jit(solution)/shard_map/cond/branch_0_fun/triangular_solve/custom-call.0 | solution.py:81
  296.3 1.5 fusion.19
  298.3 3.7 slice_subtract_fusion.1
  302.0 1.4 copy-done.3
  303.4 12.1 %custom-call.40 = f32[128,128]{1,0:T(8,128)S(1)} custom-call(f32[128,128]{1,0:T(8,128)S(1)} %slice.642), custom_call_target="Cholesky" | custom-call | tf_op jit(solution)/shard_map/cond/branch_0_fun/cholesky/custom-call.1 | solution.py:80
  316.7 9.8 %custom-call.41 = f32[1,128,128]{1,2,0:T(8,128)S(1)} custom-call(f32[1,128,128]{2,1,0:T(8,128)S(1)} %fusion.47), custom_call_target="InvertDiagBlocksLowerTriangular" | custom-call | tf_op jit(solution)/shard_map/cond/branch_0_fun/triangular_solve/custom-call.0 | solution.py:81
  327.0 1.4 fusion.21
  329.0 2.9 slice_subtract_fusion.2
  333.0 11.7 %custom-call.42 = f32[128,128]{1,0:T(8,128)S(1)} custom-call(f32[128,128]{1,0:T(8,128)S(1)} %slice.645), custom_call_target="Cholesky" | custom-call | tf_op jit(solution)/shard_map/cond/branch_0_fun/cholesky/custom-call.1 | solution.py:80
  346.2 10.0 %custom-call.43 = f32[1,128,128]{1,2,0:T(8,128)S(1)} custom-call(f32[1,128,128]{2,1,0:T(8,128)S(1)} %fusion.48), custom_call_target="InvertDiagBlocksLowerTriangular" | custom-call | tf_op jit(solution)/shard_map/cond/branch_0_fun/triangular_solve/custom-call.0 | solution.py:81
  358.3 2.3 convolution_subtract_fusion
  361.6 11.7 %custom-call.44 = f32[128,128]{1,0:T(8,128)S(1)} custom-call(f32[128,128]{1,0:T(8,128)S(1)} %slice.648), custom_call_target="Cholesky" | custom-call | tf_op jit(solution)/shard_map/cond/branch_0_fun/cholesky/custom-call.1 | solution.py:80
  374.8 9.8 %custom-call.45 = f32[1,128,128]{1,2,0:T(8,128)S(1)} custom-call(f32[1,128,128]{2,1,0:T(8,128)S(1)} %fusion.49), custom_call_target="InvertDiagBlocksLowerTriangular" | custom-call | tf_op jit(solution)/shard_map/cond/branch_0_fun/triangular_solve/custom-call.0 | solution.py:81
  386.7 1.7 convolution_subtract_fusion.1
  388.5 11.9 %custom-call.46 = f32[128,128]{1,0:T(8,128)S(1)} custom-call(f32[128,128]{1,0:T(8,128)S(1)} %slice.651), custom_call_target="Cholesky" | custom-call | tf_op jit(solution)/shard_map/cond/branch_0_fun/cholesky/custom-call.1 | solution.py:80
  401.8 9.8 %custom-call.47 = f32[1,128,128]{1,2,0:T(8,128)S(1)} custom-call(f32[1,128,128]{2,1,0:T(8,128)S(1)} %fusion.50), custom_call_target="InvertDiagBlocksLowerTriangular" | custom-call | tf_op jit(solution)/shard_map/cond/branch_0_fun/triangular_solve/custom-call.0 | solution.py:81
  413.8 11.7 %custom-call.48 = f32[128,128]{1,0:T(8,128)S(1)} custom-call(f32[128,128]{1,0:T(8,128)S(1)} %slice.654), custom_call_target="Cholesky" | custom-call | tf_op jit(solution)/shard_map/cond/branch_0_fun/cholesky/custom-call.1 | solution.py:80
  426.8 9.8 %custom-call.49 = f32[1,128,128]{1,2,0:T(8,128)S(1)} custom-call(f32[1,128,128]{2,1,0:T(8,128)S(1)} %fusion.51), custom_call_target="InvertDiagBlocksLowerTriangular" | custom-call | tf_op jit(solution)/shard_map/cond/branch_0_fun/triangular_solve/custom-call.0 | solution.py:81
  439.8 11.7 %custom-call.50 = f32[128,128]{1,0:T(8,128)S(1)} custom-call(f32[128,128]{1,0:T(8,128)S(1)} %convolution_subtract_fusion.3), custom_call_target="Cholesky" | custom-call | tf_op jit(solution)/shard_map/cond/branch_0_fun/cholesky/custom-call.1 | solution.py:80
  452.9 9.8 %custom-call.51 = f32[1,128,128]{1,2,0:T(8,128)S(1)} custom-call(f32[1,128,128]{2,1,0:T(8,128)S(1)} %fusion.52), custom_call_target="InvertDiagBlocksLowerTriangular" | custom-call | tf_op jit(solution)/shard_map/cond/branch_0_fun/triangular_solve/custom-call.0 | solution.py:81
  (230 shorter events, 52.7 us)
Async XLA Ops:
  74.9 0.6 copy-start.14
  88.5 34.5 %copy-start.23 = (f32[8]{0:T(128)S(1)}, f32[8]{0:T(128)}, u32[]{:S(2)}) copy-start(f32[8]{0:T(128)} %param.45) | copy-start | bytes 100
  118.8 15.4 %all-to-all-start.4 = ((f32[16,9,128]{2,1,0:T(8,128)}), f32[16,9,128]{2,1,0:T(8,128)S(1)}, u32[]{:S(2)}, u32[]{:S(2)}) async-start(f32[16,9,128]{2,1,0:T(8,128)} %reshape.464), calls=%async_computation.4 | async-start | bytes 262144 | tf_op jit(solution)/shard_map/all_to_all | solution.py:40
  158.4 4.8 %copy-start.22 = (s32[8]{0:T(128)S(1)}, s32[8]{0:T(128)}, u32[]{:S(2)}) copy-start(s32[8]{0:T(128)} %constant.478) | copy-start | bytes 100
  159.7 14.7 %all-to-all-start.7 = ((f32[4,4,16,10,128]{4,2,1,3,0:T(8,128)}), f32[4,4,16,10,128]{4,2,1,3,0:T(8,128)S(1)}, u32[]{:S(2)}, u32[]{:S(2)}) async-start(f32[4,4,16,10,128]{4,2,1,3,0:T(8,128)} %broadcast_in_dim.34), calls=%async_computation.7 | async-start | bytes 2621440 | tf_op jit(solution)/shard_map/all_to_all | solution.py:47
  174.7 14.0 %copy-start.6 = (f32[2,4,4,16,9,128]{5,3,2,4,1,0:T(8,128)S(1)}, f32[2,4,4,16,9,128]{5,3,2,4,1,0:T(8,128)}, u32[]{:S(2)}) copy-start(f32[2,4,4,16,9,128]{5,3,2,4,1,0:T(8,128)} %constant.477) | copy-start | bytes 7077892
  188.7 1.6 copy-start.2
  193.7 7.7 %copy-start.13 = (pred[128,128]{1,0:T(32,128)(4,1)S(1)}, pred[128,128]{1,0:T(32,128)(4,1)}, u32[]{:S(2)}) copy-start(pred[128,128]{1,0:T(32,128)(4,1)} %constant.473) | copy-start | bytes 49156
  222.2 252.0 %copy-start.15 = (f32[256]{0:T(256)S(1)}, f32[256]{0:T(256)}, u32[]{:S(2)}) copy-start(f32[256]{0:T(256)} %copy-done.14) | copy-start | bytes 3076
  225.6 5.6 %copy-start.11 = (pred[8,8,128,128]{3,1,2,0:T(8,128)(4,1)S(1)}, pred[8,8,128,128]{3,1,2,0:T(8,128)(4,1)}, u32[]{:S(2)}) copy-start(pred[8,8,128,128]{3,1,2,0:T(8,128)(4,1)} %constant.447.clone.3) | copy-start | bytes 3145732 | tf_op jit(solution)/shard_map/cond
  238.7 1.9 copy-start
  263.8 31.5 %copy-start.10 = (f32[128,128]{1,0:T(8,128)}, f32[128,128]{1,0:T(8,128)S(1)}, u32[]{:S(2)}) copy-start(f32[128,128]{1,0:T(8,128)S(1)} %fusion.39) | copy-start | bytes 196612 | tf_op jit(solution)/shard_map/cond
  270.4 1.7 copy-start.1
  295.1 6.9 %copy-start.8 = (f32[128,128]{1,0:T(8,128)}, f32[128,128]{1,0:T(8,128)S(1)}, u32[]{:S(2)}) copy-start(f32[128,128]{1,0:T(8,128)S(1)} %fusion.37) | copy-start | bytes 196612 | tf_op jit(solution)/shard_map/cond
  295.5 0.6 copy-start.20
  302.0 1.4 copy-start.3
  326.9 2.1 copy-start.9
  327.0 4.8 %copy-start.19 = (f32[1,128]{1,0:T(1,128)}, f32[1,128]{1,0:T(1,128)S(1)}, u32[]{:S(2)}) copy-start(f32[1,128]{1,0:T(1,128)S(1)} %fusion.79) | copy-start | bytes 1540 | tf_op jit(solution)/shard_map/cond
  331.8 1.2 copy-start.4
  356.6 18.2 %copy-start.16 = (f32[1,128]{1,0:T(1,128)}, f32[1,128]{1,0:T(1,128)S(1)}, u32[]{:S(2)}) copy-start(f32[1,128]{1,0:T(1,128)S(1)} %fusion.76) | copy-start | bytes 1540 | tf_op jit(solution)/shard_map/cond
  360.6 1.0 copy-start.5
  385.1 1.3 copy-start.17
  411.9 1.2 copy-start.7
  412.1 0.6 copy-start.18
  413.1 0.7 copy-start.12
  473.3 0.6 copy-start.21

commit v9 on v8

--- a/solution.py
+++ b/solution.py
@@ -132,24 +132,23 @@
 INTERPRET = False
 
 
-def cg_kernel(lam, steps, nb, u_ref, b_ref, d_ref, x_ref, st_ref, pc_ref):
+def cg_kernel(lam, steps, nb, u_ref, b_ref, d_ref, x_ref, st_ref, pc_ref, lt_ref):
     n = nb * BLOCK
     pairs = upper_pairs(nb)
+    for k, (i, j) in enumerate(pairs):
+        if i < j:
+            lt_ref[k] = jnp.transpose(u_ref[k])
 
     def matvec(p_row):
         pc_ref[...] = jnp.transpose(jnp.broadcast_to(p_row, (8, n)))
         rows = [jnp.zeros((1, BLOCK), jnp.float32) for _ in range(nb)]
-        cols = [jnp.zeros((BLOCK, 1), jnp.float32) for _ in range(nb)]
         for k, (i, j) in enumerate(pairs):
-            blk = u_ref[k]
             p_i = pc_ref[i * BLOCK : (i + 1) * BLOCK, 0:1]
-            rows[j] = rows[j] + jnp.sum(blk * p_i, axis=0, keepdims=True)
+            rows[j] = rows[j] + jnp.sum(u_ref[k] * p_i, axis=0, keepdims=True)
             if i < j:
-                p_j = p_row[:, j * BLOCK : (j + 1) * BLOCK]
-                cols[i] = cols[i] + jnp.sum(blk * p_j, axis=1, keepdims=True)
-        col = jnp.concatenate(cols, axis=0)
-        col_row = jnp.transpose(jnp.broadcast_to(col, (n, 8)))[0:1, :]
-        return jnp.concatenate(rows, axis=1) + col_row
+                p_j = pc_ref[j * BLOCK : (j + 1) * BLOCK, 0:1]
+                rows[i] = rows[i] + jnp.sum(lt_ref[k] * p_j, axis=0, keepdims=True)
+        return jnp.concatenate(rows, axis=1)
 
     b_row = b_ref[...]
     d_row = d_ref[...]
@@ -202,7 +201,10 @@
             jax.ShapeDtypeStruct((1, n), jnp.float32),
             jax.ShapeDtypeStruct((1, 128), jnp.float32),
         ),
-        scratch_shapes=[pltpu.VMEM((n, 8), jnp.float32)],
+        scratch_shapes=[
+            pltpu.VMEM((n, 8), jnp.float32),
+            pltpu.VMEM(packed.shape, jnp.float32),
+        ],
         interpret=INTERPRET,
     )(packed, rhs[None, :], inv_diag[None, :])
     ok = st[0, 0] <= (tol * tol) * lam * st[0, 1]

time: 484 us -> 479 us (0.990)
  Pallas kernels: 15.8 us -> 10.4 us
    pallas_call x1, Pallas kernels: 15.8 us -> 10.4 us  [kernel_cg(): pl.pallas_call(body, out_shape=(jax.ShapeDtypeStruct((1, n), jnp.float32)...]
where the time goes in v9:
time: 479 us; the launch traced here: 471 us
  other arithmetic  200 us (42%)
  blocking collectives  150 us (31%)
  matrix products  46.7 us (10%)
  local copies, waits for them, and re-layouts  32.3 us (7%)
  waiting for transfers between devices  21.2 us (4%)
  Pallas kernels  10.4 us (2%)
  starting transfers between devices  7.05 us (1%)
    another operation x24, other arithmetic, cholesky_solve(): factor = lax.linalg.cholesky(system[lo:up, lo:up], symmetrize_input=False)  100 us
    another operation x16, other arithmetic, cholesky_solve(): lax.linalg.triangular_solve(factor, eye, left_side=True, lower=True)  83.7 us
    all_to_all x1, blocking collectives, on_device(): lax.all_to_all(log_grads, walk_axes, split_axis=1, concat_axis=0, tiled=T...  74.7 us
    all_to_all x3, blocking collectives, all_gather(): x = lax.all_to_all(copies, axis, 0, 0, tiled=True)  38.1 us
    all_to_all x3, blocking collectives, reduce_scatter(): x = lax.all_to_all(parts, axis, 0, 0, tiled=True).sum(0)  37 us
    dot_general x7, matrix products, cholesky_solve(): trailing = system[up:, up:] - jnp.dot(panel, panel.T, precision=hi)  17.1 us
    all_to_all x1, waiting for transfers between devices, reduce_scatter(): x = lax.all_to_all(parts, axis, 0, 0, tiled=True).sum(0)  10.7 us
    all_to_all x1, waiting for transfers between devices, all_gather(): x = lax.all_to_all(copies, axis, 0, 0, tiled=True)  10.5 us
  transfers between devices with their start and end apart: 2, of which 2 were waited for; matrix products, arithmetic and copies ran while one was open for 0% of the time, Pallas kernels for 0%

profile of v9, /device:TPU:1, one launch (start us, length us, event | category | flops | bytes accessed | tf_op | source)
XLA Modules:
  0.0 471.1 jit_solution(791714636836183422)
XLA Ops:
  0.0 74.7 %all_to_all.59 = f32[8,128,256]{2,0,1:T(8,128)S(1)} all-to-all(f32[8,128,256]{2,0,1:T(8,128)} %bitcast.525), channel_id=1, replica_groups=mesh['grp'=4,'wx'=4,'wz'=16,'wc'=2] {'wx','wz','wc'}, dimensions={1} | all-to-all | bytes 2097152 | tf_op jit(solution)/shard_map/all_to_all | solution.py:222
  75.5 3.8 fusion.104
  79.8 7.4 %all_to_all.60 = f32[2,2304,128]{2,1,0:T(8,128)S(1)} all-to-all(f32[2,2304,128]{2,1,0:T(8,128)S(1)} %bitcast.523), channel_id=1, replica_groups=mesh['grp'=4,'wx'=4,'wz'=16,'wc'=2] {'wc'}, dimensions={0} | all-to-all | bytes 4718592 | tf_op jit(solution)/shard_map/all_to_all | solution.py:40
  88.5 20.0 %all_to_all.61 = f32[4,576,128]{2,1,0:T(8,128)S(1)} all-to-all(f32[4,576,128]{2,1,0:T(8,128)} %bitcast.522), channel_id=1, replica_groups=mesh['grp'=4,'wx'=4,'wz'=16,'wc'=2] {'grp'}, dimensions={0} | all-to-all | bytes 2359296 | tf_op jit(solution)/shard_map/all_to_all | solution.py:40
  108.5 9.6 %all_to_all.62 = f32[4,144,128]{2,1,0:T(8,128)S(1)} all-to-all(f32[4,144,128]{2,1,0:T(8,128)S(1)} %bitcast.524), channel_id=1, replica_groups=mesh['grp'=4,'wx'=4,'wz'=16,'wc'=2] {'wx'}, dimensions={0} | all-to-all | bytes 589824 | tf_op jit(solution)/shard_map/all_to_all | solution.py:40
  118.8 3.5 all-to-all-start.4
  123.5 10.7 %all-to-all-done.4 = f32[16,9,128]{2,1,0:T(8,128)S(1)} async-done(((f32[16,9,128]{2,1,0:T(8,128)}), f32[16,9,128]{2,1,0:T(8,128)S(1)}, u32[]{:S(2)}, u32[]{:S(2)}) %all-to-all-start.4) | async-done | bytes 73760 | tf_op jit(solution)/shard_map/all_to_all | solution.py:40
  134.3 15.8 %all_to_all.63 = f32[16,10,128]{2,1,0:T(8,128)S(1)} all-to-all(f32[16,10,128]{2,1,0:T(8,128)S(1)} %broadcast_in_dim.28), channel_id=1, replica_groups=mesh['grp'=4,'wx'=4,'wz'=16,'wc'=2] {'wz'}, dimensions={0} | all-to-all | bytes 163840 | tf_op jit(solution)/shard_map/all_to_all | solution.py:47
  150.2 8.3 %all_to_all.64 = f32[4,16,10,128]{3,1,2,0:T(8,128)S(1)} all-to-all(f32[4,16,10,128]{3,1,2,0:T(8,128)S(1)} %broadcast_in_dim.33), channel_id=1, replica_groups=mesh['grp'=4,'wx'=4,'wz'=16,'wc'=2] {'wx'}, dimensions={0} | all-to-all | bytes 655360 | tf_op jit(solution)/shard_map/all_to_all | solution.py:47
  159.7 3.5 all-to-all-start.7
  163.8 10.5 %all-to-all-done.7 = f32[4,4,16,10,128]{4,2,1,3,0:T(8,128)S(1)} async-done(((f32[4,4,16,10,128]{4,2,1,3,0:T(8,128)}), f32[4,4,16,10,128]{4,2,1,3,0:T(8,128)S(1)}, u32[]{:S(2)}, u32[]{:S(2)}) %all-to-all-start.7) | async-done | bytes 1310752 | tf_op jit(solution)/shard_map/all_to_all | solution.py:47
  174.7 14.0 %all_to_all.65 = f32[2,4,4,16,10,128]{5,3,2,4,1,0:T(8,128)S(1)} all-to-all(f32[2,4,4,16,10,128]{5,3,2,4,1,0:T(8,128)S(1)} %broadcast_in_dim.35), channel_id=1, replica_groups=mesh['grp'=4,'wx'=4,'wz'=16,'wc'=2] {'wc'}, dimensions={0} | all-to-all | bytes 5242880 | tf_op jit(solution)/shard_map/all_to_all | solution.py:47
  190.3 3.4 copy.34
  193.7 3.0 reshape.510.refs_0_
  196.7 1.5 slice_reduce_fusion
  199.8 1.5 gather_fusion.1
  203.8 10.4 %shard_map.97 = (f32[1,1024]{1,0:T(1,128)}, f32[1,128]{1,0:T(1,128)}) custom-call(f32[36,128,128]{2,1,0:T(8,128)S(1)} %reshape.510.refs_0_, f32[1,1024]{1,0:T(1,128)} %div.58.refs_1_, f32[1,1024]{1,0:T(1,128)} %bitcast.526), custom_call_target="tpu_custom_call" | custom-call | tf_op jit(solution)/shard_map/pallas_call | solution.py:198
  216.8 251.9 %conditional.1 = (f32[1024]{0:T(1024)}) conditional(s32[]{:T(128)} %bitcast.49, (f32[36,128,128]{2,1,0:T(8,128)S(1)}, f32[4,16,2,8]{3,1,0,2:T(8,128)S(1)}) %tuple.88, f32[1,1024]{1,0:T(1,128)} %get-tuple-element.211), branch_computations={%region_8.13_spmd.clone.clone, %region_11.14_spmd} | conditional | flops 4447874560 | bytes 129514016 | solution.py:258
  217.5 2.7 gather_fusion
  220.2 5.6 %copy.38 = f32[8,8,128,128]{2,1,3,0:T(8,128)} copy(f32[8,8,128,128]{3,2,1,0:T(8,128)} %bitcast.514) | data formatting | bytes 8388608 | tf_op jit(solution)/shard_map/cond/branch_0_fun/reshape | solution.py:65
  225.8 6.4 %bitcast_select_fusion = f32[8,8,128,128]{3,1,2,0:T(8,128)S(1)} fusion(pred[8,8,128,128]{3,1,2,0:T(8,128)(4,1)S(1)} %copy-done.11, f32[8,8,128,128]{2,1,3,0:T(8,128)} %copy.38, f32[8,8,128,128]{3,2,1,0:T(8,128)} %bitcast.515), kind=kLoop, calls=%fused_computation.3 | loop fusion | flops 1048576 | bytes 13631488 | tf_op jit(solution)/shard_map/cond/branch_0_fun/jit(_where)/select_n | solution.py:70
  233.3 1.9 copy-done
  235.2 11.7 %custom-call.36 = f32[128,128]{1,0:T(8,128)S(1)} custom-call(f32[128,128]{1,0:T(8,128)S(1)} %slice.636), custom_call_target="Cholesky" | custom-call | tf_op jit(solution)/shard_map/cond/branch_0_fun/cholesky/custom-call.1 | solution.py:80
  248.2 9.8 %custom-call.37 = f32[1,128,128]{1,2,0:T(8,128)S(1)} custom-call(f32[1,128,128]{2,1,0:T(8,128)S(1)} %fusion.45), custom_call_target="InvertDiagBlocksLowerTriangular" | custom-call | tf_op jit(solution)/shard_map/cond/branch_0_fun/triangular_solve/custom-call.0 | solution.py:81
  258.4 1.6 fusion.17
  259.9 5.0 %slice_subtract_fusion = f32[896,896]{1,0:T(8,128)S(1)} fusion(f32[1024,1024]{1,0:T(8,128)} %bitcast.519, f32[896,128]{1,0:T(8,128)S(1)} %fusion.17), kind=kOutput, calls=%fused_computation.4 | convolution fusion | flops 1233928192 | bytes 7340032 | tf_op jit(solution)/shard_map/cond/branch_0_fun/dot_general | solution.py:88
  265.0 1.7 copy-done.1
  266.7 11.7 %custom-call.38 = f32[128,128]{1,0:T(8,128)S(1)} custom-call(f32[128,128]{1,0:T(8,128)S(1)} %slice.639), custom_call_target="Cholesky" | custom-call | tf_op jit(solution)/shard_map/cond/branch_0_fun/cholesky/custom-call.1 | solution.py:80
  279.6 9.8 %custom-call.39 = f32[1,128,128]{1,2,0:T(8,128)S(1)} custom-call(f32[1,128,128]{2,1,0:T(8,128)S(1)} %fusion.46), custom_call_target="InvertDiagBlocksLowerTriangular" | custom-call | tf_op jit(solution)/shard_map/cond/branch_0_fun/triangular_solve/custom-call.0 | solution.py:81
  290.9 1.5 fusion.19
  292.9 3.7 slice_subtract_fusion.1
  296.6 1.4 copy-done.3
  298.0 12.1 %custom-call.40 = f32[128,128]{1,0:T(8,128)S(1)} custom-call(f32[128,128]{1,0:T(8,128)S(1)} %slice.642), custom_call_target="Cholesky" | custom-call | tf_op jit(solution)/shard_map/cond/branch_0_fun/cholesky/custom-call.1 | solution.py:80
  311.4 9.8 %custom-call.41 = f32[1,128,128]{1,2,0:T(8,128)S(1)} custom-call(f32[1,128,128]{2,1,0:T(8,128)S(1)} %fusion.47), custom_call_target="InvertDiagBlocksLowerTriangular" | custom-call | tf_op jit(solution)/shard_map/cond/branch_0_fun/triangular_solve/custom-call.0 | solution.py:81
  321.6 1.4 fusion.21
  323.6 2.9 slice_subtract_fusion.2
  327.6 11.7 %custom-call.42 = f32[128,128]{1,0:T(8,128)S(1)} custom-call(f32[128,128]{1,0:T(8,128)S(1)} %slice.645), custom_call_target="Cholesky" | custom-call | tf_op jit(solution)/shard_map/cond/branch_0_fun/cholesky/custom-call.1 | solution.py:80
  340.8 10.0 %custom-call.43 = f32[1,128,128]{1,2,0:T(8,128)S(1)} custom-call(f32[1,128,128]{2,1,0:T(8,128)S(1)} %fusion.48), custom_call_target="InvertDiagBlocksLowerTriangular" | custom-call | tf_op jit(solution)/shard_map/cond/branch_0_fun/triangular_solve/custom-call.0 | solution.py:81
  352.9 2.3 convolution_subtract_fusion
  356.2 11.7 %custom-call.44 = f32[128,128]{1,0:T(8,128)S(1)} custom-call(f32[128,128]{1,0:T(8,128)S(1)} %slice.648), custom_call_target="Cholesky" | custom-call | tf_op jit(solution)/shard_map/cond/branch_0_fun/cholesky/custom-call.1 | solution.py:80
  369.4 9.8 %custom-call.45 = f32[1,128,128]{1,2,0:T(8,128)S(1)} custom-call(f32[1,128,128]{2,1,0:T(8,128)S(1)} %fusion.49), custom_call_target="InvertDiagBlocksLowerTriangular" | custom-call | tf_op jit(solution)/shard_map/cond/branch_0_fun/triangular_solve/custom-call.0 | solution.py:81
  381.3 1.7 convolution_subtract_fusion.1
  383.1 11.9 %custom-call.46 = f32[128,128]{1,0:T(8,128)S(1)} custom-call(f32[128,128]{1,0:T(8,128)S(1)} %slice.651), custom_call_target="Cholesky" | custom-call | tf_op jit(solution)/shard_map/cond/branch_0_fun/cholesky/custom-call.1 | solution.py:80
  396.4 9.8 %custom-call.47 = f32[1,128,128]{1,2,0:T(8,128)S(1)} custom-call(f32[1,128,128]{2,1,0:T(8,128)S(1)} %fusion.50), custom_call_target="InvertDiagBlocksLowerTriangular" | custom-call | tf_op jit(solution)/shard_map/cond/branch_0_fun/triangular_solve/custom-call.0 | solution.py:81
  408.4 11.7 %custom-call.48 = f32[128,128]{1,0:T(8,128)S(1)} custom-call(f32[128,128]{1,0:T(8,128)S(1)} %slice.654), custom_call_target="Cholesky" | custom-call | tf_op jit(solution)/shard_map/cond/branch_0_fun/cholesky/custom-call.1 | solution.py:80
  421.4 9.8 %custom-call.49 = f32[1,128,128]{1,2,0:T(8,128)S(1)} custom-call(f32[1,128,128]{2,1,0:T(8,128)S(1)} %fusion.51), custom_call_target="InvertDiagBlocksLowerTriangular" | custom-call | tf_op jit(solution)/shard_map/cond/branch_0_fun/triangular_solve/custom-call.0 | solution.py:81
  434.4 11.7 %custom-call.50 = f32[128,128]{1,0:T(8,128)S(1)} custom-call(f32[128,128]{1,0:T(8,128)S(1)} %convolution_subtract_fusion.3), custom_call_target="Cholesky" | custom-call | tf_op jit(solution)/shard_map/cond/branch_0_fun/cholesky/custom-call.1 | solution.py:80
  447.5 9.8 %custom-call.51 = f32[1,128,128]{1,2,0:T(8,128)S(1)} custom-call(f32[1,128,128]{2,1,0:T(8,128)S(1)} %fusion.52), custom_call_target="InvertDiagBlocksLowerTriangular" | custom-call | tf_op jit(solution)/shard_map/cond/branch_0_fun/triangular_solve/custom-call.0 | solution.py:81
  (230 shorter events, 52.7 us)
Async XLA Ops:
  74.9 0.6 copy-start.14
  88.5 34.5 %copy-start.23 = (f32[8]{0:T(128)S(1)}, f32[8]{0:T(128)}, u32[]{:S(2)}) copy-start(f32[8]{0:T(128)} %param.45) | copy-start | bytes 100
  118.8 15.4 %all-to-all-start.4 = ((f32[16,9,128]{2,1,0:T(8,128)}), f32[16,9,128]{2,1,0:T(8,128)S(1)}, u32[]{:S(2)}, u32[]{:S(2)}) async-start(f32[16,9,128]{2,1,0:T(8,128)} %reshape.464), calls=%async_computation.4 | async-start | bytes 262144 | tf_op jit(solution)/shard_map/all_to_all | solution.py:40
  158.4 4.8 %copy-start.22 = (s32[8]{0:T(128)S(1)}, s32[8]{0:T(128)}, u32[]{:S(2)}) copy-start(s32[8]{0:T(128)} %constant.478) | copy-start | bytes 100
  159.7 14.7 %all-to-all-start.7 = ((f32[4,4,16,10,128]{4,2,1,3,0:T(8,128)}), f32[4,4,16,10,128]{4,2,1,3,0:T(8,128)S(1)}, u32[]{:S(2)}, u32[]{:S(2)}) async-start(f32[4,4,16,10,128]{4,2,1,3,0:T(8,128)} %broadcast_in_dim.34), calls=%async_computation.7 | async-start | bytes 2621440 | tf_op jit(solution)/shard_map/all_to_all | solution.py:47
  174.7 14.0 %copy-start.6 = (f32[2,4,4,16,9,128]{5,3,2,4,1,0:T(8,128)S(1)}, f32[2,4,4,16,9,128]{5,3,2,4,1,0:T(8,128)}, u32[]{:S(2)}) copy-start(f32[2,4,4,16,9,128]{5,3,2,4,1,0:T(8,128)} %constant.477) | copy-start | bytes 7077892
  188.7 1.6 copy-start.2
  193.7 7.7 %copy-start.13 = (pred[128,128]{1,0:T(32,128)(4,1)S(1)}, pred[128,128]{1,0:T(32,128)(4,1)}, u32[]{:S(2)}) copy-start(pred[128,128]{1,0:T(32,128)(4,1)} %constant.473) | copy-start | bytes 49156
  216.8 252.0 %copy-start.15 = (f32[256]{0:T(256)S(1)}, f32[256]{0:T(256)}, u32[]{:S(2)}) copy-start(f32[256]{0:T(256)} %copy-done.14) | copy-start | bytes 3076
  220.2 5.6 %copy-start.11 = (pred[8,8,128,128]{3,1,2,0:T(8,128)(4,1)S(1)}, pred[8,8,128,128]{3,1,2,0:T(8,128)(4,1)}, u32[]{:S(2)}) copy-start(pred[8,8,128,128]{3,1,2,0:T(8,128)(4,1)} %constant.447.clone.3) | copy-start | bytes 3145732 | tf_op jit(solution)/shard_map/cond
  233.3 1.9 copy-start
  258.4 31.5 %copy-start.10 = (f32[128,128]{1,0:T(8,128)}, f32[128,128]{1,0:T(8,128)S(1)}, u32[]{:S(2)}) copy-start(f32[128,128]{1,0:T(8,128)S(1)} %fusion.39) | copy-start | bytes 196612 | tf_op jit(solution)/shard_map/cond
  265.0 1.7 copy-start.1
  289.7 6.9 %copy-start.8 = (f32[128,128]{1,0:T(8,128)}, f32[128,128]{1,0:T(8,128)S(1)}, u32[]{:S(2)}) copy-start(f32[128,128]{1,0:T(8,128)S(1)} %fusion.37) | copy-start | bytes 196612 | tf_op jit(solution)/shard_map/cond
  290.1 0.6 copy-start.20
  296.6 1.4 copy-start.3
  321.5 2.1 copy-start.9
  321.6 4.8 %copy-start.19 = (f32[1,128]{1,0:T(1,128)}, f32[1,128]{1,0:T(1,128)S(1)}, u32[]{:S(2)}) copy-start(f32[1,128]{1,0:T(1,128)S(1)} %fusion.79) | copy-start | bytes 1540 | tf_op jit(solution)/shard_map/cond
  326.4 1.2 copy-start.4
  351.2 18.1 %copy-start.16 = (f32[1,128]{1,0:T(1,128)}, f32[1,128]{1,0:T(1,128)S(1)}, u32[]{:S(2)}) copy-start(f32[1,128]{1,0:T(1,128)S(1)} %fusion.76) | copy-start | bytes 1540 | tf_op jit(solution)/shard_map/cond
  355.2 1.0 copy-start.5
  379.7 1.3 copy-start.17
  406.5 1.2 copy-start.7
  406.7 0.6 copy-start.18
  407.7 0.7 copy-start.12
  467.9 0.6 copy-start.21

commit v10 on v9

--- a/solution.py
+++ b/solution.py
@@ -132,7 +132,7 @@
 INTERPRET = False
 
 
-def cg_kernel(lam, steps, nb, u_ref, b_ref, d_ref, x_ref, st_ref, pc_ref, lt_ref):
+def cg_kernel(lam, steps, nb, u_ref, b_ref, x_ref, st_ref, pc_ref, lt_ref):
     n = nb * BLOCK
     pairs = upper_pairs(nb)
     for k, (i, j) in enumerate(pairs):
@@ -151,7 +151,15 @@
         return jnp.concatenate(rows, axis=1)
 
     b_row = b_ref[...]
-    d_row = d_ref[...]
+    where = {pair: k for k, pair in enumerate(pairs)}
+    eye = lax.broadcasted_iota(jnp.int32, (BLOCK, BLOCK), 0) == lax.broadcasted_iota(
+        jnp.int32, (BLOCK, BLOCK), 1
+    )
+    diag = [
+        jnp.sum(jnp.where(eye, u_ref[where[(i, i)]], 0.0), axis=0, keepdims=True)
+        for i in range(nb)
+    ]
+    d_row = 1.0 / jnp.concatenate(diag, axis=1)
     z_row = b_row * d_row
     rz = jnp.sum(b_row * z_row, axis=1, keepdims=True)
 
@@ -190,10 +198,6 @@
 
 def kernel_cg(packed, rhs, lam, steps, tol, nb):
     n = nb * BLOCK
-    where = {pair: k for k, pair in enumerate(upper_pairs(nb))}
-    diag_blocks = packed[np.array([where[(i, i)] for i in range(nb)])]
-    eye = np.eye(BLOCK, dtype=bool)[None]
-    inv_diag = 1.0 / jnp.sum(jnp.where(eye, diag_blocks, 0.0), axis=1).reshape(n)
     body = lambda *refs: cg_kernel(lam, steps, nb, *refs)
     x, st = pl.pallas_call(
         body,
@@ -206,7 +210,7 @@
             pltpu.VMEM(packed.shape, jnp.float32),
         ],
         interpret=INTERPRET,
-    )(packed, rhs[None, :], inv_diag[None, :])
+    )(packed, rhs[None, :])
     ok = st[0, 0] <= (tol * tol) * lam * st[0, 1]
     return x[0], ok
 

time: 479 us -> 474 us (0.990)
  blocking collectives: 150 us -> 163 us
  waiting for transfers between devices: 21.2 us -> 10.6 us
    all_to_all x3 -> x4, blocking collectives: 38.1 us -> 51.7 us  [all_gather(): x = lax.all_to_all(copies, axis, 0, 0, tiled=True)]
    all_to_all x1 -> x0, waiting for transfers between devices: 10.5 us -> none  [all_gather(): x = lax.all_to_all(copies, axis, 0, 0, tiled=True)]
  transfers between devices with their start and end apart: 2 -> 1, of which waited for: 2 -> 1; matrix products, arithmetic and copies ran while one was open for 0% -> 0% of each run, Pallas kernels for 0% -> 0%
where the time goes in v10:
time: 474 us; the launch traced here: 466 us
  other arithmetic  198 us (42%)
  blocking collectives  163 us (34%)
  matrix products  46.7 us (10%)
  local copies, waits for them, and re-layouts  29.8 us (6%)
  waiting for transfers between devices  10.6 us (2%)
  Pallas kernels  10.4 us (2%)
    another operation x24, other arithmetic, cholesky_solve(): factor = lax.linalg.cholesky(system[lo:up, lo:up], symmetrize_input=False)  100 us
    another operation x16, other arithmetic, cholesky_solve(): lax.linalg.triangular_solve(factor, eye, left_side=True, lower=True)  83.7 us
    all_to_all x1, blocking collectives, on_device(): lax.all_to_all(log_grads, walk_axes, split_axis=1, concat_axis=0, tiled=T...  74.7 us
    all_to_all x4, blocking collectives, all_gather(): x = lax.all_to_all(copies, axis, 0, 0, tiled=True)  51.7 us
    all_to_all x3, blocking collectives, reduce_scatter(): x = lax.all_to_all(parts, axis, 0, 0, tiled=True).sum(0)  37 us
    dot_general x7, matrix products, cholesky_solve(): trailing = system[up:, up:] - jnp.dot(panel, panel.T, precision=hi)  17.1 us
    all_to_all x1, waiting for transfers between devices, reduce_scatter(): x = lax.all_to_all(parts, axis, 0, 0, tiled=True).sum(0)  10.6 us
    pallas_call x1, Pallas kernels, kernel_cg(): pl.pallas_call(body, out_shape=(jax.ShapeDtypeStruct((1, n), jnp.float32)...  10.4 us
  transfers between devices with their start and end apart: 1, of which 1 were waited for; matrix products, arithmetic and copies ran while one was open for 0% of the time, Pallas kernels for 0%

profile of v10, /device:TPU:1, one launch (start us, length us, event | category | flops | bytes accessed | tf_op | source)
XLA Modules:
  0.0 466.3 jit_solution(8762707645162088503)
XLA Ops:
  0.0 74.7 %all_to_all.59 = f32[8,128,256]{2,0,1:T(8,128)S(1)} all-to-all(f32[8,128,256]{2,0,1:T(8,128)} %bitcast.453), channel_id=1, replica_groups=mesh['grp'=4,'wx'=4,'wz'=16,'wc'=2] {'wx','wz','wc'}, dimensions={1} | all-to-all | bytes 2097152 | tf_op jit(solution)/shard_map/all_to_all | solution.py:226
  75.0 3.8 fusion.104
  79.3 7.5 %all_to_all.60 = f32[2,2304,128]{2,1,0:T(8,128)S(1)} all-to-all(f32[2,2304,128]{2,1,0:T(8,128)S(1)} %bitcast.451), channel_id=1, replica_groups=mesh['grp'=4,'wx'=4,'wz'=16,'wc'=2] {'wc'}, dimensions={0} | all-to-all | bytes 4718592 | tf_op jit(solution)/shard_map/all_to_all | solution.py:40
  88.0 20.0 %all_to_all.61 = f32[4,576,128]{2,1,0:T(8,128)S(1)} all-to-all(f32[4,576,128]{2,1,0:T(8,128)} %bitcast.450), channel_id=1, replica_groups=mesh['grp'=4,'wx'=4,'wz'=16,'wc'=2] {'grp'}, dimensions={0} | all-to-all | bytes 2359296 | tf_op jit(solution)/shard_map/all_to_all | solution.py:40
  108.1 9.6 %all_to_all.62 = f32[4,144,128]{2,1,0:T(8,128)S(1)} all-to-all(f32[4,144,128]{2,1,0:T(8,128)S(1)} %bitcast.452), channel_id=1, replica_groups=mesh['grp'=4,'wx'=4,'wz'=16,'wc'=2] {'wx'}, dimensions={0} | all-to-all | bytes 589824 | tf_op jit(solution)/shard_map/all_to_all | solution.py:40
  118.3 3.5 all-to-all-start.4
  123.2 10.6 %all-to-all-done.4 = f32[16,9,128]{2,1,0:T(8,128)S(1)} async-done(((f32[16,9,128]{2,1,0:T(8,128)}), f32[16,9,128]{2,1,0:T(8,128)S(1)}, u32[]{:S(2)}, u32[]{:S(2)}) %all-to-all-start.4) | async-done | bytes 73760 | tf_op jit(solution)/shard_map/all_to_all | solution.py:40
  133.8 15.8 %all_to_all.63 = f32[16,10,128]{2,1,0:T(8,128)S(1)} all-to-all(f32[16,10,128]{2,1,0:T(8,128)S(1)} %broadcast_in_dim.13), channel_id=1, replica_groups=mesh['grp'=4,'wx'=4,'wz'=16,'wc'=2] {'wz'}, dimensions={0} | all-to-all | bytes 163840 | tf_op jit(solution)/shard_map/all_to_all | solution.py:47
  149.7 8.3 %all_to_all.64 = f32[4,16,10,128]{3,1,2,0:T(8,128)S(1)} all-to-all(f32[4,16,10,128]{3,1,2,0:T(8,128)S(1)} %broadcast_in_dim.14), channel_id=1, replica_groups=mesh['grp'=4,'wx'=4,'wz'=16,'wc'=2] {'wx'}, dimensions={0} | all-to-all | bytes 655360 | tf_op jit(solution)/shard_map/all_to_all | solution.py:47
  158.1 13.6 %all_to_all.65 = f32[4,4,16,10,128]{4,2,1,3,0:T(8,128)S(1)} all-to-all(f32[4,4,16,10,128]{4,2,1,3,0:T(8,128)S(1)} %broadcast_in_dim.15), channel_id=1, replica_groups=mesh['grp'=4,'wx'=4,'wz'=16,'wc'=2] {'grp'}, dimensions={0} | all-to-all | bytes 2621440 | tf_op jit(solution)/shard_map/all_to_all | solution.py:47
  172.1 14.0 %all_to_all.66 = f32[2,4,4,16,10,128]{5,3,2,4,1,0:T(8,128)S(1)} all-to-all(f32[2,4,4,16,10,128]{5,3,2,4,1,0:T(8,128)S(1)} %broadcast_in_dim.16), channel_id=1, replica_groups=mesh['grp'=4,'wx'=4,'wz'=16,'wc'=2] {'wc'}, dimensions={0} | all-to-all | bytes 5242880 | tf_op jit(solution)/shard_map/all_to_all | solution.py:47
  186.1 1.5 copy-done.2
  190.5 2.1 slice_add_fusion
  192.6 3.4 copy.31
  196.0 3.0 reshape.497.refs_0_
  199.0 10.4 %shard_map.70 = (f32[1,1024]{1,0:T(1,128)}, f32[1,128]{1,0:T(1,128)}) custom-call(f32[36,128,128]{2,1,0:T(8,128)S(1)} %reshape.497.refs_0_, f32[1,1024]{1,0:T(1,128)} %div.42.refs_1_), custom_call_target="tpu_custom_call" | custom-call | tf_op jit(solution)/shard_map/pallas_call | solution.py:202
  209.4 1.4 fusion.102
  212.1 251.9 %conditional.1 = (f32[1024]{0:T(1024)}) conditional(s32[]{:T(128)} %bitcast.48, (f32[36,128,128]{2,1,0:T(8,128)S(1)}, f32[4,16,2,8]{3,1,0,2:T(8,128)S(1)}) %tuple.82, f32[1,1024]{1,0:T(1,128)} %get-tuple-element.211), branch_computations={%region_7.12_spmd.clone, %region_10.0_spmd} | conditional | flops 4447874560 | bytes 129514016 | solution.py:262
  212.7 2.7 gather_fusion
  215.5 5.6 %copy.27 = f32[8,8,128,128]{2,1,3,0:T(8,128)} copy(f32[8,8,128,128]{3,2,1,0:T(8,128)} %bitcast.442) | data formatting | bytes 8388608 | tf_op jit(solution)/shard_map/cond/branch_0_fun/reshape | solution.py:65
  221.1 6.4 %bitcast_select_fusion = f32[8,8,128,128]{3,1,2,0:T(8,128)S(1)} fusion(pred[8,8,128,128]{3,1,2,0:T(8,128)(4,1)S(1)} %copy-done.11, f32[8,8,128,128]{2,1,3,0:T(8,128)} %copy.27, f32[8,8,128,128]{3,2,1,0:T(8,128)} %bitcast.443), kind=kLoop, calls=%fused_computation.2 | loop fusion | flops 1048576 | bytes 13631488 | tf_op jit(solution)/shard_map/cond/branch_0_fun/jit(_where)/select_n | solution.py:70
  228.5 1.9 copy-done
  230.5 11.7 %custom-call.20 = f32[128,128]{1,0:T(8,128)S(1)} custom-call(f32[128,128]{1,0:T(8,128)S(1)} %slice.599), custom_call_target="Cholesky" | custom-call | tf_op jit(solution)/shard_map/cond/branch_0_fun/cholesky/custom-call.1 | solution.py:80
  243.5 9.8 %custom-call.21 = f32[1,128,128]{1,2,0:T(8,128)S(1)} custom-call(f32[1,128,128]{2,1,0:T(8,128)S(1)} %fusion.45), custom_call_target="InvertDiagBlocksLowerTriangular" | custom-call | tf_op jit(solution)/shard_map/cond/branch_0_fun/triangular_solve/custom-call.0 | solution.py:81
  253.6 1.6 fusion.17
  255.2 5.0 %slice_subtract_fusion = f32[896,896]{1,0:T(8,128)S(1)} fusion(f32[1024,1024]{1,0:T(8,128)} %bitcast.447, f32[896,128]{1,0:T(8,128)S(1)} %fusion.17), kind=kOutput, calls=%fused_computation.3 | convolution fusion | flops 1233928192 | bytes 7340032 | tf_op jit(solution)/shard_map/cond/branch_0_fun/dot_general | solution.py:88
  260.3 1.7 copy-done.1
  261.9 11.7 %custom-call.22 = f32[128,128]{1,0:T(8,128)S(1)} custom-call(f32[128,128]{1,0:T(8,128)S(1)} %slice.602), custom_call_target="Cholesky" | custom-call | tf_op jit(solution)/shard_map/cond/branch_0_fun/cholesky/custom-call.1 | solution.py:80
  274.9 9.8 %custom-call.23 = f32[1,128,128]{1,2,0:T(8,128)S(1)} custom-call(f32[1,128,128]{2,1,0:T(8,128)S(1)} %fusion.46), custom_call_target="InvertDiagBlocksLowerTriangular" | custom-call | tf_op jit(solution)/shard_map/cond/branch_0_fun/triangular_solve/custom-call.0 | solution.py:81
  286.1 1.5 fusion.19
  288.1 3.7 slice_subtract_fusion.1
  291.9 1.4 copy-done.3
  293.3 12.1 %custom-call.24 = f32[128,128]{1,0:T(8,128)S(1)} custom-call(f32[128,128]{1,0:T(8,128)S(1)} %slice.605), custom_call_target="Cholesky" | custom-call | tf_op jit(solution)/shard_map/cond/branch_0_fun/cholesky/custom-call.1 | solution.py:80
  306.6 9.8 %custom-call.25 = f32[1,128,128]{1,2,0:T(8,128)S(1)} custom-call(f32[1,128,128]{2,1,0:T(8,128)S(1)} %fusion.47), custom_call_target="InvertDiagBlocksLowerTriangular" | custom-call | tf_op jit(solution)/shard_map/cond/branch_0_fun/triangular_solve/custom-call.0 | solution.py:81
  316.9 1.4 fusion.21
  318.8 2.9 slice_subtract_fusion.2
  322.9 11.7 %custom-call.26 = f32[128,128]{1,0:T(8,128)S(1)} custom-call(f32[128,128]{1,0:T(8,128)S(1)} %slice.608), custom_call_target="Cholesky" | custom-call | tf_op jit(solution)/shard_map/cond/branch_0_fun/cholesky/custom-call.1 | solution.py:80
  336.1 10.0 %custom-call.27 = f32[1,128,128]{1,2,0:T(8,128)S(1)} custom-call(f32[1,128,128]{2,1,0:T(8,128)S(1)} %fusion.48), custom_call_target="InvertDiagBlocksLowerTriangular" | custom-call | tf_op jit(solution)/shard_map/cond/branch_0_fun/triangular_solve/custom-call.0 | solution.py:81
  348.2 2.3 convolution_subtract_fusion
  351.5 11.7 %custom-call.28 = f32[128,128]{1,0:T(8,128)S(1)} custom-call(f32[128,128]{1,0:T(8,128)S(1)} %slice.611), custom_call_target="Cholesky" | custom-call | tf_op jit(solution)/shard_map/cond/branch_0_fun/cholesky/custom-call.1 | solution.py:80
  364.7 9.8 %custom-call.29 = f32[1,128,128]{1,2,0:T(8,128)S(1)} custom-call(f32[1,128,128]{2,1,0:T(8,128)S(1)} %fusion.49), custom_call_target="InvertDiagBlocksLowerTriangular" | custom-call | tf_op jit(solution)/shard_map/cond/branch_0_fun/triangular_solve/custom-call.0 | solution.py:81
  376.6 1.7 convolution_subtract_fusion.1
  378.3 11.9 %custom-call.30 = f32[128,128]{1,0:T(8,128)S(1)} custom-call(f32[128,128]{1,0:T(8,128)S(1)} %slice.614), custom_call_target="Cholesky" | custom-call | tf_op jit(solution)/shard_map/cond/branch_0_fun/cholesky/custom-call.1 | solution.py:80
  391.7 9.8 %custom-call.31 = f32[1,128,128]{1,2,0:T(8,128)S(1)} custom-call(f32[1,128,128]{2,1,0:T(8,128)S(1)} %fusion.50), custom_call_target="InvertDiagBlocksLowerTriangular" | custom-call | tf_op jit(solution)/shard_map/cond/branch_0_fun/triangular_solve/custom-call.0 | solution.py:81
  403.7 11.7 %custom-call.32 = f32[128,128]{1,0:T(8,128)S(1)} custom-call(f32[128,128]{1,0:T(8,128)S(1)} %slice.617), custom_call_target="Cholesky" | custom-call | tf_op jit(solution)/shard_map/cond/branch_0_fun/cholesky/custom-call.1 | solution.py:80
  416.7 9.8 %custom-call.33 = f32[1,128,128]{1,2,0:T(8,128)S(1)} custom-call(f32[1,128,128]{2,1,0:T(8,128)S(1)} %fusion.51), custom_call_target="InvertDiagBlocksLowerTriangular" | custom-call | tf_op jit(solution)/shard_map/cond/branch_0_fun/triangular_solve/custom-call.0 | solution.py:81
  429.7 11.7 %custom-call.34 = f32[128,128]{1,0:T(8,128)S(1)} custom-call(f32[128,128]{1,0:T(8,128)S(1)} %convolution_subtract_fusion.3), custom_call_target="Cholesky" | custom-call | tf_op jit(solution)/shard_map/cond/branch_0_fun/cholesky/custom-call.1 | solution.py:80
  442.7 9.8 %custom-call.35 = f32[1,128,128]{1,2,0:T(8,128)S(1)} custom-call(f32[1,128,128]{2,1,0:T(8,128)S(1)} %fusion.52), custom_call_target="InvertDiagBlocksLowerTriangular" | custom-call | tf_op jit(solution)/shard_map/cond/branch_0_fun/triangular_solve/custom-call.0 | solution.py:81
  (217 shorter events, 46.6 us)
Async XLA Ops:
  88.0 34.5 %copy-start.19 = (f32[8]{0:T(128)S(1)}, f32[8]{0:T(128)}, u32[]{:S(2)}) copy-start(f32[8]{0:T(128)} %param.42) | copy-start | bytes 100
  118.3 15.4 %all-to-all-start.4 = ((f32[16,9,128]{2,1,0:T(8,128)}), f32[16,9,128]{2,1,0:T(8,128)S(1)}, u32[]{:S(2)}, u32[]{:S(2)}) async-start(f32[16,9,128]{2,1,0:T(8,128)} %reshape.451), calls=%async_computation.4 | async-start | bytes 262144 | tf_op jit(solution)/shard_map/all_to_all | solution.py:40
  172.0 18.4 %copy-start.6 = (f32[2,4,4,16,9,128]{5,3,2,4,1,0:T(8,128)S(1)}, f32[2,4,4,16,9,128]{5,3,2,4,1,0:T(8,128)}, u32[]{:S(2)}) copy-start(f32[2,4,4,16,9,128]{5,3,2,4,1,0:T(8,128)} %constant.463) | copy-start | bytes 7077892
  186.1 1.5 copy-start.2
  215.5 5.6 %copy-start.11 = (pred[8,8,128,128]{3,1,2,0:T(8,128)(4,1)S(1)}, pred[8,8,128,128]{3,1,2,0:T(8,128)(4,1)}, u32[]{:S(2)}) copy-start(pred[8,8,128,128]{3,1,2,0:T(8,128)(4,1)} %constant.435.clone.2) | copy-start | bytes 3145732 | tf_op jit(solution)/shard_map/cond
  228.5 1.9 copy-start
  253.6 31.5 %copy-start.10 = (f32[128,128]{1,0:T(8,128)}, f32[128,128]{1,0:T(8,128)S(1)}, u32[]{:S(2)}) copy-start(f32[128,128]{1,0:T(8,128)S(1)} %fusion.39) | copy-start | bytes 196612 | tf_op jit(solution)/shard_map/cond
  260.2 1.7 copy-start.1
  285.0 6.9 %copy-start.8 = (f32[128,128]{1,0:T(8,128)}, f32[128,128]{1,0:T(8,128)S(1)}, u32[]{:S(2)}) copy-start(f32[128,128]{1,0:T(8,128)S(1)} %fusion.37) | copy-start | bytes 196612 | tf_op jit(solution)/shard_map/cond
  285.3 0.6 copy-start.17
  291.8 1.4 copy-start.3
  316.7 2.1 copy-start.9
  316.9 4.8 %copy-start.16 = (f32[1,128]{1,0:T(1,128)}, f32[1,128]{1,0:T(1,128)S(1)}, u32[]{:S(2)}) copy-start(f32[1,128]{1,0:T(1,128)S(1)} %fusion.79) | copy-start | bytes 1540 | tf_op jit(solution)/shard_map/cond
  321.7 1.2 copy-start.4
  346.5 18.2 %copy-start.13 = (f32[1,128]{1,0:T(1,128)}, f32[1,128]{1,0:T(1,128)S(1)}, u32[]{:S(2)}) copy-start(f32[1,128]{1,0:T(1,128)S(1)} %fusion.76) | copy-start | bytes 1540 | tf_op jit(solution)/shard_map/cond
  350.5 1.0 copy-start.5
  374.9 1.3 copy-start.14
  401.8 1.2 copy-start.7
  402.0 0.6 copy-start.15
  403.0 0.7 copy-start.12
  463.1 0.6 copy-start.18
